TPU v7x, 32 devices: a whole 2x2x4 slice. The times are simulated.
32 devices in a mesh: grp: 2 (over y), ctx: 4 (over z), tp: 4 (over x, core).
Axes of the slice: x: 2, y: 2, z: 4, core: 2. Of those that a mesh axis runs over, the one named last changes fastest.
Arguments:
- tokens: bfloat16 [3072, 4096], P(('grp', 'ctx'), 'tp'), parts along dimension 0, may hold values from -6 to 6
- norm_gain: bfloat16 [4096], P('tp'), may hold values from 0.099609375 to 1.8984375
- w_in: bfloat16 [4096, 3, 2048], P('ctx', None, 'tp'), may hold values from -0.09375 to 0.09375
- short_taps: float32 [3, 3, 2048], P(None, None, 'tp'), may hold values from -3.5 to 3.5
- rates: float32 [128, 64], P('tp'), may hold values from 6.510417e-06 to 0.03
- residues: float32 [128, 64], P('tp'), may hold values from -4 to 4
- w_out: bfloat16 [2048, 4096], P(None, 'tp'), may hold values from -0.125 to 0.125
Outputs:
- layer_out: bfloat16 [3072, 4096], P(('grp', 'ctx'), 'tp'), parts along dimension 0
There are 2 independent parts, one for each index of `grp`. A program takes and returns all parts, laid end to end along the dimension named above; an argument that names none is the same for every part. Nothing has to cross between parts.
All inputs are finite; a program needn't handle non-finite values.
Results may differ from a plain program's by a relative error of at most 0.0067.
Values may be sent and summed in bfloat16 or wider, within the bound.
No kernel may reach another device: no remote copies, remote signals or barrier semaphores. Data moves between devices by JAX's collectives and lax.ppermute only.
A program may use at most 128 MiB of HBM per device.

v0:
```python
import jax
import jax.numpy as jnp
from jax import lax
from jax.sharding import PartitionSpec as P

BLOCK = 128


def shifted(x, axis, by):
    count = lax.axis_size(axis)
    pairs = [(i, i + by) for i in range(count) if 0 <= i + by < count]
    return lax.ppermute(x, axis, pairs)


def short_filter(extended, taps, count):
    values = extended.astype(jnp.float32)
    result = jnp.zeros((count, values.shape[1]), jnp.float32)
    span = taps.shape[0]
    for tap_index in range(span):
        begin = span - 1 - tap_index
        result = result + taps[tap_index] * values[begin : begin + count]
    return result


def banded(series):
    group_count, length = series.shape
    padded = jnp.concatenate([series, jnp.zeros_like(series)], axis=1)
    tiled = jnp.tile(padded, (1, length))
    return tiled[:, : length * (2 * length - 1)].reshape(group_count, length, 2 * length - 1)


def gather_by_permutes(x, axis):
    count = lax.axis_size(axis)
    me = lax.axis_index(axis)
    pieces = [x]
    for by in range(1, count):
        pairs = [(s, (s + by) % count) for s in range(count)]
        pieces.append(lax.ppermute(x, axis, pairs))
    stacked = jnp.stack(pieces[::-1], axis=0)
    return jnp.roll(stacked, me + 1, axis=0)


def gather_by_swaps(x, axis):
    count = lax.axis_size(axis)
    me = lax.axis_index(axis)
    bits = []
    b = 1
    while b < count:
        bits.append(b)
        b *= 2
    if 2 ** len(bits) != count:
        return lax.all_gather(x, axis, axis=0)
    held = x[None]
    masks = [0]
    for bit in bits[::-1]:
        pairs = [(q, q ^ bit) for q in range(count)]
        held = jnp.concatenate([held, lax.ppermute(held, axis, pairs)], axis=0)
        masks = masks + [m ^ bit for m in masks]
    inverse = [masks.index(m) for m in range(count)]
    table = jnp.array(inverse, jnp.int32)
    where = jnp.take(table, jnp.bitwise_xor(jnp.arange(count, dtype=jnp.int32), me))
    return jnp.take(held, where, axis=0)


def body(tokens, norm_gain, w_in, short_taps, rates, residues, w_out):
    tok_rows = tokens.shape[0]
    local_width = w_in.shape[2]
    local_groups = rates.shape[0]
    group_size = local_width // local_groups
    block_rows = BLOCK
    reach = block_rows - 1
    mode_count = rates.shape[1]
    highest = lax.Precision.HIGHEST
    n_ctx = lax.axis_size("ctx")
    n_grp = lax.axis_size("grp")
    me_ctx = lax.axis_index("ctx")
    me_grp = lax.axis_index("grp")
    shard_rows = w_in.shape[0]
    piece = shard_rows // n_grp
    streams = w_in.shape[1]

    span = short_taps.shape[0]
    halo = span - 1
    decay = rates[:, :, None]
    coef = residues * jnp.sqrt(-jnp.expm1(-2.0 * rates)) * mode_count ** (-0.5)
    lags = jnp.arange(block_rows).astype(jnp.float32)
    powers = jnp.exp(-decay * lags)
    long_taps = jnp.einsum("gn,gnt->gt", coef, powers, precision=highest)
    kernel = banded(long_taps[:, ::-1])[:, :, reach:]
    tail = jnp.exp(-decay * (reach - lags))
    entry = coef[:, None, :] * jnp.exp(-rates[:, None, :] * (lags[None, :, None] + 1.0))

    with_gain = jnp.concatenate([tokens, norm_gain[None]], axis=0)
    stacked = gather_by_swaps(with_gain, "tp")
    whole_rows = jnp.concatenate(list(stacked), axis=1)
    before = shifted(whole_rows[tok_rows - halo : tok_rows], "ctx", 1)
    gathered = jnp.concatenate([before, whole_rows], axis=0)
    own = lax.dynamic_slice_in_dim(w_in, me_grp * piece, piece, axis=0)

    def relay_send(got):
        doubled = jnp.concatenate([got, got], axis=0)
        return lax.dynamic_slice_in_dim(doubled, me_ctx + 1, n_ctx - 1, axis=0)

    def relay(send):
        received = []
        for by in range(1, n_grp):
            pairs = [(q, (q + by) % n_grp) for q in range(n_grp)]
            received.append(lax.ppermute(send, "grp", pairs))
        return received

    order = [0, 2, 1] if streams == 3 else list(range(streams))
    relayed = {}
    for s in order:
        got = lax.all_gather(own[:, s, :], "ctx", axis=0)
        if s == order[0]:
            got, kernel, tail, entry = lax.optimization_barrier((got, kernel, tail, entry))
        if s == order[-1] and len(order) > 1:
            relayed[s] = (got, None)
            continue
        send = relay_send(got)
        if s == order[0]:
            send, gathered = lax.optimization_barrier((send, gathered))
        relayed[s] = (got, relay(send))

    ext_rows = tok_rows + halo
    values = gathered[:ext_rows].astype(jnp.float32)
    gain_whole = gathered[ext_rows]
    scale = lax.rsqrt(jnp.mean(values * values, axis=1, keepdims=True) + 1e-06)
    normed = (values * scale * gain_whole.astype(jnp.float32)).astype(jnp.bfloat16)
    blocks = normed.reshape(ext_rows, n_ctx * n_grp, piece).transpose(1, 0, 2)
    shard_ids = jnp.arange(n_ctx, dtype=jnp.int32)
    mine = jnp.take(blocks, shard_ids * n_grp + me_grp, axis=0)
    others = []
    for by in range(1, n_grp):
        src_grp = (me_grp - by) % n_grp
        rolled = ((shard_ids + me_ctx) % n_ctx) * n_grp + src_grp
        others.append((src_grp, jnp.take(blocks, rolled, axis=0)))
    def project(s, received):
        got = relayed[s][0]
        acc = jnp.einsum("ktr,krc->tc", mine, got, preferred_element_type=jnp.float32)
        for (src_grp, part), recv in zip(others, received):
            local = lax.dynamic_slice_in_dim(w_in[:, s, :], src_grp * piece, piece, axis=0)
            acc = acc + jnp.dot(part[0], local, preferred_element_type=jnp.float32)
            acc = acc + jnp.einsum(
                "ktr,krc->tc", part[1:], recv, preferred_element_type=jnp.float32
            )
        rounded = lax.reduce_precision(acc, exponent_bits=8, mantissa_bits=7)
        return short_filter(rounded, short_taps[:, s, :], tok_rows)

    last = order[-1]
    filtered = {s: project(s, relayed[s][1]) for s in order[:-1]}
    first = order[0]
    if relayed[last][1] is None:
        filtered[first], tied = lax.optimization_barrier((filtered[first], relayed[last][0]))
        relayed[last] = (tied, relay(relay_send(tied)))
    product = filtered[0] * filtered[2]
    blocks = tok_rows // block_rows
    current = product.reshape(blocks, block_rows, local_groups, group_size)
    near = jnp.einsum("gij,bjgc->bigc", kernel, current, precision=highest)
    ends = jnp.einsum("gni,bigc->bgnc", tail, current, precision=highest)
    step_decay = jnp.exp(-decay * block_rows)

    def advance(state, end_block):
        return (step_decay * state + end_block, state)

    zero_state = jnp.zeros((local_groups, mode_count, group_size), jnp.float32)
    own_state, local_starts = lax.scan(advance, zero_state, ends)
    incoming = jnp.zeros_like(own_state)
    for by in range(1, n_ctx):
        pairs = [(k, k + by) for k in range(n_ctx - by)]
        arrived = lax.ppermute(own_state, "ctx", pairs)
        incoming = incoming + jnp.exp(-decay * (tok_rows * (by - 1.0))) * arrived
    block_index = jnp.arange(blocks).astype(jnp.float32)
    lead = jnp.exp(-decay[None] * block_rows * block_index[:, None, None, None])
    starts = lead * incoming[None] + local_starts
    distant = jnp.einsum("gin,bgnc->bigc", entry, starts, precision=highest)
    conv_out = (near + distant).reshape(tok_rows, local_width)
    late, conv_out = lax.optimization_barrier((relayed[last][1], conv_out))
    second = project(last, late)
    gated = (second * conv_out).astype(jnp.bfloat16)
    pieces = gather_by_swaps(gated, "tp")
    mixed = jnp.einsum("qtc,qcf->tf", pieces, w_out.reshape(pieces.shape[0], local_width, -1),
                       preferred_element_type=jnp.float32)
    return (tokens.astype(jnp.float32) + mixed).astype(jnp.bfloat16)


def solution(mesh):
    in_specs = (
        P(("grp", "ctx"), "tp"),
        P("tp"),
        P("ctx", None, "tp"),
        P(None, None, "tp"),
        P("tp", None),
        P("tp", None),
        P(None, "tp"),
    )
    out_specs = P(("grp", "ctx"), "tp")
    return jax.shard_map(body, mesh=mesh, in_specs=in_specs, out_specs=out_specs, check_vma=False)
```

profile of v0, /device:TPU:0, one launch (start us, length us, event | category | flops | bytes accessed | tf_op | source)
XLA Modules:
  0.0 227.3 jit_solution(12688740877966783868)
XLA Ops:
  6.5 2.7 %constant_dynamic-slice_fusion.2 = (bf16[512,1,512]{2,0,1:T(8,128)(2,1)}, bf16[512,1,512]{2,0,1:T(8,128)(2,1)}, bf16[512,1,512]{2,0,1:T(8,128)(2,1)}) fusion(bf16[1024,3,512]{2,0,1:T(8,128)(2,1)} %param.17, s32[]{:T(128)S(6)} %select_n.56, s32[]{:T(128)S(6)} %add.190, s32[]{:T(128)S(6)} %add.189), kind=kLoop, calls=%fused_computation.123 | loop fusion | bytes 3145740 | tf_op jit(solution)/shard_map/slice | solution.py:114
  10.2 3.0 %collective-permute-start = (bf16[1,385,1024]{2,1,0:T(8,128)(2,1)S(1)}, bf16[1,385,1024]{2,1,0:T(8,128)(2,1)S(1)}, u32[]{:S(2)}, u32[]{:S(2)}) collective-permute-start(bf16[1,385,1024]{2,1,0:T(8,128)(2,1)S(1)} %maximum_bitcast_fusion), channel_id=1, source_target_pairs={{0,2},{1,3},{2,0},{3,1},{4,6},{5,7},{6,4},{7,5},{8,10},{9,11},{10,... | collective-permute-start | bytes 2365448 | tf_op jit(solution)/shard_map/ppermute | solution.py:57
  16.4 14.7 %collective-permute-done = bf16[1,385,1024]{2,1,0:T(8,128)(2,1)S(1)} collective-permute-done((bf16[1,385,1024]{2,1,0:T(8,128)(2,1)S(1)}, bf16[1,385,1024]{2,1,0:T(8,128)(2,1)S(1)}, u32[]{:S(2)}, u32[]{:S(2)}) %collective-permute-start) | collective-permute-done | bytes 788512 | tf_op jit(solution)/shard_map/ppermute | solution.py:57
  42.0 2.7 %gather_fusion = bf16[4,385,1024]{2,1,0:T(8,128)(2,1)S(1)} fusion(bf16[4,385,1024]{2,1,0:T(8,128)(2,1)} %pad_maximum_fusion, s32[1024]{0:T(1024)S(1)} %pad_clamp_fusion.2), kind=kCustom, calls=%fused_computation.3 | custom fusion | bytes 6307856 | tf_op jit(solution)/shard_map/jit(_take)/gather | solution.py:62
  47.1 4.3 %collective-permute-start.2 = (bf16[2,4096]{1,0:T(2,128)(2,1)S(1)}, bf16[2,4096]{1,0:T(2,128)(2,1)}, u32[]{:S(2)}, u32[]{:S(2)}) collective-permute-start(bf16[2,4096]{1,0:T(2,128)(2,1)S(1)} %pad_maximum_fusion.4), channel_id=1, source_target_pairs={{0,4},{4,8},{8,12},{1,5},{5,9},{9,13},{2,6},{6,10},{10,14},{3,7},{... | collective-permute-start | bytes 49160 | tf_op jit(solution)/shard_map/ppermute | solution.py:12
  52.3 2.4 %copy.57 = f32[4,8,128,256]{3,1,2,0:T(8,128)S(1)} copy(f32[4,8,128,256]{3,2,1,0:T(8,128)S(1)} %bitcast.139) | data formatting | bytes 8388608
  54.8 2.3 %slice.159 = f32[32,32640]{1,0:T(8,128)} slice(f32[32,32768]{1,0:T(8,128)S(1)} %bitcast.140), slice={[0:32], [0:32640]} | slice | bytes 8355840 | tf_op jit(solution)/shard_map/slice | solution.py:29
  57.0 9.4 %reshape.113 = f32[32,128,255]{2,1,0:T(8,128)} reshape(f32[32,32640]{1,0:T(8,128)} %slice.159) | data formatting | bytes 8355840 | tf_op jit(solution)/shard_map/reshape | solution.py:29
  66.5 4.3 %slice.160 = f32[32,128,128]{2,1,0:T(8,128)} slice(f32[32,128,255]{2,1,0:T(8,128)} %reshape.113), slice={[0:32], [0:128], [127:255]} | slice | bytes 4194304 | tf_op jit(solution)/shard_map/slice | solution.py:89
  70.8 3.5 %maximum_maximum_fusion = bf16[387,4096]{1,0:T(8,128)(2,1)S(1)} fusion(bf16[385,1024]{1,0:T(8,128)(2,1)} %copy-done.3, bf16[385,1024]{1,0:T(8,128)(2,1)} %copy-done.4, bf16[385,1024]{1,0:T(8,128)(2,1)} %copy-done.5, bf16[385,1024]{1,0:T(8,128)(2,1)} %copy-done.2, bf16[2,4096]{1,0:T(2,128)(2,1)} %collective-permute-done.2), kind=kLoop, calls=%fused_computation.19 | loop fusion | flops 15851520 | bytes 6340608 | tf_op jit(solution)/shard_map/concatenate | solution.py:97
  74.3 3.1 %fusion.7 = bf16[3,512,512]{2,1,0:T(8,128)(2,1)} fusion(s32[]{:T(128)S(6)} %select_n.57, bf16[4,512,512]{2,1,0:T(8,128)(2,1)} %bitcast.149), kind=kLoop, calls=%fused_computation.29 | loop fusion | flops 786432 | bytes 3670020 | tf_op jit(solution)/shard_map/concatenate | solution.py:101
  87.6 16.5 %all-gather.11.cloned.1.call-done = bf16[2048,1,512]{2,0,1:T(8,128)(2,1)} async-done(((bf16[512,1,512]{2,0,1:T(8,128)(2,1)}), bf16[2048,1,512]{2,0,1:T(8,128)(2,1)}) %all-gather.11.cloned.1.call-update) | async-done | bytes 2097168 | tf_op jit(solution)/shard_map/all_gather | solution.py:114
  104.2 3.3 %fusion.5 = bf16[3,512,512]{2,1,0:T(8,128)(2,1)} fusion(s32[]{:T(128)S(6)} %select_n.57, bf16[4,512,512]{2,1,0:T(8,128)(2,1)} %bitcast.151), kind=kLoop, calls=%fused_computation.27 | loop fusion | flops 786432 | bytes 3670020 | tf_op jit(solution)/shard_map/concatenate | solution.py:101
  108.9 2.5 %convolution_bitcast_fusion.5 = f32[386,512]{1,0:T(8,128)S(1)} fusion(bf16[4,512,512]{2,1,0:T(8,128)(2,1)S(1)} %bitcast.150, bf16[4,386,512]{2,1,0:T(8,128)(2,1)} %gather_fusion.3, pred[4]{0:T(512)(128)(4,1)S(1)} %copy-done.40), kind=kOutput, calls=%fused_computation.41 | convolution fusion | flops 810291200 | bytes 4468740 | tf_op jit(solution)/shard_map/ktr,krc->tc/dot_general | solution.py:140
  116.2 7.5 %collective-permute-done.3 = bf16[3,512,512]{2,1,0:T(8,128)(2,1)} collective-permute-done((bf16[3,512,512]{2,1,0:T(8,128)(2,1)}, bf16[3,512,512]{2,1,0:T(8,128)(2,1)}, u32[]{:S(2)}, u32[]{:S(2)}) %collective-permute-start.3) | collective-permute-done | bytes 1572896 | tf_op jit(solution)/shard_map/ppermute | solution.py:108
  123.7 2.2 fusion.21
  126.2 24.1 %all-gather.9.cloned.1.call-done = bf16[2048,1,512]{2,0,1:T(8,128)(2,1)} async-done(((bf16[512,1,512]{2,0,1:T(8,128)(2,1)}), bf16[2048,1,512]{2,0,1:T(8,128)(2,1)}) %all-gather.9.cloned.1.call-update) | async-done | bytes 2097168 | tf_op jit(solution)/shard_map/all_gather | solution.py:114
  150.2 6.3 %collective-permute-done.5 = bf16[3,512,512]{2,1,0:T(8,128)(2,1)} collective-permute-done((bf16[3,512,512]{2,1,0:T(8,128)(2,1)}, bf16[3,512,512]{2,1,0:T(8,128)(2,1)}, u32[]{:S(2)}, u32[]{:S(2)}) %collective-permute-start.5) | collective-permute-done | bytes 1572896 | tf_op jit(solution)/shard_map/ppermute | solution.py:108
  156.6 2.2 fusion.23
  159.7 3.2 %fusion.6 = bf16[3,512,512]{2,1,0:T(8,128)(2,1)} fusion(s32[]{:T(128)S(6)} %select_n.57, bf16[4,512,512]{2,1,0:T(8,128)(2,1)} %bitcast.147), kind=kLoop, calls=%fused_computation.28 | loop fusion | flops 786432 | bytes 3670020 | tf_op jit(solution)/shard_map/concatenate | solution.py:101
  166.4 2.6 %while.13 = (s32[]{:T(128)}, f32[32,64,16]{1,2,0:T(8,128)S(1)}, f32[3,32,64,16]{2,3,1,0:T(8,128)}, f32[32,64,1]{1,0,2:T(8,128)S(1)}, f32[3,32,64,16]{2,3,0,1:T(8,128)S(1)}, /*index=5*/s32[]{:T(128)}, s32[]{:T(128)}) while((s32[]{:T(128)}, f32[32,64,16]{1,2,0:T(8,128)S(1)}, f32[3,32,64,16]{2,3,1,0:T(8,128)}, ...), condition=%wide.region_2.5_spmd.clone, body=%wide.region_1.0_spmd.clone.sunk | while | flops 131075 | bytes 795228 | solution.py:167
  169.0 3.3 %collective-permute-start.6 = (f32[32,64,16]{1,2,0:T(8,128)S(1)}, f32[32,64,16]{1,2,0:T(8,128)S(1)}, u32[]{:S(2)}, u32[]{:S(2)}) collective-permute-start(f32[32,64,16]{1,2,0:T(8,128)S(1)} %get-tuple-element.52), channel_id=1, source_target_pairs={{0,4},{4,8},{8,12},{1,5},{5,9},{9,13},{2,6},{6,10},{10,14},{3,7},{... | collective-permute-start | bytes 393224 | tf_op jit(solution)/shard_map/ppermute | solution.py:171
  172.4 3.0 %collective-permute-start.7 = (f32[32,64,16]{1,2,0:T(8,128)S(1)}, f32[32,64,16]{1,2,0:T(8,128)S(1)}, u32[]{:S(2)}, u32[]{:S(2)}) collective-permute-start(f32[32,64,16]{1,2,0:T(8,128)S(1)} %get-tuple-element.52), channel_id=1, source_target_pairs={{0,8},{4,12},{1,9},{5,13},{2,10},{6,14},{3,11},{7,15},{16,24},{20,... | collective-permute-start | bytes 393224 | tf_op jit(solution)/shard_map/ppermute | solution.py:171
  176.6 3.1 %convolution_bitcast_fusion.4 = f32[386,512]{1,0:T(8,128)S(1)} fusion(bf16[4,512,512]{2,1,0:T(8,128)(2,1)} %bitcast.148, bf16[4,386,512]{2,1,0:T(8,128)(2,1)} %gather_fusion.3, pred[4]{0:T(512)(128)(4,1)S(1)} %copy-done.40), kind=kOutput, calls=%fused_computation.40 | convolution fusion | flops 810291200 | bytes 4468740 | tf_op jit(solution)/shard_map/ktr,krc->tc/dot_general | solution.py:140
  181.1 3.6 %collective-permute-done.7 = f32[32,64,16]{1,2,0:T(8,128)S(1)} collective-permute-done((f32[32,64,16]{1,2,0:T(8,128)S(1)}, f32[32,64,16]{1,2,0:T(8,128)S(1)}, u32[]{:S(2)}, u32[]{:S(2)}) %collective-permute-start.7) | collective-permute-done | bytes 131104 | tf_op jit(solution)/shard_map/ppermute | solution.py:171
  184.7 3.7 %collective-permute-done.8 = f32[32,64,16]{1,2,0:T(8,128)S(1)} collective-permute-done((f32[32,64,16]{1,2,0:T(8,128)S(1)}, f32[32,64,16]{1,2,0:T(8,128)S(1)}, u32[]{:S(2)}, u32[]{:S(2)}) %collective-permute-start.8) | collective-permute-done | bytes 131104 | tf_op jit(solution)/shard_map/ppermute | solution.py:171
  190.1 3.4 %fusion.17 = f32[3,128,32,16]{1,3,0,2:T(8,128)S(1)} fusion(f32[32,3,16,128]{3,2,1,0:T(8,128)S(1)} %fusion.26, f32[32,128,128]{2,1,0:T(8,128)S(1)} %copy-done.1, f32[3,128,32,16]{1,0,3,2:T(4,128)S(1)} %reshape.115), kind=kOutput, calls=%fused_computation.46 | convolution fusion | flops 302186496 | bytes 4456448 | tf_op jit(solution)/shard_map/gij,bjgc->bigc/dot_general | solution.py:159
  194.0 4.8 %collective-permute-done.4 = bf16[3,512,512]{2,1,0:T(8,128)(2,1)} collective-permute-done((bf16[3,512,512]{2,1,0:T(8,128)(2,1)}, bf16[3,512,512]{2,1,0:T(8,128)(2,1)}, u32[]{:S(2)}, u32[]{:S(2)}) %collective-permute-start.4) | collective-permute-done | bytes 1572896 | tf_op jit(solution)/shard_map/ppermute | solution.py:108
  200.0 2.5 %fusion.25 = f32[386,512]{1,0:T(8,128)S(1)} fusion(f32[386,512]{1,0:T(8,128)} %convolution_add_fusion.1, bf16[4,386,512]{2,1,0:T(8,128)(2,1)S(1)} %copy-done.9, bf16[3,512,512]{2,1,0:T(8,128)(2,1)} %collective-permute-done.4), kind=kOutput, calls=%fused_computation.53 | convolution fusion | flops 607520768 | bytes 4734976 | tf_op jit(solution)/shard_map/ktr,krc->tc/dot_general | solution.py:144
  204.3 8.0 %collective-permute-done.9 = bf16[1,384,512]{2,1,0:T(8,128)(2,1)S(1)} collective-permute-done((bf16[1,384,512]{2,1,0:T(8,128)(2,1)S(1)}, bf16[1,384,512]{2,1,0:T(8,128)(2,1)S(1)}, u32[]{:S(2)}, u32[]{:S(2)}) %collective-permute-start.9) | collective-permute-done | bytes 393248 | tf_op jit(solution)/shard_map/ppermute | solution.py:57
  212.4 2.3 collective-permute-done.10
  215.7 5.1 %fusion.8 = bf16[384,1024]{1,0:T(8,128)(2,1)} fusion(bf16[384,1024]{1,0:T(8,128)(2,1)} %param.15, bf16[4,512,1024]{2,1,0:T(8,128)(2,1)} %bitcast.166, bf16[4,384,512]{2,1,0:T(8,128)(2,1)S(1)} %gather_fusion.1, pred[4]{0:T(512)(128)(4,1)S(1)} %copy-done.37), kind=kOutput, calls=%fused_computation.32 | convolution fusion | flops 1612578816 | bytes 7340036 | tf_op jit(solution)/shard_map/qtc,qcf->tf/dot_general | solution.py:182
  (167 shorter events, 50.3 us)
Async XLA Ops:
  6.5 67.8 %all-gather.7.cloned.1.call-start = ((), (), s32[]{:S(2)}) async-start(), calls=%async_computation | async-start | bytes 2621440 | tf_op jit(solution)/shard_map/all_gather | solution.py:114
  9.3 94.9 %all-gather.11.cloned.1.call-start = ((), (), s32[]{:S(2)}) async-start(), calls=%async_computation.2 | async-start | bytes 2621440 | tf_op jit(solution)/shard_map/all_gather | solution.py:114
  9.3 6.4 %copy-start.25 = (f32[3,3,512]{2,1,0:T(4,128)S(1)}, f32[3,3,512]{2,1,0:T(4,128)}, u32[]{:S(2)}) copy-start(f32[3,3,512]{2,1,0:T(4,128)} %param.18) | copy-start | bytes 55300
  10.0 140.2 %all-gather.9.cloned.1.call-start = ((), (), s32[]{:S(2)}) async-start(), calls=%async_computation.1 | async-start | bytes 2621440 | tf_op jit(solution)/shard_map/all_gather | solution.py:114
  10.2 20.9 %collective-permute-start = (bf16[1,385,1024]{2,1,0:T(8,128)(2,1)S(1)}, bf16[1,385,1024]{2,1,0:T(8,128)(2,1)S(1)}, u32[]{:S(2)}, u32[]{:S(2)}) collective-permute-start(bf16[1,385,1024]{2,1,0:T(8,128)(2,1)S(1)} %maximum_bitcast_fusion), channel_id=1, source_target_pairs={{0,2},{1,3},{2,0},{3,1},{4,6},{5,7},{6,4},{7,5},{8,10},{9,11},{10,... | collective-permute-start | bytes 2365448 | tf_op jit(solution)/shard_map/ppermute | solution.py:57
  14.5 30.2 %copy-start.36 = (pred[4]{0:T(512)(128)(4,1)}, pred[4]{0:T(512)(128)(4,1)S(1)}, u32[]{:S(2)}) copy-start(pred[4]{0:T(512)(128)(4,1)S(1)} %get-tuple-element.112) | copy-start | bytes 16
  14.5 27.4 %copy-start.35 = (s32[1024]{0:T(1024)}, s32[1024]{0:T(1024)S(1)}, u32[]{:S(2)}) copy-start(s32[1024]{0:T(1024)S(1)} %pad_clamp_fusion.2) | copy-start | bytes 12292
  31.3 6.5 %copy-start.6 = (bf16[1024,3,512]{2,0,1:T(8,128)(2,1)S(1)}, bf16[1024,3,512]{2,0,1:T(8,128)(2,1)}, u32[]{:S(2)}) copy-start(bf16[1024,3,512]{2,0,1:T(8,128)(2,1)} %param.17) | copy-start | bytes 9437188
  32.9 6.7 %collective-permute-start.1 = (bf16[2,385,1024]{2,0,1:T(2,128)(2,1)S(1)}, bf16[2,385,1024]{2,0,1:T(2,128)(2,1)S(1)}, u32[]{:S(2)}, u32[]{:S(2)}) collective-permute-start(bf16[2,385,1024]{2,0,1:T(2,128)(2,1)S(1)} %copy.41), channel_id=1, source_target_pairs={{0,1},{1,0},{2,3},{3,2},{4,5},{5,4},{6,7},{7,6},{8,9},{9,8},{10,11... | collective-permute-start | bytes 4730888 | tf_op jit(solution)/shard_map/ppermute | solution.py:57
  47.1 23.7 %collective-permute-start.2 = (bf16[2,4096]{1,0:T(2,128)(2,1)S(1)}, bf16[2,4096]{1,0:T(2,128)(2,1)}, u32[]{:S(2)}, u32[]{:S(2)}) collective-permute-start(bf16[2,4096]{1,0:T(2,128)(2,1)S(1)} %pad_maximum_fusion.4), channel_id=1, source_target_pairs={{0,4},{4,8},{8,12},{1,5},{5,9},{9,13},{2,6},{6,10},{10,14},{3,7},{... | collective-permute-start | bytes 49160 | tf_op jit(solution)/shard_map/ppermute | solution.py:12
  86.1 37.6 %collective-permute-start.3 = (bf16[3,512,512]{2,1,0:T(8,128)(2,1)}, bf16[3,512,512]{2,1,0:T(8,128)(2,1)}, u32[]{:S(2)}, u32[]{:S(2)}) collective-permute-start(bf16[3,512,512]{2,1,0:T(8,128)(2,1)} %fusion.7), channel_id=1, source_target_pairs={{0,16},{16,0},{1,17},{17,1},{2,18},{18,2},{3,19},{19,3},{4,20},{20... | collective-permute-start | bytes 4718600 | tf_op jit(solution)/shard_map/ppermute | solution.py:108
  104.2 4.7 %copy-start.40 = (pred[4]{0:T(512)(128)(4,1)S(1)}, pred[4]{0:T(512)(128)(4,1)}, u32[]{:S(2)}) copy-start(pred[4]{0:T(512)(128)(4,1)} %compare_and_fusion.1) | copy-start | bytes 16
  107.4 49.1 %collective-permute-start.5 = (bf16[3,512,512]{2,1,0:T(8,128)(2,1)}, bf16[3,512,512]{2,1,0:T(8,128)(2,1)}, u32[]{:S(2)}, u32[]{:S(2)}) collective-permute-start(bf16[3,512,512]{2,1,0:T(8,128)(2,1)} %fusion.5), channel_id=1, source_target_pairs={{0,16},{16,0},{1,17},{17,1},{2,18},{18,2},{3,19},{19,3},{4,20},{20... | collective-permute-start | bytes 4718600 | tf_op jit(solution)/shard_map/ppermute | solution.py:108
  111.6 44.9 %copy-start.8 = (bf16[4,386,512]{2,1,0:T(8,128)(2,1)}, bf16[4,386,512]{2,1,0:T(8,128)(2,1)S(1)}, u32[]{:S(2)}) copy-start(bf16[4,386,512]{2,1,0:T(8,128)(2,1)S(1)} %broadcast_select_fusion.1) | copy-start | bytes 4743172
  116.2 9.7 %copy-start.32 = (f32[1,1,512]{2,1,0:T(1,128)S(1)}, f32[1,1,512]{2,1,0:T(1,128)}, u32[]{:S(2)}) copy-start(f32[1,1,512]{2,1,0:T(1,128)} %get-tuple-element.128) | copy-start | bytes 6148
  116.2 9.7 %copy-start.33 = (f32[1,1,512]{2,1,0:T(1,128)S(1)}, f32[1,1,512]{2,1,0:T(1,128)}, u32[]{:S(2)}) copy-start(f32[1,1,512]{2,1,0:T(1,128)} %get-tuple-element.129) | copy-start | bytes 6148
  116.2 9.7 %copy-start.34 = (f32[1,1,512]{2,1,0:T(1,128)S(1)}, f32[1,1,512]{2,1,0:T(1,128)}, u32[]{:S(2)}) copy-start(f32[1,1,512]{2,1,0:T(1,128)} %get-tuple-element.130) | copy-start | bytes 6148
  150.2 8.5 %copy-start.29 = (f32[1,1,512]{2,1,0:T(1,128)S(1)}, f32[1,1,512]{2,1,0:T(1,128)}, u32[]{:S(2)}) copy-start(f32[1,1,512]{2,1,0:T(1,128)} %get-tuple-element.125) | copy-start | bytes 6148
  150.2 8.6 %copy-start.30 = (f32[1,1,512]{2,1,0:T(1,128)S(1)}, f32[1,1,512]{2,1,0:T(1,128)}, u32[]{:S(2)}) copy-start(f32[1,1,512]{2,1,0:T(1,128)} %get-tuple-element.126) | copy-start | bytes 6148
  150.2 8.6 %copy-start.31 = (f32[1,1,512]{2,1,0:T(1,128)S(1)}, f32[1,1,512]{2,1,0:T(1,128)}, u32[]{:S(2)}) copy-start(f32[1,1,512]{2,1,0:T(1,128)} %get-tuple-element.127) | copy-start | bytes 6148
  162.9 35.9 %collective-permute-start.4 = (bf16[3,512,512]{2,1,0:T(8,128)(2,1)}, bf16[3,512,512]{2,1,0:T(8,128)(2,1)}, u32[]{:S(2)}, u32[]{:S(2)}) collective-permute-start(bf16[3,512,512]{2,1,0:T(8,128)(2,1)} %fusion.6), channel_id=1, source_target_pairs={{0,16},{16,0},{1,17},{17,1},{2,18},{18,2},{3,19},{19,3},{4,20},{20... | collective-permute-start | bytes 4718600 | tf_op jit(solution)/shard_map/ppermute | solution.py:108
  169.0 10.8 %copy-start.9 = (bf16[4,386,512]{2,1,0:T(8,128)(2,1)S(1)}, bf16[4,386,512]{2,1,0:T(8,128)(2,1)}, u32[]{:S(2)}) copy-start(bf16[4,386,512]{2,1,0:T(8,128)(2,1)} %copy-done.8) | copy-start | bytes 4743172
  169.0 10.8 %copy-start.13 = (bf16[1024,1,512]{2,0,1:T(8,128)(2,1)S(1)}, bf16[1024,1,512]{2,0,1:T(8,128)(2,1)}, u32[]{:S(2)}) copy-start(bf16[1024,1,512]{2,0,1:T(8,128)(2,1)} %get-tuple-element.118) | copy-start | bytes 3145732
  169.0 12.1 %collective-permute-start.6 = (f32[32,64,16]{1,2,0:T(8,128)S(1)}, f32[32,64,16]{1,2,0:T(8,128)S(1)}, u32[]{:S(2)}, u32[]{:S(2)}) collective-permute-start(f32[32,64,16]{1,2,0:T(8,128)S(1)} %get-tuple-element.52), channel_id=1, source_target_pairs={{0,4},{4,8},{8,12},{1,5},{5,9},{9,13},{2,6},{6,10},{10,14},{3,7},{... | collective-permute-start | bytes 393224 | tf_op jit(solution)/shard_map/ppermute | solution.py:171
  172.4 12.3 %collective-permute-start.7 = (f32[32,64,16]{1,2,0:T(8,128)S(1)}, f32[32,64,16]{1,2,0:T(8,128)S(1)}, u32[]{:S(2)}, u32[]{:S(2)}) collective-permute-start(f32[32,64,16]{1,2,0:T(8,128)S(1)} %get-tuple-element.52), channel_id=1, source_target_pairs={{0,8},{4,12},{1,9},{5,13},{2,10},{6,14},{3,11},{7,15},{16,24},{20,... | collective-permute-start | bytes 393224 | tf_op jit(solution)/shard_map/ppermute | solution.py:171
  175.3 13.1 %collective-permute-start.8 = (f32[32,64,16]{1,2,0:T(8,128)S(1)}, f32[32,64,16]{1,2,0:T(8,128)S(1)}, u32[]{:S(2)}, u32[]{:S(2)}) collective-permute-start(f32[32,64,16]{1,2,0:T(8,128)S(1)} %get-tuple-element.52), channel_id=1, source_target_pairs={{0,12},{1,13},{2,14},{3,15},{16,28},{17,29},{18,30},{19,31}} | collective-permute-start | bytes 393224 | tf_op jit(solution)/shard_map/ppermute | solution.py:171
  179.8 8.6 %copy-start.21 = (f32[32,64]{1,0:T(8,128)S(1)}, f32[32,64]{1,0:T(8,128)}, u32[]{:S(2)}) copy-start(f32[32,64]{1,0:T(8,128)} %get-tuple-element.135) | copy-start | bytes 24580
  179.8 8.6 %copy-start.22 = (f32[32,64]{1,0:T(8,128)S(1)}, f32[32,64]{1,0:T(8,128)}, u32[]{:S(2)}) copy-start(f32[32,64]{1,0:T(8,128)} %get-tuple-element.136) | copy-start | bytes 24580
  179.8 8.7 %copy-start.11 = (f32[32,128,64]{1,2,0:T(8,128)S(1)}, f32[32,128,64]{1,2,0:T(8,128)}, u32[]{:S(2)}) copy-start(f32[32,128,64]{1,2,0:T(8,128)} %exponential_multiply_fusion) | copy-start | bytes 3145732
  179.8 8.7 %copy-start.20 = (f32[3,32,64,16]{2,3,1,0:T(8,128)S(1)}, f32[3,32,64,16]{2,3,1,0:T(8,128)}, u32[]{:S(2)}) copy-start(f32[3,32,64,16]{2,3,1,0:T(8,128)} %get-tuple-element.53) | copy-start | bytes 1179652
  202.8 9.5 %collective-permute-start.9 = (bf16[1,384,512]{2,1,0:T(8,128)(2,1)S(1)}, bf16[1,384,512]{2,1,0:T(8,128)(2,1)S(1)}, u32[]{:S(2)}, u32[]{:S(2)}) collective-permute-start(bf16[1,384,512]{2,1,0:T(8,128)(2,1)S(1)} %fusion.53), channel_id=1, source_target_pairs={{0,2},{1,3},{2,0},{3,1},{4,6},{5,7},{6,4},{7,5},{8,10},{9,11},{10,... | collective-permute-start | bytes 1179656 | tf_op jit(solution)/shard_map/ppermute | solution.py:57
  212.4 2.4 %collective-permute-start.10 = (bf16[2,384,512]{2,1,0:T(8,128)(2,1)S(1)}, bf16[2,384,512]{2,1,0:T(8,128)(2,1)S(1)}, u32[]{:S(2)}, u32[]{:S(2)}) collective-permute-start(bf16[2,384,512]{2,1,0:T(8,128)(2,1)S(1)} %pad_maximum_fusion.3), channel_id=1, source_target_pairs={{0,1},{1,0},{2,3},{3,2},{4,5},{5,4},{6,7},{7,6},{8,9},{9,8},{10,11... | collective-permute-start | bytes 2359304 | tf_op jit(solution)/shard_map/ppermute | solution.py:57
  (23 other events, 58.4 us)
Sparse Core Ops, SparseCore 0:
  9.4 48.3 all-gather.6
  59.4 44.7 all-gather.10
  105.7 44.4 all-gather.8
where the time goes:
time: 228 us; the launch traced here: 227 us
  waiting for transfers between devices  92.2 us (40%)
  local copies, waits for them, and re-layouts  44.2 us (19%)
  matrix products  28.4 us (12%)
  other arithmetic  27.3 us (12%)
  starting transfers between devices  21.3 us (9%)
  between operations  13.9 us (6%)
    all_gather x3, waiting for transfers between devices, body(): got = lax.all_gather(own[:, s, :], 'ctx', axis=0)  40.6 us
    ppermute x4, waiting for transfers between devices, gather_by_swaps(): held = jnp.concatenate([held, lax.ppermute(held, axis, pairs)], axis=0)  25 us
    ppermute x3, waiting for transfers between devices, relay(): received.append(lax.ppermute(send, 'grp', pairs))  18.6 us
    concatenate x3, other arithmetic, relay_send(): doubled = jnp.concatenate([got, got], axis=0)  9.58 us
    reshape x1, local copies, waits for them, and re-layouts, banded(): tiled[:, :length * (2 * length - 1)]  9.44 us
    unnamed x85, local copies, waits for them, and re-layouts  8.8 us
    ppermute x3, starting transfers between devices, body(): arrived = lax.ppermute(own_state, 'ctx', pairs)  7.59 us
    ppermute x3, waiting for transfers between devices, body(): arrived = lax.ppermute(own_state, 'ctx', pairs)  7.3 us
  transfers between devices with their start and end apart: 14, of which 10 were waited for; matrix products, arithmetic and copies ran while one was open for 33% of the time, Pallas kernels for 0%

commit v1 on v0

--- a/solution.py
+++ b/solution.py
@@ -86,7 +86,10 @@
     lags = jnp.arange(block_rows).astype(jnp.float32)
     powers = jnp.exp(-decay * lags)
     long_taps = jnp.einsum("gn,gnt->gt", coef, powers, precision=highest)
-    kernel = banded(long_taps[:, ::-1])[:, :, reach:]
+    falling = coef[:, None, :] * jnp.exp(-rates[:, None, :] * lags[None, :, None])
+    rising = jnp.exp(rates[:, None, :] * lags[None, :, None])
+    square = jnp.einsum("gin,gjn->gij", falling, rising, precision=highest)
+    kernel = jnp.where(lags[None, :, None] >= lags[None, None, :], square, 0.0)
     tail = jnp.exp(-decay * (reach - lags))
     entry = coef[:, None, :] * jnp.exp(-rates[:, None, :] * (lags[None, :, None] + 1.0))
 

time: 228 us -> 222 us (0.974)
  local copies, waits for them, and re-layouts: 44.2 us -> 25.2 us
  waiting for transfers between devices: 92.2 us -> 101 us
  matrix products: 28.4 us -> 32.8 us
    all_gather x3, waiting for transfers between devices: 40.6 us -> 62.1 us  [body(): got = lax.all_gather(own[:, s, :], 'ctx', axis=0)]
    ppermute x3, waiting for transfers between devices: 18.6 us -> 6.31 us  [relay(): received.append(lax.ppermute(send, 'grp', pairs))]
    reshape x1 -> x0, local copies, waits for them, and re-layouts: 9.44 us -> none  [banded(): tiled[:, :length * (2 * length - 1)]]
    slice x2 -> x0, local copies, waits for them, and re-layouts: 6.57 us -> none  [the longest x1 4.29 us: body(): kernel = banded(long_taps[:, ::-1])[:, :, reach:]]
    dot_general x1, matrix products: 1.13 us -> 5.54 us  [body(): square = jnp.einsum('gin,gjn->gij', falling, rising, precision=highest)]
    unnamed x85 -> x84, local copies, waits for them, and re-layouts: 8.8 us -> 6.37 us
  transfers between devices with their start and end apart: 14 -> 14, of which waited for: 10 -> 9; matrix products, arithmetic and copies ran while one was open for 33% -> 28% of each run, Pallas kernels for 0% -> 0%
where the time goes in v1:
time: 222 us; the launch traced here: 221 us
  waiting for transfers between devices  101 us (45%)
  matrix products  32.8 us (15%)
  other arithmetic  27.4 us (12%)
  local copies, waits for them, and re-layouts  25.2 us (11%)
  starting transfers between devices  20.7 us (9%)
  between operations  13.9 us (6%)
    all_gather x3, waiting for transfers between devices, body(): got = lax.all_gather(own[:, s, :], 'ctx', axis=0)  62.1 us
    ppermute x4, waiting for transfers between devices, gather_by_swaps(): held = jnp.concatenate([held, lax.ppermute(held, axis, pairs)], axis=0)  25.3 us
    concatenate x3, other arithmetic, relay_send(): doubled = jnp.concatenate([got, got], axis=0)  9.71 us
    ppermute x3, starting transfers between devices, body(): arrived = lax.ppermute(own_state, 'ctx', pairs)  7.12 us
    dot_general x3, matrix products, project(): jnp.einsum('ktr,krc->tc', part[1:], recv, preferred_element_type=jnp.floa...  6.87 us
    ppermute x3, waiting for transfers between devices, body(): arrived = lax.ppermute(own_state, 'ctx', pairs)  6.71 us
    dot_general x3, matrix products, project(): jnp.einsum('ktr,krc->tc', mine, got, preferred_element_type=jnp.float32)  6.63 us
    unnamed x84, local copies, waits for them, and re-layouts  6.37 us
  transfers between devices with their start and end apart: 14, of which 9 were waited for; matrix products, arithmetic and copies ran while one was open for 28% of the time, Pallas kernels for 0%

profile of v1, /device:TPU:0, one launch (start us, length us, event | category | flops | bytes accessed | tf_op | source)
XLA Modules:
  0.0 221.4 jit_solution(7598251973647644961)
XLA Ops:
  6.5 2.6 %constant_dynamic-slice_fusion.2 = (bf16[512,1,512]{2,0,1:T(8,128)(2,1)}, bf16[512,1,512]{2,0,1:T(8,128)(2,1)}, bf16[512,1,512]{2,0,1:T(8,128)(2,1)}) fusion(bf16[1024,3,512]{2,0,1:T(8,128)(2,1)} %param.17, s32[]{:T(128)S(6)} %select_n.60, s32[]{:T(128)S(6)} %add.188, s32[]{:T(128)S(6)} %add.187), kind=kLoop, calls=%fused_computation.129 | loop fusion | bytes 3145740 | tf_op jit(solution)/shard_map/slice | solution.py:117
  10.1 3.0 %collective-permute-start = (bf16[1,385,1024]{2,1,0:T(8,128)(2,1)S(1)}, bf16[1,385,1024]{2,1,0:T(8,128)(2,1)S(1)}, u32[]{:S(2)}, u32[]{:S(2)}) collective-permute-start(bf16[1,385,1024]{2,1,0:T(8,128)(2,1)S(1)} %maximum_bitcast_fusion), channel_id=1, source_target_pairs={{0,2},{1,3},{2,0},{3,1},{4,6},{5,7},{6,4},{7,5},{8,10},{9,11},{10,... | collective-permute-start | bytes 2365448 | tf_op jit(solution)/shard_map/ppermute | solution.py:57
  16.4 14.6 %collective-permute-done = bf16[1,385,1024]{2,1,0:T(8,128)(2,1)S(1)} collective-permute-done((bf16[1,385,1024]{2,1,0:T(8,128)(2,1)S(1)}, bf16[1,385,1024]{2,1,0:T(8,128)(2,1)S(1)}, u32[]{:S(2)}, u32[]{:S(2)}) %collective-permute-start) | collective-permute-done | bytes 788512 | tf_op jit(solution)/shard_map/ppermute | solution.py:57
  36.5 5.5 %convolution_select_fusion = f32[32,128,128]{2,1,0:T(8,128)} fusion(pred[128,128]{1,0:T(8,128)(4,1)S(1)} %broadcast_compare_fusion, f32[32,64]{1,0:T(8,128)S(1)} %copy-done.24, f32[128]{0:T(128)S(1)} %iota_convert_fusion.1, f32[32,64]{1,0:T(8,128)S(1)} %get-tuple-element.139, f32[32,64]{1,0:T(8,128)S(1)} %get-tuple-element.138), kind=kOutput, calls=%fused_computation.24 | convolution fusion | flops 403963904 | bytes 2138624 | tf_op jit(solution)/shard_map/gin,gjn->gij/dot_general | solution.py:91
  42.1 1.8 fusion.65
  44.3 2.0 pad_maximum_fusion
  46.3 2.7 %gather_fusion = bf16[4,385,1024]{2,1,0:T(8,128)(2,1)S(1)} fusion(bf16[4,385,1024]{2,1,0:T(8,128)(2,1)} %pad_maximum_fusion, s32[1024]{0:T(1024)S(1)} %pad_clamp_fusion.2), kind=kCustom, calls=%fused_computation.3 | custom fusion | bytes 6307856 | tf_op jit(solution)/shard_map/jit(_take)/gather | solution.py:62
  51.3 4.3 %collective-permute-start.2 = (bf16[2,4096]{1,0:T(2,128)(2,1)S(1)}, bf16[2,4096]{1,0:T(2,128)(2,1)}, u32[]{:S(2)}, u32[]{:S(2)}) collective-permute-start(bf16[2,4096]{1,0:T(2,128)(2,1)S(1)} %pad_maximum_fusion.4), channel_id=1, source_target_pairs={{0,4},{4,8},{8,12},{1,5},{5,9},{9,13},{2,6},{6,10},{10,14},{3,7},{... | collective-permute-start | bytes 49160 | tf_op jit(solution)/shard_map/ppermute | solution.py:12
  56.5 3.5 %maximum_maximum_fusion = bf16[387,4096]{1,0:T(8,128)(2,1)S(1)} fusion(bf16[385,1024]{1,0:T(8,128)(2,1)} %copy-done.2, bf16[385,1024]{1,0:T(8,128)(2,1)} %copy-done.3, bf16[385,1024]{1,0:T(8,128)(2,1)} %copy-done.4, bf16[385,1024]{1,0:T(8,128)(2,1)} %copy-done.1, bf16[2,4096]{1,0:T(2,128)(2,1)} %collective-permute-done.2), kind=kLoop, calls=%fused_computation.19 | loop fusion | flops 15851520 | bytes 6340608 | tf_op jit(solution)/shard_map/concatenate | solution.py:100
  60.0 3.2 %fusion.7 = bf16[3,512,512]{2,1,0:T(8,128)(2,1)} fusion(s32[]{:T(128)S(6)} %select_n.62, bf16[4,512,512]{2,1,0:T(8,128)(2,1)} %bitcast.139), kind=kLoop, calls=%fused_computation.30 | loop fusion | flops 786432 | bytes 3670020 | tf_op jit(solution)/shard_map/concatenate | solution.py:104
  67.8 1.9 gather_fusion.4
  69.7 2.0 gather_fusion.3
  73.2 30.6 %all-gather.11.cloned.1.call-done = bf16[2048,1,512]{2,0,1:T(8,128)(2,1)} async-done(((bf16[512,1,512]{2,0,1:T(8,128)(2,1)}), bf16[2048,1,512]{2,0,1:T(8,128)(2,1)}) %all-gather.11.cloned.1.call-update) | async-done | bytes 2097168 | tf_op jit(solution)/shard_map/all_gather | solution.py:117
  103.8 3.3 %fusion.5 = bf16[3,512,512]{2,1,0:T(8,128)(2,1)} fusion(s32[]{:T(128)S(6)} %select_n.62, bf16[4,512,512]{2,1,0:T(8,128)(2,1)} %bitcast.141), kind=kLoop, calls=%fused_computation.28 | loop fusion | flops 786432 | bytes 3670020 | tf_op jit(solution)/shard_map/concatenate | solution.py:104
  108.5 2.5 %convolution_bitcast_fusion.5 = f32[386,512]{1,0:T(8,128)S(1)} fusion(bf16[4,512,512]{2,1,0:T(8,128)(2,1)S(1)} %bitcast.140, bf16[4,386,512]{2,1,0:T(8,128)(2,1)} %gather_fusion.3, pred[4]{0:T(512)(128)(4,1)S(1)} %copy-done.40), kind=kOutput, calls=%fused_computation.42 | convolution fusion | flops 810291200 | bytes 4468740 | tf_op jit(solution)/shard_map/ktr,krc->tc/dot_general | solution.py:143
  115.9 2.2 fusion.21
  118.3 31.5 %all-gather.9.cloned.1.call-done = bf16[2048,1,512]{2,0,1:T(8,128)(2,1)} async-done(((bf16[512,1,512]{2,0,1:T(8,128)(2,1)}), bf16[2048,1,512]{2,0,1:T(8,128)(2,1)}) %all-gather.9.cloned.1.call-update) | async-done | bytes 2097168 | tf_op jit(solution)/shard_map/all_gather | solution.py:117
  149.9 2.2 fusion.23
  153.0 3.3 %fusion.6 = bf16[3,512,512]{2,1,0:T(8,128)(2,1)} fusion(s32[]{:T(128)S(6)} %select_n.62, bf16[4,512,512]{2,1,0:T(8,128)(2,1)} %bitcast.137), kind=kLoop, calls=%fused_computation.29 | loop fusion | flops 786432 | bytes 3670020 | tf_op jit(solution)/shard_map/concatenate | solution.py:104
  157.7 2.0 convolution_bitcast_fusion.6
  159.7 2.6 %while.13 = (s32[]{:T(128)}, f32[32,64,16]{1,2,0:T(8,128)S(1)}, f32[3,32,64,16]{2,3,1,0:T(8,128)}, f32[32,64,1]{1,0,2:T(8,128)S(1)}, f32[3,32,64,16]{2,3,0,1:T(8,128)S(1)}, /*index=5*/s32[]{:T(128)}, s32[]{:T(128)}) while((s32[]{:T(128)}, f32[32,64,16]{1,2,0:T(8,128)S(1)}, f32[3,32,64,16]{2,3,1,0:T(8,128)}, ...), condition=%wide.region_2.5_spmd.clone, body=%wide.region_1.4_spmd.clone.sunk | while | flops 131075 | bytes 795228 | solution.py:170
  162.3 2.3 %collective-permute-start.6 = (f32[32,64,16]{1,2,0:T(8,128)S(1)}, f32[32,64,16]{1,2,0:T(8,128)S(1)}, u32[]{:S(2)}, u32[]{:S(2)}) collective-permute-start(f32[32,64,16]{1,2,0:T(8,128)S(1)} %get-tuple-element.52), channel_id=1, source_target_pairs={{0,4},{4,8},{8,12},{1,5},{5,9},{9,13},{2,6},{6,10},{10,14},{3,7},{... | collective-permute-start | bytes 393224 | tf_op jit(solution)/shard_map/ppermute | solution.py:174
  164.6 3.5 %collective-permute-start.7 = (f32[32,64,16]{1,2,0:T(8,128)S(1)}, f32[32,64,16]{1,2,0:T(8,128)S(1)}, u32[]{:S(2)}, u32[]{:S(2)}) collective-permute-start(f32[32,64,16]{1,2,0:T(8,128)S(1)} %get-tuple-element.52), channel_id=1, source_target_pairs={{0,8},{4,12},{1,9},{5,13},{2,10},{6,14},{3,11},{7,15},{16,24},{20,... | collective-permute-start | bytes 393224 | tf_op jit(solution)/shard_map/ppermute | solution.py:174
  169.5 3.1 %convolution_bitcast_fusion.4 = f32[386,512]{1,0:T(8,128)S(1)} fusion(bf16[4,512,512]{2,1,0:T(8,128)(2,1)} %bitcast.138, bf16[4,386,512]{2,1,0:T(8,128)(2,1)} %gather_fusion.3, pred[4]{0:T(512)(128)(4,1)S(1)} %copy-done.40), kind=kOutput, calls=%fused_computation.41 | convolution fusion | flops 810291200 | bytes 4468740 | tf_op jit(solution)/shard_map/ktr,krc->tc/dot_general | solution.py:143
  174.0 2.8 %collective-permute-done.7 = f32[32,64,16]{1,2,0:T(8,128)S(1)} collective-permute-done((f32[32,64,16]{1,2,0:T(8,128)S(1)}, f32[32,64,16]{1,2,0:T(8,128)S(1)}, u32[]{:S(2)}, u32[]{:S(2)}) %collective-permute-start.7) | collective-permute-done | bytes 131104 | tf_op jit(solution)/shard_map/ppermute | solution.py:174
  176.8 3.9 %collective-permute-done.8 = f32[32,64,16]{1,2,0:T(8,128)S(1)} collective-permute-done((f32[32,64,16]{1,2,0:T(8,128)S(1)}, f32[32,64,16]{1,2,0:T(8,128)S(1)}, u32[]{:S(2)}, u32[]{:S(2)}) %collective-permute-start.8) | collective-permute-done | bytes 131104 | tf_op jit(solution)/shard_map/ppermute | solution.py:174
  182.4 3.4 %fusion.17 = f32[3,128,32,16]{1,3,0,2:T(8,128)S(1)} fusion(f32[32,3,16,128]{3,2,1,0:T(8,128)S(1)} %fusion.26, f32[32,128,128]{2,1,0:T(8,128)S(1)} %copy-done.15, f32[3,128,32,16]{1,0,3,2:T(4,128)S(1)} %reshape.139), kind=kOutput, calls=%fused_computation.47 | convolution fusion | flops 302186496 | bytes 4456448 | tf_op jit(solution)/shard_map/gij,bjgc->bigc/dot_general | solution.py:162
  186.2 6.3 %collective-permute-done.4 = bf16[3,512,512]{2,1,0:T(8,128)(2,1)} collective-permute-done((bf16[3,512,512]{2,1,0:T(8,128)(2,1)}, bf16[3,512,512]{2,1,0:T(8,128)(2,1)}, u32[]{:S(2)}, u32[]{:S(2)}) %collective-permute-start.4) | collective-permute-done | bytes 1572896 | tf_op jit(solution)/shard_map/ppermute | solution.py:111
  193.7 2.5 %fusion.25 = f32[386,512]{1,0:T(8,128)S(1)} fusion(f32[386,512]{1,0:T(8,128)} %convolution_add_fusion.1, bf16[4,386,512]{2,1,0:T(8,128)(2,1)S(1)} %copy-done.8, bf16[3,512,512]{2,1,0:T(8,128)(2,1)} %collective-permute-done.4), kind=kOutput, calls=%fused_computation.54 | convolution fusion | flops 607520768 | bytes 4734976 | tf_op jit(solution)/shard_map/ktr,krc->tc/dot_general | solution.py:147
  198.0 8.4 %collective-permute-done.9 = bf16[1,384,512]{2,1,0:T(8,128)(2,1)S(1)} collective-permute-done((bf16[1,384,512]{2,1,0:T(8,128)(2,1)S(1)}, bf16[1,384,512]{2,1,0:T(8,128)(2,1)S(1)}, u32[]{:S(2)}, u32[]{:S(2)}) %collective-permute-start.9) | collective-permute-done | bytes 393248 | tf_op jit(solution)/shard_map/ppermute | solution.py:57
  206.6 2.3 %collective-permute-done.10 = bf16[2,384,512]{2,1,0:T(8,128)(2,1)S(1)} collective-permute-done((bf16[2,384,512]{2,1,0:T(8,128)(2,1)S(1)}, bf16[2,384,512]{2,1,0:T(8,128)(2,1)S(1)}, u32[]{:S(2)}, u32[]{:S(2)}) %collective-permute-start.10) | collective-permute-done | bytes 786464 | tf_op jit(solution)/shard_map/ppermute | solution.py:57
  209.8 5.1 %fusion.8 = bf16[384,1024]{1,0:T(8,128)(2,1)} fusion(bf16[384,1024]{1,0:T(8,128)(2,1)} %param.15, bf16[4,512,1024]{2,1,0:T(8,128)(2,1)} %bitcast.154, bf16[4,384,512]{2,1,0:T(8,128)(2,1)S(1)} %gather_fusion.1, pred[4]{0:T(512)(128)(4,1)S(1)} %copy-done.37), kind=kOutput, calls=%fused_computation.33 | convolution fusion | flops 1612578816 | bytes 7340036 | tf_op jit(solution)/shard_map/qtc,qcf->tf/dot_general | solution.py:185
  (161 shorter events, 39.4 us)
Async XLA Ops:
  6.5 53.5 %all-gather.7.cloned.1.call-start = ((), (), s32[]{:S(2)}) async-start(), calls=%async_computation | async-start | bytes 2621440 | tf_op jit(solution)/shard_map/all_gather | solution.py:117
  6.5 3.5 %copy-start.19 = (bf16[384,1024]{1,0:T(8,128)(2,1)S(1)}, bf16[384,1024]{1,0:T(8,128)(2,1)}, u32[]{:S(2)}) copy-start(bf16[384,1024]{1,0:T(8,128)(2,1)} %param.15) | copy-start | bytes 2359300
  9.2 4.0 %copy-start = (s32[4]{0:T(128)S(1)}, s32[4]{0:T(128)}, u32[]{:S(2)}) copy-start(s32[4]{0:T(128)} %constant.136.clone2.1) | copy-start | bytes 52
  9.2 94.6 %all-gather.11.cloned.1.call-start = ((), (), s32[]{:S(2)}) async-start(), calls=%async_computation.2 | async-start | bytes 2621440 | tf_op jit(solution)/shard_map/all_gather | solution.py:117
  9.2 6.5 %copy-start.25 = (f32[3,3,512]{2,1,0:T(4,128)S(1)}, f32[3,3,512]{2,1,0:T(4,128)}, u32[]{:S(2)}) copy-start(f32[3,3,512]{2,1,0:T(4,128)} %param.18) | copy-start | bytes 55300
  9.9 139.9 %all-gather.9.cloned.1.call-start = ((), (), s32[]{:S(2)}) async-start(), calls=%async_computation.1 | async-start | bytes 2621440 | tf_op jit(solution)/shard_map/all_gather | solution.py:117
  10.1 20.9 %collective-permute-start = (bf16[1,385,1024]{2,1,0:T(8,128)(2,1)S(1)}, bf16[1,385,1024]{2,1,0:T(8,128)(2,1)S(1)}, u32[]{:S(2)}, u32[]{:S(2)}) collective-permute-start(bf16[1,385,1024]{2,1,0:T(8,128)(2,1)S(1)} %maximum_bitcast_fusion), channel_id=1, source_target_pairs={{0,2},{1,3},{2,0},{3,1},{4,6},{5,7},{6,4},{7,5},{8,10},{9,11},{10,... | collective-permute-start | bytes 2365448 | tf_op jit(solution)/shard_map/ppermute | solution.py:57
  13.9 35.1 %copy-start.36 = (pred[4]{0:T(512)(128)(4,1)}, pred[4]{0:T(512)(128)(4,1)S(1)}, u32[]{:S(2)}) copy-start(pred[4]{0:T(512)(128)(4,1)S(1)} %get-tuple-element.112) | copy-start | bytes 16
  14.4 31.8 %copy-start.35 = (s32[1024]{0:T(1024)}, s32[1024]{0:T(1024)S(1)}, u32[]{:S(2)}) copy-start(s32[1024]{0:T(1024)S(1)} %pad_clamp_fusion.2) | copy-start | bytes 12292
  32.8 11.1 %collective-permute-start.1 = (bf16[2,385,1024]{2,0,1:T(2,128)(2,1)S(1)}, bf16[2,385,1024]{2,0,1:T(2,128)(2,1)S(1)}, u32[]{:S(2)}, u32[]{:S(2)}) collective-permute-start(bf16[2,385,1024]{2,0,1:T(2,128)(2,1)S(1)} %copy.41), channel_id=1, source_target_pairs={{0,1},{1,0},{2,3},{3,2},{4,5},{5,4},{6,7},{7,6},{8,9},{9,8},{10,11... | collective-permute-start | bytes 4730888 | tf_op jit(solution)/shard_map/ppermute | solution.py:57
  34.9 7.1 %copy-start.5 = (bf16[1024,3,512]{2,0,1:T(8,128)(2,1)S(1)}, bf16[1024,3,512]{2,0,1:T(8,128)(2,1)}, u32[]{:S(2)}) copy-start(bf16[1024,3,512]{2,0,1:T(8,128)(2,1)} %param.17) | copy-start | bytes 9437188
  51.3 5.1 %collective-permute-start.2 = (bf16[2,4096]{1,0:T(2,128)(2,1)S(1)}, bf16[2,4096]{1,0:T(2,128)(2,1)}, u32[]{:S(2)}, u32[]{:S(2)}) collective-permute-start(bf16[2,4096]{1,0:T(2,128)(2,1)S(1)} %pad_maximum_fusion.4), channel_id=1, source_target_pairs={{0,4},{4,8},{8,12},{1,5},{5,9},{9,13},{2,6},{6,10},{10,14},{3,7},{... | collective-permute-start | bytes 49160 | tf_op jit(solution)/shard_map/ppermute | solution.py:12
  71.7 44.2 %collective-permute-start.3 = (bf16[3,512,512]{2,1,0:T(8,128)(2,1)}, bf16[3,512,512]{2,1,0:T(8,128)(2,1)}, u32[]{:S(2)}, u32[]{:S(2)}) collective-permute-start(bf16[3,512,512]{2,1,0:T(8,128)(2,1)} %fusion.7), channel_id=1, source_target_pairs={{0,16},{16,0},{1,17},{17,1},{2,18},{18,2},{3,19},{19,3},{4,20},{20... | collective-permute-start | bytes 4718600 | tf_op jit(solution)/shard_map/ppermute | solution.py:111
  103.8 4.8 %copy-start.16 = (bf16[2048,1,512]{2,0,1:T(8,128)(2,1)S(1)}, bf16[2048,1,512]{2,0,1:T(8,128)(2,1)}, u32[]{:S(2)}) copy-start(bf16[2048,1,512]{2,0,1:T(8,128)(2,1)} %all-gather.7.cloned.1.call-done) | copy-start | bytes 6291460
  103.8 4.8 %copy-start.40 = (pred[4]{0:T(512)(128)(4,1)S(1)}, pred[4]{0:T(512)(128)(4,1)}, u32[]{:S(2)}) copy-start(pred[4]{0:T(512)(128)(4,1)} %compare_and_fusion.1) | copy-start | bytes 16
  107.1 3.9 %copy-start.6 = (bf16[4,386,512]{2,1,0:T(8,128)(2,1)S(1)}, bf16[4,386,512]{2,1,0:T(8,128)(2,1)}, u32[]{:S(2)}) copy-start(bf16[4,386,512]{2,1,0:T(8,128)(2,1)} %gather_fusion.4) | copy-start | bytes 4743172
  107.1 4.0 %copy-start.39 = (pred[4]{0:T(512)(128)(4,1)S(1)}, pred[4]{0:T(512)(128)(4,1)}, u32[]{:S(2)}) copy-start(pred[4]{0:T(512)(128)(4,1)} %get-tuple-element.110) | copy-start | bytes 16
  107.1 42.8 %collective-permute-start.5 = (bf16[3,512,512]{2,1,0:T(8,128)(2,1)}, bf16[3,512,512]{2,1,0:T(8,128)(2,1)}, u32[]{:S(2)}, u32[]{:S(2)}) collective-permute-start(bf16[3,512,512]{2,1,0:T(8,128)(2,1)} %fusion.5), channel_id=1, source_target_pairs={{0,16},{16,0},{1,17},{17,1},{2,18},{18,2},{3,19},{19,3},{4,20},{20... | collective-permute-start | bytes 4718600 | tf_op jit(solution)/shard_map/ppermute | solution.py:111
  111.3 38.6 %copy-start.7 = (bf16[4,386,512]{2,1,0:T(8,128)(2,1)}, bf16[4,386,512]{2,1,0:T(8,128)(2,1)S(1)}, u32[]{:S(2)}) copy-start(bf16[4,386,512]{2,1,0:T(8,128)(2,1)S(1)} %broadcast_select_fusion.1) | copy-start | bytes 4743172
  153.0 4.8 %copy-start.9 = (f32[32,64,128]{2,1,0:T(8,128)S(1)}, f32[32,64,128]{2,1,0:T(8,128)}, u32[]{:S(2)}) copy-start(f32[32,64,128]{2,1,0:T(8,128)} %multiply_exponential_fusion) | copy-start | bytes 3145732
  156.3 36.3 %collective-permute-start.4 = (bf16[3,512,512]{2,1,0:T(8,128)(2,1)}, bf16[3,512,512]{2,1,0:T(8,128)(2,1)}, u32[]{:S(2)}, u32[]{:S(2)}) collective-permute-start(bf16[3,512,512]{2,1,0:T(8,128)(2,1)} %fusion.6), channel_id=1, source_target_pairs={{0,16},{16,0},{1,17},{17,1},{2,18},{18,2},{3,19},{19,3},{4,20},{20... | collective-permute-start | bytes 4718600 | tf_op jit(solution)/shard_map/ppermute | solution.py:111
  162.3 10.3 %copy-start.8 = (bf16[4,386,512]{2,1,0:T(8,128)(2,1)S(1)}, bf16[4,386,512]{2,1,0:T(8,128)(2,1)}, u32[]{:S(2)}) copy-start(bf16[4,386,512]{2,1,0:T(8,128)(2,1)} %copy-done.7) | copy-start | bytes 4743172
  162.3 10.3 %copy-start.12 = (bf16[1024,1,512]{2,0,1:T(8,128)(2,1)S(1)}, bf16[1024,1,512]{2,0,1:T(8,128)(2,1)}, u32[]{:S(2)}) copy-start(bf16[1024,1,512]{2,0,1:T(8,128)(2,1)} %get-tuple-element.118) | copy-start | bytes 3145732
  162.3 11.6 %collective-permute-start.6 = (f32[32,64,16]{1,2,0:T(8,128)S(1)}, f32[32,64,16]{1,2,0:T(8,128)S(1)}, u32[]{:S(2)}, u32[]{:S(2)}) collective-permute-start(f32[32,64,16]{1,2,0:T(8,128)S(1)} %get-tuple-element.52), channel_id=1, source_target_pairs={{0,4},{4,8},{8,12},{1,5},{5,9},{9,13},{2,6},{6,10},{10,14},{3,7},{... | collective-permute-start | bytes 393224 | tf_op jit(solution)/shard_map/ppermute | solution.py:174
  164.6 12.2 %collective-permute-start.7 = (f32[32,64,16]{1,2,0:T(8,128)S(1)}, f32[32,64,16]{1,2,0:T(8,128)S(1)}, u32[]{:S(2)}, u32[]{:S(2)}) collective-permute-start(f32[32,64,16]{1,2,0:T(8,128)S(1)} %get-tuple-element.52), channel_id=1, source_target_pairs={{0,8},{4,12},{1,9},{5,13},{2,10},{6,14},{3,11},{7,15},{16,24},{20,... | collective-permute-start | bytes 393224 | tf_op jit(solution)/shard_map/ppermute | solution.py:174
  168.1 12.5 %collective-permute-start.8 = (f32[32,64,16]{1,2,0:T(8,128)S(1)}, f32[32,64,16]{1,2,0:T(8,128)S(1)}, u32[]{:S(2)}, u32[]{:S(2)}) collective-permute-start(f32[32,64,16]{1,2,0:T(8,128)S(1)} %get-tuple-element.52), channel_id=1, source_target_pairs={{0,12},{1,13},{2,14},{3,15},{16,28},{17,29},{18,30},{19,31}} | collective-permute-start | bytes 393224 | tf_op jit(solution)/shard_map/ppermute | solution.py:174
  172.6 8.1 %copy-start.21 = (f32[32,64]{1,0:T(8,128)S(1)}, f32[32,64]{1,0:T(8,128)}, u32[]{:S(2)}) copy-start(f32[32,64]{1,0:T(8,128)} %get-tuple-element.135) | copy-start | bytes 24580
  172.6 8.1 %copy-start.22 = (f32[32,64]{1,0:T(8,128)S(1)}, f32[32,64]{1,0:T(8,128)}, u32[]{:S(2)}) copy-start(f32[32,64]{1,0:T(8,128)} %get-tuple-element.136) | copy-start | bytes 24580
  172.6 8.2 %copy-start.10 = (f32[32,128,64]{1,2,0:T(8,128)S(1)}, f32[32,128,64]{1,2,0:T(8,128)}, u32[]{:S(2)}) copy-start(f32[32,128,64]{1,2,0:T(8,128)} %exponential_multiply_fusion) | copy-start | bytes 3145732
  172.6 8.2 %copy-start.20 = (f32[3,32,64,16]{2,3,1,0:T(8,128)S(1)}, f32[3,32,64,16]{2,3,1,0:T(8,128)}, u32[]{:S(2)}) copy-start(f32[3,32,64,16]{2,3,1,0:T(8,128)} %get-tuple-element.53) | copy-start | bytes 1179652
  196.5 9.9 %collective-permute-start.9 = (bf16[1,384,512]{2,1,0:T(8,128)(2,1)S(1)}, bf16[1,384,512]{2,1,0:T(8,128)(2,1)S(1)}, u32[]{:S(2)}, u32[]{:S(2)}) collective-permute-start(bf16[1,384,512]{2,1,0:T(8,128)(2,1)S(1)} %fusion.57), channel_id=1, source_target_pairs={{0,2},{1,3},{2,0},{3,1},{4,6},{5,7},{6,4},{7,5},{8,10},{9,11},{10,... | collective-permute-start | bytes 1179656 | tf_op jit(solution)/shard_map/ppermute | solution.py:57
  206.5 2.4 %collective-permute-start.10 = (bf16[2,384,512]{2,1,0:T(8,128)(2,1)S(1)}, bf16[2,384,512]{2,1,0:T(8,128)(2,1)S(1)}, u32[]{:S(2)}, u32[]{:S(2)}) collective-permute-start(bf16[2,384,512]{2,1,0:T(8,128)(2,1)S(1)} %pad_maximum_fusion.3), channel_id=1, source_target_pairs={{0,1},{1,0},{2,3},{3,2},{4,5},{5,4},{6,7},{7,6},{8,9},{9,8},{10,11... | collective-permute-start | bytes 2359304 | tf_op jit(solution)/shard_map/ppermute | solution.py:57
  (23 other events, 46.2 us)
Sparse Core Ops, SparseCore 0:
  9.3 48.3 all-gather.6
  59.3 44.4 all-gather.10
  105.4 44.4 all-gather.8

commit v2 on v1

--- a/solution.py
+++ b/solution.py
@@ -101,8 +101,24 @@
     own = lax.dynamic_slice_in_dim(w_in, me_grp * piece, piece, axis=0)
 
     def relay_send(got):
-        doubled = jnp.concatenate([got, got], axis=0)
-        return lax.dynamic_slice_in_dim(doubled, me_ctx + 1, n_ctx - 1, axis=0)
+        return got[1:]
+
+    def gather_ctx(piece_arr):
+        if n_ctx > 8:
+            got = lax.all_gather(piece_arr, "ctx", axis=0)
+            doubled = jnp.concatenate([got, got], axis=0)
+            return lax.dynamic_slice_in_dim(doubled, me_ctx, n_ctx, axis=0)
+        rights, lefts = [], []
+        to_right, to_left = piece_arr, piece_arr
+        for _ in range(1, n_ctx):
+            to_right = lax.ppermute(to_right, "ctx", [(k, k + 1) for k in range(n_ctx - 1)])
+            to_left = lax.ppermute(to_left, "ctx", [(k + 1, k) for k in range(n_ctx - 1)])
+            rights.append(to_right)
+            lefts.append(to_left)
+        rolled = [piece_arr]
+        for m in range(1, n_ctx):
+            rolled.append(jnp.where(me_ctx + m < n_ctx, lefts[m - 1], rights[n_ctx - m - 1]))
+        return jnp.stack(rolled, axis=0)
 
     def relay(send):
         received = []
@@ -114,7 +130,7 @@
     order = [0, 2, 1] if streams == 3 else list(range(streams))
     relayed = {}
     for s in order:
-        got = lax.all_gather(own[:, s, :], "ctx", axis=0)
+        got = gather_ctx(own[:, s, :])
         if s == order[0]:
             got, kernel, tail, entry = lax.optimization_barrier((got, kernel, tail, entry))
         if s == order[-1] and len(order) > 1:
@@ -132,7 +148,7 @@
     normed = (values * scale * gain_whole.astype(jnp.float32)).astype(jnp.bfloat16)
     blocks = normed.reshape(ext_rows, n_ctx * n_grp, piece).transpose(1, 0, 2)
     shard_ids = jnp.arange(n_ctx, dtype=jnp.int32)
-    mine = jnp.take(blocks, shard_ids * n_grp + me_grp, axis=0)
+    mine = jnp.take(blocks, ((shard_ids + me_ctx) % n_ctx) * n_grp + me_grp, axis=0)
     others = []
     for by in range(1, n_grp):
         src_grp = (me_grp - by) % n_grp

time: 222 us -> 249 us (1.12); the launches traced: 221 us -> 244 us
  starting transfers between devices: 20.7 us -> 67.3 us
  waiting for transfers between devices: 101 us -> 74.9 us
  between operations: 13.9 us -> 1.06 us
  other arithmetic: 27.4 us -> 36.1 us
  local copies, waits for them, and re-layouts: 25.2 us -> 29.2 us
  matrix products: 32.8 us -> 35.7 us
    all_gather x3 -> x0, waiting for transfers between devices: 62.1 us -> none  [body(): got = lax.all_gather(own[:, s, :], 'ctx', axis=0)]
    ppermute x0 -> x18, starting transfers between devices: none -> 51 us  [the longest x9 39.4 us: gather_ctx(): lax.ppermute(to_right, 'ctx', [(k, k + 1) for k in range(n_ctx - 1)])]
    ppermute x0 -> x18, waiting for transfers between devices: none -> 41 us  [the longest x9 41 us: gather_ctx(): lax.ppermute(to_left, 'ctx', [(k + 1, k) for k in range(n_ctx - 1)])]
    ppermute x4, waiting for transfers between devices: 25.3 us -> 9.52 us  [gather_by_swaps(): held = jnp.concatenate([held, lax.ppermute(held, axis, pairs)], axis=0)]
    ppermute x3, waiting for transfers between devices: 6.31 us -> 18.9 us  [relay(): received.append(lax.ppermute(send, 'grp', pairs))]
    another operation x0 -> x12, other arithmetic: none -> 11.8 us  [gather_ctx(): return jnp.stack(rolled, axis=0)]
    concatenate x3 -> x0, other arithmetic: 9.71 us -> none  [relay_send(): doubled = jnp.concatenate([got, got], axis=0)]
    another operation x0 -> x1, local copies, waits for them, and re-layouts: none -> 2.99 us  [gather_ctx(): return jnp.stack(rolled, axis=0)]
  transfers between devices with their start and end apart: 14 -> 29, of which waited for: 9 -> 13; matrix products, arithmetic and copies ran while one was open for 28% -> 33% of each run, Pallas kernels for 0% -> 0%
where the time goes in v2:
time: 249 us; the launch traced here: 244 us
  waiting for transfers between devices  74.9 us (30%)
  starting transfers between devices  67.3 us (27%)
  other arithmetic  36.1 us (14%)
  matrix products  35.7 us (14%)
  local copies, waits for them, and re-layouts  29.2 us (12%)
    ppermute x9, waiting for transfers between devices, gather_ctx(): lax.ppermute(to_left, 'ctx', [(k + 1, k) for k in range(n_ctx - 1)])  41 us
    ppermute x9, starting transfers between devices, gather_ctx(): lax.ppermute(to_right, 'ctx', [(k, k + 1) for k in range(n_ctx - 1)])  39.4 us
    ppermute x3, waiting for transfers between devices, relay(): received.append(lax.ppermute(send, 'grp', pairs))  18.9 us
    another operation x12, other arithmetic, gather_ctx(): return jnp.stack(rolled, axis=0)  11.8 us
    ppermute x9, starting transfers between devices, gather_ctx(): lax.ppermute(to_left, 'ctx', [(k + 1, k) for k in range(n_ctx - 1)])  11.6 us
    ppermute x4, waiting for transfers between devices, gather_by_swaps(): held = jnp.concatenate([held, lax.ppermute(held, axis, pairs)], axis=0)  9.52 us
    dot_general x3, matrix products, project(): jnp.einsum('ktr,krc->tc', part[1:], recv, preferred_element_type=jnp.floa...  6.93 us
    dot_general x3, matrix products, project(): jnp.einsum('ktr,krc->tc', mine, got, preferred_element_type=jnp.float32)  6.76 us
  transfers between devices with their start and end apart: 29, of which 13 were waited for; matrix products, arithmetic and copies ran while one was open for 33% of the time, Pallas kernels for 0%

profile of v2, /device:TPU:0, one launch (start us, length us, event | category | flops | bytes accessed | tf_op | source)
XLA Modules:
  0.0 244.2 jit_solution(731779257413629129)
XLA Ops:
  0.0 3.0 %dynamic-slice_bitcast_fusion.3 = (bf16[1,512,512]{2,1,0:T(8,128)(2,1)}, bf16[512,512]{1,0:T(8,128)(2,1)}, bf16[512,512]{1,0:T(8,128)(2,1)}, bf16[512,512]{1,0:T...) fusion(bf16[1024,3,512]{2,0,1:T(8,128)(2,1)} %param.17, s32[]{:T(128)S(6)} %select_n.101, ...), kind=kLoop, calls=%fused_computation.120 | loop fusion | bytes 4718604 | tf_op jit(solution)/shard_map/stack;squeeze | solution.py:121
  3.0 5.0 %collective-permute-start.1 = (bf16[512,512]{1,0:T(8,128)(2,1)}, bf16[512,512]{1,0:T(8,128)(2,1)S(1)}, u32[]{:S(2)}, u32[]{:S(2)}) collective-permute-start(bf16[512,512]{1,0:T(8,128)(2,1)} %get-tuple-element.126), channel_id=1, source_target_pairs={{0,4},{4,8},{8,12},{1,5},{5,9},{9,13},{2,6},{6,10},{10,14},{3,7},{... | collective-permute-start | bytes 1572872 | tf_op jit(solution)/shard_map/ppermute | solution.py:114
  10.9 4.6 %collective-permute-start.11 = (bf16[512,512]{1,0:T(8,128)(2,1)}, bf16[512,512]{1,0:T(8,128)(2,1)S(1)}, u32[]{:S(2)}, u32[]{:S(2)}) collective-permute-start(bf16[512,512]{1,0:T(8,128)(2,1)} %get-tuple-element.124), channel_id=1, source_target_pairs={{0,4},{4,8},{8,12},{1,5},{5,9},{9,13},{2,6},{6,10},{10,14},{3,7},{... | collective-permute-start | bytes 1572872 | tf_op jit(solution)/shard_map/ppermute | solution.py:114
  15.5 4.2 %collective-permute-start.18 = (bf16[512,512]{1,0:T(8,128)(2,1)}, bf16[512,512]{1,0:T(8,128)(2,1)}, u32[]{:S(2)}, u32[]{:S(2)}) collective-permute-start(bf16[512,512]{1,0:T(8,128)(2,1)} %get-tuple-element.125), channel_id=1, source_target_pairs={{0,4},{4,8},{8,12},{1,5},{5,9},{9,13},{2,6},{6,10},{10,14},{3,7},{... | collective-permute-start | bytes 1572872 | tf_op jit(solution)/shard_map/ppermute | solution.py:114
  19.8 3.6 %fusion.81 = (bf16[1024,1,512]{2,0,1:T(8,128)(2,1)}, bf16[1024,1,512]{2,0,1:T(8,128)(2,1)}, bf16[1024,1,512]{2,0,1:T(8,128)(2,1)}) fusion(bf16[1024,3,512]{2,0,1:T(8,128)(2,1)} %param.17), kind=kLoop, calls=%fused_computation.165 | loop fusion | bytes 6291456 | tf_op jit(solution)/shard_map/slice | solution.py:161
  27.3 5.6 %convolution_select_fusion = f32[32,128,128]{2,1,0:T(8,128)} fusion(pred[128,128]{1,0:T(8,128)(4,1)S(1)} %broadcast_compare_fusion, f32[32,64]{1,0:T(8,128)S(1)} %copy-done.30, f32[128]{0:T(128)S(1)} %iota_convert_fusion.1, f32[32,64]{1,0:T(8,128)S(1)} %get-tuple-element.144, f32[32,64]{1,0:T(8,128)S(1)} %get-tuple-element.143), kind=kOutput, calls=%fused_computation.28 | convolution fusion | flops 403963904 | bytes 2138624 | tf_op jit(solution)/shard_map/gin,gjn->gij/dot_general | solution.py:91
  37.8 6.0 %collective-permute-start.2 = (bf16[512,512]{1,0:T(8,128)(2,1)S(1)}, bf16[512,512]{1,0:T(8,128)(2,1)}, u32[]{:S(2)}, u32[]{:S(2)}) collective-permute-start(bf16[512,512]{1,0:T(8,128)(2,1)S(1)} %collective-permute-done.1), channel_id=1, source_target_pairs={{0,4},{4,8},{8,12},{1,5},{5,9},{9,13},{2,6},{6,10},{10,14},{3,7},{... | collective-permute-start | bytes 1572872 | tf_op jit(solution)/shard_map/ppermute | solution.py:114
  47.8 3.4 %collective-permute-done.17 = bf16[512,512]{1,0:T(8,128)(2,1)} collective-permute-done((bf16[512,512]{1,0:T(8,128)(2,1)}, bf16[512,512]{1,0:T(8,128)(2,1)}, u32[]{:S(2)}, u32[]{:S(2)}) %collective-permute-start.17) | collective-permute-done | bytes 524320 | tf_op jit(solution)/shard_map/ppermute | solution.py:115
  51.1 3.5 %collective-permute-start.19 = (bf16[512,512]{1,0:T(8,128)(2,1)}, bf16[512,512]{1,0:T(8,128)(2,1)S(1)}, u32[]{:S(2)}, u32[]{:S(2)}) collective-permute-start(bf16[512,512]{1,0:T(8,128)(2,1)} %collective-permute-done.18), channel_id=1, source_target_pairs={{0,4},{4,8},{8,12},{1,5},{5,9},{9,13},{2,6},{6,10},{10,14},{3,7},{... | collective-permute-start | bytes 1572872 | tf_op jit(solution)/shard_map/ppermute | solution.py:114
  59.0 3.4 %collective-permute-done.10 = bf16[512,512]{1,0:T(8,128)(2,1)} collective-permute-done((bf16[512,512]{1,0:T(8,128)(2,1)}, bf16[512,512]{1,0:T(8,128)(2,1)}, u32[]{:S(2)}, u32[]{:S(2)}) %collective-permute-start.10) | collective-permute-done | bytes 524320 | tf_op jit(solution)/shard_map/ppermute | solution.py:115
  62.4 3.5 %collective-permute-start.12 = (bf16[512,512]{1,0:T(8,128)(2,1)S(1)}, bf16[512,512]{1,0:T(8,128)(2,1)S(1)}, u32[]{:S(2)}, u32[]{:S(2)}) collective-permute-start(bf16[512,512]{1,0:T(8,128)(2,1)S(1)} %collective-permute-done.11), channel_id=1, source_target_pairs={{0,4},{4,8},{8,12},{1,5},{5,9},{9,13},{2,6},{6,10},{10,14},{3,7},{... | collective-permute-start | bytes 1572872 | tf_op jit(solution)/shard_map/ppermute | solution.py:114
  67.2 6.4 %collective-permute-done.4 = bf16[512,512]{1,0:T(8,128)(2,1)} collective-permute-done((bf16[512,512]{1,0:T(8,128)(2,1)}, bf16[512,512]{1,0:T(8,128)(2,1)}, u32[]{:S(2)}, u32[]{:S(2)}) %collective-permute-start.4) | collective-permute-done | bytes 524320 | tf_op jit(solution)/shard_map/ppermute | solution.py:115
  74.7 3.5 %collective-permute-start.3 = (bf16[512,512]{1,0:T(8,128)(2,1)}, bf16[512,512]{1,0:T(8,128)(2,1)S(1)}, u32[]{:S(2)}, u32[]{:S(2)}) collective-permute-start(bf16[512,512]{1,0:T(8,128)(2,1)} %collective-permute-done.2), channel_id=1, source_target_pairs={{0,4},{4,8},{8,12},{1,5},{5,9},{9,13},{2,6},{6,10},{10,14},{3,7},{... | collective-permute-start | bytes 1572872 | tf_op jit(solution)/shard_map/ppermute | solution.py:114
  78.3 6.5 %collective-permute-done.21 = bf16[512,512]{1,0:T(8,128)(2,1)S(1)} collective-permute-done((bf16[512,512]{1,0:T(8,128)(2,1)}, bf16[512,512]{1,0:T(8,128)(2,1)S(1)}, u32[]{:S(2)}, u32[]{:S(2)}) %collective-permute-start.21) | collective-permute-done | bytes 524320 | tf_op jit(solution)/shard_map/ppermute | solution.py:115
  87.4 8.6 %collective-permute-done.14 = bf16[512,512]{1,0:T(8,128)(2,1)S(1)} collective-permute-done((bf16[512,512]{1,0:T(8,128)(2,1)}, bf16[512,512]{1,0:T(8,128)(2,1)S(1)}, u32[]{:S(2)}, u32[]{:S(2)}) %collective-permute-start.14) | collective-permute-done | bytes 524320 | tf_op jit(solution)/shard_map/ppermute | solution.py:115
  96.0 3.5 %collective-permute-start.20 = (bf16[512,512]{1,0:T(8,128)(2,1)S(1)}, bf16[512,512]{1,0:T(8,128)(2,1)S(1)}, u32[]{:S(2)}, u32[]{:S(2)}) collective-permute-start(bf16[512,512]{1,0:T(8,128)(2,1)S(1)} %collective-permute-done.19), channel_id=1, source_target_pairs={{0,4},{4,8},{8,12},{1,5},{5,9},{9,13},{2,6},{6,10},{10,14},{3,7},{... | collective-permute-start | bytes 1572872 | tf_op jit(solution)/shard_map/ppermute | solution.py:114
  100.4 6.8 %collective-permute-done.22 = bf16[512,512]{1,0:T(8,128)(2,1)S(1)} collective-permute-done((bf16[512,512]{1,0:T(8,128)(2,1)S(1)}, bf16[512,512]{1,0:T(8,128)(2,1)S(1)}, u32[]{:S(2)}, u32[]{:S(2)}) %collective-permute-start.22) | collective-permute-done | bytes 524320 | tf_op jit(solution)/shard_map/ppermute | solution.py:115
  108.6 5.6 %collective-permute-start.13 = (bf16[512,512]{1,0:T(8,128)(2,1)S(1)}, bf16[512,512]{1,0:T(8,128)(2,1)S(1)}, u32[]{:S(2)}, u32[]{:S(2)}) collective-permute-start(bf16[512,512]{1,0:T(8,128)(2,1)S(1)} %collective-permute-done.12), channel_id=1, source_target_pairs={{0,4},{4,8},{8,12},{1,5},{5,9},{9,13},{2,6},{6,10},{10,14},{3,7},{... | collective-permute-start | bytes 1572872 | tf_op jit(solution)/shard_map/ppermute | solution.py:114
  121.2 6.0 %collective-permute-done.15 = bf16[512,512]{1,0:T(8,128)(2,1)S(1)} collective-permute-done((bf16[512,512]{1,0:T(8,128)(2,1)S(1)}, bf16[512,512]{1,0:T(8,128)(2,1)S(1)}, u32[]{:S(2)}, u32[]{:S(2)}) %collective-permute-start.15) | collective-permute-done | bytes 524320 | tf_op jit(solution)/shard_map/ppermute | solution.py:115
  132.4 2.8 %gather_fusion = bf16[4,385,1024]{2,1,0:T(8,128)(2,1)S(1)} fusion(bf16[4,385,1024]{2,1,0:T(8,128)(2,1)} %pad_maximum_fusion, s32[1024]{0:T(1024)} %pad_clamp_fusion.2), kind=kCustom, calls=%fused_computation.3 | custom fusion | bytes 6307856 | tf_op jit(solution)/shard_map/jit(_take)/gather | solution.py:62
  136.6 3.6 %collective-permute-start.8 = (bf16[2,4096]{1,0:T(2,128)(2,1)S(1)}, bf16[2,4096]{1,0:T(2,128)(2,1)S(1)}, u32[]{:S(2)}, u32[]{:S(2)}) collective-permute-start(bf16[2,4096]{1,0:T(2,128)(2,1)S(1)} %pad_maximum_fusion.7), channel_id=1, source_target_pairs={{0,4},{4,8},{8,12},{1,5},{5,9},{9,13},{2,6},{6,10},{10,14},{3,7},{... | collective-permute-start | bytes 49160 | tf_op jit(solution)/shard_map/ppermute | solution.py:12
  160.3 3.3 %convolution_bitcast_fusion.4 = f32[386,512]{1,0:T(8,128)S(1)} fusion(bf16[4,512,512]{2,1,0:T(8,128)(2,1)} %pad_maximum_fusion.1, bf16[4,386,512]{2,1,0:T(8,128)(2,1)} %gather_fusion.3, pred[4]{0:T(512)(128)(4,1)} %get-tuple-element.112), kind=kOutput, calls=%fused_computation.43 | convolution fusion | flops 810291200 | bytes 4468740 | tf_op jit(solution)/shard_map/ktr,krc->tc/dot_general | solution.py:159
  167.8 16.8 %collective-permute-done.9 = bf16[3,512,512]{2,1,0:T(8,128)(2,1)} collective-permute-done((bf16[3,512,512]{2,1,0:T(8,128)(2,1)}, bf16[3,512,512]{2,1,0:T(8,128)(2,1)}, u32[]{:S(2)}, u32[]{:S(2)}) %collective-permute-start.9) | collective-permute-done | bytes 1572896 | tf_op jit(solution)/shard_map/ppermute | solution.py:127
  193.2 2.7 %convolution_bitcast_fusion.5 = f32[3,32,64,16]{2,3,0,1:T(8,128)} fusion(f32[32,64,128]{2,1,0:T(8,128)S(1)} %copy-done.6, f32[3,128,32,16]{1,0,3,2:T(4,128)S(1)} %reshape.139), kind=kOutput, calls=%fused_computation.49 | convolution fusion | flops 150994944 | bytes 2228224 | tf_op jit(solution)/shard_map/gni,bigc->bgnc/dot_general | solution.py:179
  195.9 5.5 %while.13 = (s32[]{:T(128)}, f32[32,64,16]{1,2,0:T(8,128)S(1)}, f32[3,32,64,16]{2,3,1,0:T(8,128)}, f32[32,64,1]{1,0,2:T(8,128)S(1)}, f32[3,32,64,16]{2,3,0,1:T(8,128)}, /*index=5*/s32[]{:T(128)}, s32[]{:T(128)}) while((s32[]{:T(128)}, f32[32,64,16]{1,2,0:T(8,128)S(1)}, f32[3,32,64,16]{2,3,1,0:T(8,128)}, ...), condition=%wide.region_2.5_spmd.clone, body=%wide.region_1.4_spmd.clone.sunk | while | flops 131075 | bytes 795228 | solution.py:186
  201.4 2.6 %collective-permute-start.24 = (f32[32,64,16]{1,2,0:T(8,128)S(1)}, f32[32,64,16]{1,2,0:T(8,128)S(1)}, u32[]{:S(2)}, u32[]{:S(2)}) collective-permute-start(f32[32,64,16]{1,2,0:T(8,128)S(1)} %get-tuple-element.52), channel_id=1, source_target_pairs={{0,4},{4,8},{8,12},{1,5},{5,9},{9,13},{2,6},{6,10},{10,14},{3,7},{... | collective-permute-start | bytes 393224 | tf_op jit(solution)/shard_map/ppermute | solution.py:190
  207.2 2.5 %convolution_bitcast_fusion.3 = f32[386,512]{1,0:T(8,128)S(1)} fusion(bf16[4,512,512]{2,1,0:T(8,128)(2,1)S(1)} %copy-done.1, bf16[4,386,512]{2,1,0:T(8,128)(2,1)} %gather_fusion.3, pred[4]{0:T(512)(128)(4,1)S(1)} %copy-done.43), kind=kOutput, calls=%fused_computation.42 | convolution fusion | flops 810291200 | bytes 4468740 | tf_op jit(solution)/shard_map/ktr,krc->tc/dot_general | solution.py:159
  212.1 2.6 %collective-permute-done.25 = f32[32,64,16]{1,2,0:T(8,128)S(1)} collective-permute-done((f32[32,64,16]{1,2,0:T(8,128)S(1)}, f32[32,64,16]{1,2,0:T(8,128)S(1)}, u32[]{:S(2)}, u32[]{:S(2)}) %collective-permute-start.25) | collective-permute-done | bytes 131104 | tf_op jit(solution)/shard_map/ppermute | solution.py:190
  214.7 2.8 %collective-permute-done.26 = f32[32,64,16]{1,2,0:T(8,128)S(1)} collective-permute-done((f32[32,64,16]{1,2,0:T(8,128)S(1)}, f32[32,64,16]{1,2,0:T(8,128)S(1)}, u32[]{:S(2)}, u32[]{:S(2)}) %collective-permute-start.26) | collective-permute-done | bytes 131104 | tf_op jit(solution)/shard_map/ppermute | solution.py:190
  218.9 3.4 %fusion.25 = f32[3,128,32,16]{1,3,0,2:T(8,128)S(1)} fusion(f32[32,3,16,128]{3,2,1,0:T(8,128)S(1)} %fusion.41, f32[32,128,128]{2,1,0:T(8,128)S(1)} %copy-done.11, f32[3,128,32,16]{1,0,3,2:T(4,128)S(1)} %reshape.139), kind=kOutput, calls=%fused_computation.48 | convolution fusion | flops 302186496 | bytes 4456448 | tf_op jit(solution)/shard_map/gij,bjgc->bigc/dot_general | solution.py:178
  228.5 7.2 %collective-permute-done.27 = bf16[1,384,512]{2,1,0:T(8,128)(2,1)S(1)} collective-permute-done((bf16[1,384,512]{2,1,0:T(8,128)(2,1)S(1)}, bf16[1,384,512]{2,1,0:T(8,128)(2,1)S(1)}, u32[]{:S(2)}, u32[]{:S(2)}) %collective-permute-start.27) | collective-permute-done | bytes 393248 | tf_op jit(solution)/shard_map/ppermute | solution.py:57
  239.1 5.1 %fusion.13 = bf16[384,1024]{1,0:T(8,128)(2,1)} fusion(bf16[384,1024]{1,0:T(8,128)(2,1)} %param.15, bf16[4,512,1024]{2,1,0:T(8,128)(2,1)} %bitcast.176, bf16[4,384,512]{2,1,0:T(8,128)(2,1)S(1)} %gather_fusion.1, pred[4]{0:T(512)(128)(4,1)S(1)} %copy-done.41), kind=kOutput, calls=%fused_computation.35 | convolution fusion | flops 1612578816 | bytes 7340036 | tf_op jit(solution)/shard_map/qtc,qcf->tf/dot_general | solution.py:201
  (205 shorter events, 95.2 us)
Async XLA Ops:
  3.0 31.2 %collective-permute-start.1 = (bf16[512,512]{1,0:T(8,128)(2,1)}, bf16[512,512]{1,0:T(8,128)(2,1)S(1)}, u32[]{:S(2)}, u32[]{:S(2)}) collective-permute-start(bf16[512,512]{1,0:T(8,128)(2,1)} %get-tuple-element.126), channel_id=1, source_target_pairs={{0,4},{4,8},{8,12},{1,5},{5,9},{9,13},{2,6},{6,10},{10,14},{3,7},{... | collective-permute-start | bytes 1572872 | tf_op jit(solution)/shard_map/ppermute | solution.py:114
  8.0 28.6 %collective-permute-start = (bf16[512,512]{1,0:T(8,128)(2,1)}, bf16[512,512]{1,0:T(8,128)(2,1)}, u32[]{:S(2)}, u32[]{:S(2)}) collective-permute-start(bf16[512,512]{1,0:T(8,128)(2,1)} %get-tuple-element.126), channel_id=1, source_target_pairs={{4,0},{8,4},{12,8},{5,1},{9,5},{13,9},{6,2},{10,6},{14,10},{7,3},{... | collective-permute-start | bytes 1572872 | tf_op jit(solution)/shard_map/ppermute | solution.py:115
  9.4 45.3 %collective-permute-start.6 = (bf16[1,385,1024]{2,1,0:T(8,128)(2,1)S(1)}, bf16[1,385,1024]{2,1,0:T(8,128)(2,1)S(1)}, u32[]{:S(2)}, u32[]{:S(2)}) collective-permute-start(bf16[1,385,1024]{2,1,0:T(8,128)(2,1)S(1)} %maximum_bitcast_fusion), channel_id=1, source_target_pairs={{0,2},{1,3},{2,0},{3,1},{4,6},{5,7},{6,4},{7,5},{8,10},{9,11},{10,... | collective-permute-start | bytes 2365448 | tf_op jit(solution)/shard_map/ppermute | solution.py:57
  10.9 26.9 %collective-permute-start.11 = (bf16[512,512]{1,0:T(8,128)(2,1)}, bf16[512,512]{1,0:T(8,128)(2,1)S(1)}, u32[]{:S(2)}, u32[]{:S(2)}) collective-permute-start(bf16[512,512]{1,0:T(8,128)(2,1)} %get-tuple-element.124), channel_id=1, source_target_pairs={{0,4},{4,8},{8,12},{1,5},{5,9},{9,13},{2,6},{6,10},{10,14},{3,7},{... | collective-permute-start | bytes 1572872 | tf_op jit(solution)/shard_map/ppermute | solution.py:114
  15.5 28.3 %collective-permute-start.18 = (bf16[512,512]{1,0:T(8,128)(2,1)}, bf16[512,512]{1,0:T(8,128)(2,1)}, u32[]{:S(2)}, u32[]{:S(2)}) collective-permute-start(bf16[512,512]{1,0:T(8,128)(2,1)} %get-tuple-element.125), channel_id=1, source_target_pairs={{0,4},{4,8},{8,12},{1,5},{5,9},{9,13},{2,6},{6,10},{10,14},{3,7},{... | collective-permute-start | bytes 1572872 | tf_op jit(solution)/shard_map/ppermute | solution.py:114
  34.1 17.0 %collective-permute-start.17 = (bf16[512,512]{1,0:T(8,128)(2,1)}, bf16[512,512]{1,0:T(8,128)(2,1)}, u32[]{:S(2)}, u32[]{:S(2)}) collective-permute-start(bf16[512,512]{1,0:T(8,128)(2,1)} %get-tuple-element.125), channel_id=1, source_target_pairs={{4,0},{8,4},{12,8},{5,1},{9,5},{13,9},{6,2},{10,6},{14,10},{7,3},{... | collective-permute-start | bytes 1572872 | tf_op jit(solution)/shard_map/ppermute | solution.py:115
  36.5 25.8 %collective-permute-start.10 = (bf16[512,512]{1,0:T(8,128)(2,1)}, bf16[512,512]{1,0:T(8,128)(2,1)}, u32[]{:S(2)}, u32[]{:S(2)}) collective-permute-start(bf16[512,512]{1,0:T(8,128)(2,1)} %get-tuple-element.124), channel_id=1, source_target_pairs={{4,0},{8,4},{12,8},{5,1},{9,5},{13,9},{6,2},{10,6},{14,10},{7,3},{... | collective-permute-start | bytes 1572872 | tf_op jit(solution)/shard_map/ppermute | solution.py:115
  37.8 28.1 %collective-permute-start.2 = (bf16[512,512]{1,0:T(8,128)(2,1)S(1)}, bf16[512,512]{1,0:T(8,128)(2,1)}, u32[]{:S(2)}, u32[]{:S(2)}) collective-permute-start(bf16[512,512]{1,0:T(8,128)(2,1)S(1)} %collective-permute-done.1), channel_id=1, source_target_pairs={{0,4},{4,8},{8,12},{1,5},{5,9},{9,13},{2,6},{6,10},{10,14},{3,7},{... | collective-permute-start | bytes 1572872 | tf_op jit(solution)/shard_map/ppermute | solution.py:114
  43.8 29.8 %collective-permute-start.4 = (bf16[512,512]{1,0:T(8,128)(2,1)}, bf16[512,512]{1,0:T(8,128)(2,1)}, u32[]{:S(2)}, u32[]{:S(2)}) collective-permute-start(bf16[512,512]{1,0:T(8,128)(2,1)} %collective-permute-done), channel_id=1, source_target_pairs={{4,0},{8,4},{12,8},{5,1},{9,5},{13,9},{6,2},{10,6},{14,10},{7,3},{... | collective-permute-start | bytes 1572872 | tf_op jit(solution)/shard_map/ppermute | solution.py:115
  51.1 23.6 %collective-permute-start.19 = (bf16[512,512]{1,0:T(8,128)(2,1)}, bf16[512,512]{1,0:T(8,128)(2,1)S(1)}, u32[]{:S(2)}, u32[]{:S(2)}) collective-permute-start(bf16[512,512]{1,0:T(8,128)(2,1)} %collective-permute-done.18), channel_id=1, source_target_pairs={{0,4},{4,8},{8,12},{1,5},{5,9},{9,13},{2,6},{6,10},{10,14},{3,7},{... | collective-permute-start | bytes 1572872 | tf_op jit(solution)/shard_map/ppermute | solution.py:114
  54.7 30.1 %collective-permute-start.21 = (bf16[512,512]{1,0:T(8,128)(2,1)}, bf16[512,512]{1,0:T(8,128)(2,1)S(1)}, u32[]{:S(2)}, u32[]{:S(2)}) collective-permute-start(bf16[512,512]{1,0:T(8,128)(2,1)} %collective-permute-done.17), channel_id=1, source_target_pairs={{4,0},{8,4},{12,8},{5,1},{9,5},{13,9},{6,2},{10,6},{14,10},{7,3},{... | collective-permute-start | bytes 1572872 | tf_op jit(solution)/shard_map/ppermute | solution.py:115
  62.4 23.7 %collective-permute-start.12 = (bf16[512,512]{1,0:T(8,128)(2,1)S(1)}, bf16[512,512]{1,0:T(8,128)(2,1)S(1)}, u32[]{:S(2)}, u32[]{:S(2)}) collective-permute-start(bf16[512,512]{1,0:T(8,128)(2,1)S(1)} %collective-permute-done.11), channel_id=1, source_target_pairs={{0,4},{4,8},{8,12},{1,5},{5,9},{9,13},{2,6},{6,10},{10,14},{3,7},{... | collective-permute-start | bytes 1572872 | tf_op jit(solution)/shard_map/ppermute | solution.py:114
  65.9 30.1 %collective-permute-start.14 = (bf16[512,512]{1,0:T(8,128)(2,1)}, bf16[512,512]{1,0:T(8,128)(2,1)S(1)}, u32[]{:S(2)}, u32[]{:S(2)}) collective-permute-start(bf16[512,512]{1,0:T(8,128)(2,1)} %collective-permute-done.10), channel_id=1, source_target_pairs={{4,0},{8,4},{12,8},{5,1},{9,5},{13,9},{6,2},{10,6},{14,10},{7,3},{... | collective-permute-start | bytes 1572872 | tf_op jit(solution)/shard_map/ppermute | solution.py:115
  73.6 56.3 %collective-permute-start.7 = (bf16[2,385,1024]{2,0,1:T(2,128)(2,1)S(1)}, bf16[2,385,1024]{2,0,1:T(2,128)(2,1)S(1)}, u32[]{:S(2)}, u32[]{:S(2)}) collective-permute-start(bf16[2,385,1024]{2,0,1:T(2,128)(2,1)S(1)} %copy.41), channel_id=1, source_target_pairs={{0,1},{1,0},{2,3},{3,2},{4,5},{5,4},{6,7},{7,6},{8,9},{9,8},{10,11... | collective-permute-start | bytes 4730888 | tf_op jit(solution)/shard_map/ppermute | solution.py:57
  74.7 42.1 %collective-permute-start.3 = (bf16[512,512]{1,0:T(8,128)(2,1)}, bf16[512,512]{1,0:T(8,128)(2,1)S(1)}, u32[]{:S(2)}, u32[]{:S(2)}) collective-permute-start(bf16[512,512]{1,0:T(8,128)(2,1)} %collective-permute-done.2), channel_id=1, source_target_pairs={{0,4},{4,8},{8,12},{1,5},{5,9},{9,13},{2,6},{6,10},{10,14},{3,7},{... | collective-permute-start | bytes 1572872 | tf_op jit(solution)/shard_map/ppermute | solution.py:114
  84.7 22.5 %collective-permute-start.22 = (bf16[512,512]{1,0:T(8,128)(2,1)S(1)}, bf16[512,512]{1,0:T(8,128)(2,1)S(1)}, u32[]{:S(2)}, u32[]{:S(2)}) collective-permute-start(bf16[512,512]{1,0:T(8,128)(2,1)S(1)} %collective-permute-done.21), channel_id=1, source_target_pairs={{4,0},{8,4},{12,8},{5,1},{9,5},{13,9},{6,2},{10,6},{14,10},{7,3},{... | collective-permute-start | bytes 1572872 | tf_op jit(solution)/shard_map/ppermute | solution.py:115
  86.1 29.3 %copy-start.12 = (bf16[1,512,512]{2,1,0:T(8,128)(2,1)}, bf16[1,512,512]{2,1,0:T(8,128)(2,1)S(1)}, u32[]{:S(2)}) copy-start(bf16[1,512,512]{2,1,0:T(8,128)(2,1)S(1)} %select_bitcast_fusion.1) | copy-start | bytes 1572868
  86.1 33.4 %collective-permute-start.5 = (bf16[512,512]{1,0:T(8,128)(2,1)}, bf16[512,512]{1,0:T(8,128)(2,1)S(1)}, u32[]{:S(2)}, u32[]{:S(2)}) collective-permute-start(bf16[512,512]{1,0:T(8,128)(2,1)} %collective-permute-done.4), channel_id=1, source_target_pairs={{4,0},{8,4},{12,8},{5,1},{9,5},{13,9},{6,2},{10,6},{14,10},{7,3},{... | collective-permute-start | bytes 1572872 | tf_op jit(solution)/shard_map/ppermute | solution.py:115
  96.0 12.6 %collective-permute-start.20 = (bf16[512,512]{1,0:T(8,128)(2,1)S(1)}, bf16[512,512]{1,0:T(8,128)(2,1)S(1)}, u32[]{:S(2)}, u32[]{:S(2)}) collective-permute-start(bf16[512,512]{1,0:T(8,128)(2,1)S(1)} %collective-permute-done.19), channel_id=1, source_target_pairs={{0,4},{4,8},{8,12},{1,5},{5,9},{9,13},{2,6},{6,10},{10,14},{3,7},{... | collective-permute-start | bytes 1572872 | tf_op jit(solution)/shard_map/ppermute | solution.py:114
  107.2 19.9 %collective-permute-start.15 = (bf16[512,512]{1,0:T(8,128)(2,1)S(1)}, bf16[512,512]{1,0:T(8,128)(2,1)S(1)}, u32[]{:S(2)}, u32[]{:S(2)}) collective-permute-start(bf16[512,512]{1,0:T(8,128)(2,1)S(1)} %collective-permute-done.14), channel_id=1, source_target_pairs={{4,0},{8,4},{12,8},{5,1},{9,5},{13,9},{6,2},{10,6},{14,10},{7,3},{... | collective-permute-start | bytes 1572872 | tf_op jit(solution)/shard_map/ppermute | solution.py:115
  108.6 19.4 %collective-permute-start.13 = (bf16[512,512]{1,0:T(8,128)(2,1)S(1)}, bf16[512,512]{1,0:T(8,128)(2,1)S(1)}, u32[]{:S(2)}, u32[]{:S(2)}) collective-permute-start(bf16[512,512]{1,0:T(8,128)(2,1)S(1)} %collective-permute-done.12), channel_id=1, source_target_pairs={{0,4},{4,8},{8,12},{1,5},{5,9},{9,13},{2,6},{6,10},{10,14},{3,7},{... | collective-permute-start | bytes 1572872 | tf_op jit(solution)/shard_map/ppermute | solution.py:114
  116.8 47.2 %collective-permute-start.23 = (bf16[3,512,512]{2,1,0:T(8,128)(2,1)}, bf16[3,512,512]{2,1,0:T(8,128)(2,1)}, u32[]{:S(2)}, u32[]{:S(2)}) collective-permute-start(bf16[3,512,512]{2,1,0:T(8,128)(2,1)} %pad_maximum_fusion.4), channel_id=1, source_target_pairs={{0,16},{16,0},{1,17},{17,1},{2,18},{18,2},{3,19},{19,3},{4,20},{20... | collective-permute-start | bytes 4718600 | tf_op jit(solution)/shard_map/ppermute | solution.py:127
  136.6 7.3 %collective-permute-start.8 = (bf16[2,4096]{1,0:T(2,128)(2,1)S(1)}, bf16[2,4096]{1,0:T(2,128)(2,1)S(1)}, u32[]{:S(2)}, u32[]{:S(2)}) collective-permute-start(bf16[2,4096]{1,0:T(2,128)(2,1)S(1)} %pad_maximum_fusion.7), channel_id=1, source_target_pairs={{0,4},{4,8},{8,12},{1,5},{5,9},{9,13},{2,6},{6,10},{10,14},{3,7},{... | collective-permute-start | bytes 49160 | tf_op jit(solution)/shard_map/ppermute | solution.py:12
  150.6 34.1 %collective-permute-start.9 = (bf16[3,512,512]{2,1,0:T(8,128)(2,1)}, bf16[3,512,512]{2,1,0:T(8,128)(2,1)}, u32[]{:S(2)}, u32[]{:S(2)}) collective-permute-start(bf16[3,512,512]{2,1,0:T(8,128)(2,1)} %slice.122), channel_id=1, source_target_pairs={{0,16},{16,0},{1,17},{17,1},{2,18},{18,2},{3,19},{19,3},{4,20},{20... | collective-permute-start | bytes 4718600 | tf_op jit(solution)/shard_map/ppermute | solution.py:127
  167.8 19.1 %copy-start.38 = (f32[1,1,512]{2,1,0:T(1,128)S(1)}, f32[1,1,512]{2,1,0:T(1,128)}, u32[]{:S(2)}) copy-start(f32[1,1,512]{2,1,0:T(1,128)} %get-tuple-element.133) | copy-start | bytes 6148
  167.8 19.1 %copy-start.39 = (f32[1,1,512]{2,1,0:T(1,128)S(1)}, f32[1,1,512]{2,1,0:T(1,128)}, u32[]{:S(2)}) copy-start(f32[1,1,512]{2,1,0:T(1,128)} %get-tuple-element.134) | copy-start | bytes 6148
  191.7 33.2 %collective-permute-start.16 = (bf16[3,512,512]{2,1,0:T(8,128)(2,1)}, bf16[3,512,512]{2,1,0:T(8,128)(2,1)}, u32[]{:S(2)}, u32[]{:S(2)}) collective-permute-start(bf16[3,512,512]{2,1,0:T(8,128)(2,1)} %slice.137), channel_id=1, source_target_pairs={{0,16},{16,0},{1,17},{17,1},{2,18},{18,2},{3,19},{19,3},{4,20},{20... | collective-permute-start | bytes 4718600 | tf_op jit(solution)/shard_map/ppermute | solution.py:127
  201.4 10.7 %collective-permute-start.24 = (f32[32,64,16]{1,2,0:T(8,128)S(1)}, f32[32,64,16]{1,2,0:T(8,128)S(1)}, u32[]{:S(2)}, u32[]{:S(2)}) collective-permute-start(f32[32,64,16]{1,2,0:T(8,128)S(1)} %get-tuple-element.52), channel_id=1, source_target_pairs={{0,4},{4,8},{8,12},{1,5},{5,9},{9,13},{2,6},{6,10},{10,14},{3,7},{... | collective-permute-start | bytes 393224 | tf_op jit(solution)/shard_map/ppermute | solution.py:190
  204.0 10.7 %collective-permute-start.25 = (f32[32,64,16]{1,2,0:T(8,128)S(1)}, f32[32,64,16]{1,2,0:T(8,128)S(1)}, u32[]{:S(2)}, u32[]{:S(2)}) collective-permute-start(f32[32,64,16]{1,2,0:T(8,128)S(1)} %get-tuple-element.52), channel_id=1, source_target_pairs={{0,8},{4,12},{1,9},{5,13},{2,10},{6,14},{3,11},{7,15},{16,24},{20,... | collective-permute-start | bytes 393224 | tf_op jit(solution)/shard_map/ppermute | solution.py:190
  205.9 11.6 %collective-permute-start.26 = (f32[32,64,16]{1,2,0:T(8,128)S(1)}, f32[32,64,16]{1,2,0:T(8,128)S(1)}, u32[]{:S(2)}, u32[]{:S(2)}) collective-permute-start(f32[32,64,16]{1,2,0:T(8,128)S(1)} %get-tuple-element.52), channel_id=1, source_target_pairs={{0,12},{1,13},{2,14},{3,15},{16,28},{17,29},{18,30},{19,31}} | collective-permute-start | bytes 393224 | tf_op jit(solution)/shard_map/ppermute | solution.py:190
  227.9 7.8 %collective-permute-start.27 = (bf16[1,384,512]{2,1,0:T(8,128)(2,1)S(1)}, bf16[1,384,512]{2,1,0:T(8,128)(2,1)S(1)}, u32[]{:S(2)}, u32[]{:S(2)}) collective-permute-start(bf16[1,384,512]{2,1,0:T(8,128)(2,1)S(1)} %fusion.73), channel_id=1, source_target_pairs={{0,2},{1,3},{2,0},{3,1},{4,6},{5,7},{6,4},{7,5},{8,10},{9,11},{10,... | collective-permute-start | bytes 1179656 | tf_op jit(solution)/shard_map/ppermute | solution.py:57
  235.8 2.4 collective-permute-start.28
  (41 other events, 184.5 us)

commit v3 on v1

--- a/solution.py
+++ b/solution.py
@@ -181,9 +181,30 @@
     late, conv_out = lax.optimization_barrier((relayed[last][1], conv_out))
     second = project(last, late)
     gated = (second * conv_out).astype(jnp.bfloat16)
-    pieces = gather_by_swaps(gated, "tp")
-    mixed = jnp.einsum("qtc,qcf->tf", pieces, w_out.reshape(pieces.shape[0], local_width, -1),
-                       preferred_element_type=jnp.float32)
+    count = lax.axis_size("tp")
+    me_tp = lax.axis_index("tp")
+
+    def contribution(block, source):
+        rows = lax.dynamic_slice_in_dim(w_out, source * local_width, local_width, axis=0)
+        return jnp.dot(block, rows, preferred_element_type=jnp.float32)
+
+    if count & (count - 1) == 0:
+        mixed = contribution(gated, me_tp)
+        held = gated[None]
+        masks = [0]
+        bit = count // 2
+        while bit >= 1:
+            pairs = [(q, q ^ bit) for q in range(count)]
+            arrived = lax.ppermute(held, "tp", pairs)
+            for q, m in enumerate(masks):
+                mixed = mixed + contribution(arrived[q], jnp.bitwise_xor(me_tp, m ^ bit))
+            held = jnp.concatenate([held, arrived], axis=0)
+            masks = masks + [m ^ bit for m in masks]
+            bit //= 2
+    else:
+        pieces = gather_by_swaps(gated, "tp")
+        mixed = jnp.einsum("qtc,qcf->tf", pieces, w_out.reshape(pieces.shape[0], local_width, -1),
+                           preferred_element_type=jnp.float32)
     return (tokens.astype(jnp.float32) + mixed).astype(jnp.bfloat16)
 
 

time: 222 us -> 220 us (level)
    ppermute x4 -> x2, waiting for transfers between devices: 25.3 us -> 14.7 us  [gather_by_swaps(): held = jnp.concatenate([held, lax.ppermute(held, axis, pairs)], axis=0)]
    ppermute x0 -> x2, waiting for transfers between devices: none -> 8.37 us  [body(): arrived = lax.ppermute(held, 'tp', pairs)]
    ppermute x4 -> x2, starting transfers between devices: 4.71 us -> 3.1 us  [gather_by_swaps(): held = jnp.concatenate([held, lax.ppermute(held, axis, pairs)], axis=0)]
    dot_general x1 -> x4, matrix products: 5.1 us -> 5.94 us  [contribution(): return jnp.dot(block, rows, preferred_element_type=jnp.float32)]
    unnamed x84 -> x82, local copies, waits for them, and re-layouts: 6.37 us -> 6.89 us
  transfers between devices with their start and end apart: 14 -> 14, of which waited for: 9 -> 8; matrix products, arithmetic and copies ran while one was open for 28% -> 30% of each run, Pallas kernels for 0% -> 0%
where the time goes in v3:
time: 220 us
  waiting for transfers between devices  99.2 us (45%)
  matrix products  33.6 us (15%)
  other arithmetic  27.3 us (12%)
  local copies, waits for them, and re-layouts  24.9 us (11%)
  starting transfers between devices  20.7 us (9%)
  between operations  14 us (6%)
    all_gather x3, waiting for transfers between devices, body(): got = lax.all_gather(own[:, s, :], 'ctx', axis=0)  62.1 us
    ppermute x2, waiting for transfers between devices, gather_by_swaps(): held = jnp.concatenate([held, lax.ppermute(held, axis, pairs)], axis=0)  14.7 us
    concatenate x3, other arithmetic, relay_send(): doubled = jnp.concatenate([got, got], axis=0)  9.73 us
    ppermute x2, waiting for transfers between devices, body(): arrived = lax.ppermute(held, 'tp', pairs)  8.37 us
    ppermute x3, starting transfers between devices, body(): arrived = lax.ppermute(own_state, 'ctx', pairs)  7.12 us
    unnamed x82, local copies, waits for them, and re-layouts  6.89 us
    dot_general x3, matrix products, project(): jnp.einsum('ktr,krc->tc', part[1:], recv, preferred_element_type=jnp.floa...  6.87 us
    ppermute x3, waiting for transfers between devices, body(): arrived = lax.ppermute(own_state, 'ctx', pairs)  6.71 us
  transfers between devices with their start and end apart: 14, of which 8 were waited for; matrix products, arithmetic and copies ran while one was open for 30% of the time, Pallas kernels for 0%

profile of v3, /device:TPU:0, one launch (start us, length us, event | category | flops | bytes accessed | tf_op | source)
XLA Modules:
  0.0 219.7 jit_solution(16810002187112651789)
XLA Ops:
  6.5 2.6 %constant_dynamic-slice_fusion.2 = (bf16[512,1,512]{2,0,1:T(8,128)(2,1)}, bf16[512,1,512]{2,0,1:T(8,128)(2,1)}, bf16[512,1,512]{2,0,1:T(8,128)(2,1)}) fusion(bf16[1024,3,512]{2,0,1:T(8,128)(2,1)} %param.14, s32[]{:T(128)S(6)} %select_n.104, s32[]{:T(128)S(6)} %add.242, s32[]{:T(128)S(6)} %add.241), kind=kLoop, calls=%fused_computation.136 | loop fusion | bytes 3145740 | tf_op jit(solution)/shard_map/slice | solution.py:117
  10.1 3.0 %collective-permute-start = (bf16[1,385,1024]{2,1,0:T(8,128)(2,1)S(1)}, bf16[1,385,1024]{2,1,0:T(8,128)(2,1)S(1)}, u32[]{:S(2)}, u32[]{:S(2)}) collective-permute-start(bf16[1,385,1024]{2,1,0:T(8,128)(2,1)S(1)} %maximum_bitcast_fusion), channel_id=1, source_target_pairs={{0,2},{1,3},{2,0},{3,1},{4,6},{5,7},{6,4},{7,5},{8,10},{9,11},{10,... | collective-permute-start | bytes 2365448 | tf_op jit(solution)/shard_map/ppermute | solution.py:57
  16.3 14.6 %collective-permute-done = bf16[1,385,1024]{2,1,0:T(8,128)(2,1)S(1)} collective-permute-done((bf16[1,385,1024]{2,1,0:T(8,128)(2,1)S(1)}, bf16[1,385,1024]{2,1,0:T(8,128)(2,1)S(1)}, u32[]{:S(2)}, u32[]{:S(2)}) %collective-permute-start) | collective-permute-done | bytes 788512 | tf_op jit(solution)/shard_map/ppermute | solution.py:57
  36.6 5.5 %convolution_select_fusion = f32[32,128,128]{2,1,0:T(8,128)} fusion(pred[128,128]{1,0:T(8,128)(4,1)S(1)} %broadcast_compare_fusion, f32[32,64]{1,0:T(8,128)S(1)} %copy-done.26, f32[128]{0:T(128)S(1)} %iota_convert_fusion.1, f32[32,64]{1,0:T(8,128)S(1)} %get-tuple-element.136, f32[32,64]{1,0:T(8,128)S(1)} %get-tuple-element.135), kind=kOutput, calls=%fused_computation.23 | convolution fusion | flops 403963904 | bytes 2138624 | tf_op jit(solution)/shard_map/gin,gjn->gij/dot_general | solution.py:91
  42.1 1.8 fusion.73
  44.3 2.0 pad_maximum_fusion
  46.3 2.7 %gather_fusion.1 = bf16[4,385,1024]{2,1,0:T(8,128)(2,1)S(1)} fusion(bf16[4,385,1024]{2,1,0:T(8,128)(2,1)} %pad_maximum_fusion, s32[1024]{0:T(1024)S(1)} %pad_clamp_fusion.2), kind=kCustom, calls=%fused_computation.3 | custom fusion | bytes 6307856 | tf_op jit(solution)/shard_map/jit(_take)/gather | solution.py:62
  51.3 4.3 %collective-permute-start.2 = (bf16[2,4096]{1,0:T(2,128)(2,1)S(1)}, bf16[2,4096]{1,0:T(2,128)(2,1)}, u32[]{:S(2)}, u32[]{:S(2)}) collective-permute-start(bf16[2,4096]{1,0:T(2,128)(2,1)S(1)} %pad_maximum_fusion.3), channel_id=1, source_target_pairs={{0,4},{4,8},{8,12},{1,5},{5,9},{9,13},{2,6},{6,10},{10,14},{3,7},{... | collective-permute-start | bytes 49160 | tf_op jit(solution)/shard_map/ppermute | solution.py:12
  56.5 3.5 %maximum_maximum_fusion = bf16[387,4096]{1,0:T(8,128)(2,1)S(1)} fusion(bf16[385,1024]{1,0:T(8,128)(2,1)} %copy-done.2, bf16[385,1024]{1,0:T(8,128)(2,1)} %copy-done.3, bf16[385,1024]{1,0:T(8,128)(2,1)} %copy-done.4, bf16[385,1024]{1,0:T(8,128)(2,1)} %copy-done.1, bf16[2,4096]{1,0:T(2,128)(2,1)} %collective-permute-done.2), kind=kLoop, calls=%fused_computation.18 | loop fusion | flops 15851520 | bytes 6340608 | tf_op jit(solution)/shard_map/concatenate | solution.py:100
  60.0 3.2 %fusion.7 = bf16[3,512,512]{2,1,0:T(8,128)(2,1)} fusion(s32[]{:T(128)S(6)} %select_n.106, bf16[4,512,512]{2,1,0:T(8,128)(2,1)} %bitcast.152), kind=kLoop, calls=%fused_computation.29 | loop fusion | flops 786432 | bytes 3670020 | tf_op jit(solution)/shard_map/concatenate | solution.py:104
  67.8 1.9 gather_fusion.3
  69.7 2.0 gather_fusion.2
  73.2 30.5 %all-gather.11.cloned.1.call-done = bf16[2048,1,512]{2,0,1:T(8,128)(2,1)} async-done(((bf16[512,1,512]{2,0,1:T(8,128)(2,1)}), bf16[2048,1,512]{2,0,1:T(8,128)(2,1)}) %all-gather.11.cloned.1.call-update) | async-done | bytes 2097168 | tf_op jit(solution)/shard_map/all_gather | solution.py:117
  103.8 3.3 %fusion.5 = bf16[3,512,512]{2,1,0:T(8,128)(2,1)} fusion(s32[]{:T(128)S(6)} %select_n.106, bf16[4,512,512]{2,1,0:T(8,128)(2,1)} %bitcast.154), kind=kLoop, calls=%fused_computation.27 | loop fusion | flops 786432 | bytes 3670020 | tf_op jit(solution)/shard_map/concatenate | solution.py:104
  108.5 2.5 %convolution_bitcast_fusion.5 = f32[386,512]{1,0:T(8,128)S(1)} fusion(bf16[4,512,512]{2,1,0:T(8,128)(2,1)S(1)} %bitcast.153, bf16[4,386,512]{2,1,0:T(8,128)(2,1)} %gather_fusion.2, pred[4]{0:T(512)(128)(4,1)S(1)} %copy-done.39), kind=kOutput, calls=%fused_computation.36 | convolution fusion | flops 810291200 | bytes 4468740 | tf_op jit(solution)/shard_map/ktr,krc->tc/dot_general | solution.py:143
  115.8 2.2 %fusion.15 = f32[386,512]{1,0:T(8,128)S(1)} fusion(f32[386,512]{1,0:T(8,128)S(1)} %convolution_add_fusion.2, bf16[4,386,512]{2,1,0:T(8,128)(2,1)S(1)} %broadcast_select_fusion.1, bf16[3,512,512]{2,1,0:T(8,128)(2,1)} %collective-permute-done.3), kind=kOutput, calls=%fused_computation.44 | convolution fusion | flops 607520768 | bytes 4734976 | tf_op jit(solution)/shard_map/ktr,krc->tc/dot_general | solution.py:147
  118.3 31.5 %all-gather.9.cloned.1.call-done = bf16[2048,1,512]{2,0,1:T(8,128)(2,1)} async-done(((bf16[512,1,512]{2,0,1:T(8,128)(2,1)}), bf16[2048,1,512]{2,0,1:T(8,128)(2,1)}) %all-gather.9.cloned.1.call-update) | async-done | bytes 2097168 | tf_op jit(solution)/shard_map/all_gather | solution.py:117
  149.9 2.2 %fusion.17 = f32[386,512]{1,0:T(8,128)S(1)} fusion(f32[386,512]{1,0:T(8,128)S(1)} %convolution_add_fusion, bf16[4,386,512]{2,1,0:T(8,128)(2,1)S(1)} %broadcast_select_fusion.1, bf16[3,512,512]{2,1,0:T(8,128)(2,1)} %collective-permute-done.5), kind=kOutput, calls=%fused_computation.46 | convolution fusion | flops 607520768 | bytes 4734976 | tf_op jit(solution)/shard_map/ktr,krc->tc/dot_general | solution.py:147
  153.0 3.3 %fusion.6 = bf16[3,512,512]{2,1,0:T(8,128)(2,1)} fusion(s32[]{:T(128)S(6)} %select_n.106, bf16[4,512,512]{2,1,0:T(8,128)(2,1)} %bitcast.150), kind=kLoop, calls=%fused_computation.28 | loop fusion | flops 786432 | bytes 3670020 | tf_op jit(solution)/shard_map/concatenate | solution.py:104
  157.7 2.0 convolution_bitcast_fusion.6
  159.7 2.6 %while.13 = (s32[]{:T(128)}, f32[32,64,16]{1,2,0:T(8,128)S(1)}, f32[3,32,64,16]{2,3,1,0:T(8,128)}, f32[32,64,1]{1,0,2:T(8,128)S(1)}, f32[3,32,64,16]{2,3,0,1:T(8,128)S(1)}, /*index=5*/s32[]{:T(128)}, s32[]{:T(128)}) while((s32[]{:T(128)}, f32[32,64,16]{1,2,0:T(8,128)S(1)}, f32[3,32,64,16]{2,3,1,0:T(8,128)}, ...), condition=%wide.region_2.4_spmd.clone, body=%wide.region_1.3_spmd.clone.sunk | while | flops 131075 | bytes 795228 | solution.py:170
  162.3 2.3 %collective-permute-start.6 = (f32[32,64,16]{1,2,0:T(8,128)S(1)}, f32[32,64,16]{1,2,0:T(8,128)S(1)}, u32[]{:S(2)}, u32[]{:S(2)}) collective-permute-start(f32[32,64,16]{1,2,0:T(8,128)S(1)} %get-tuple-element.51), channel_id=1, source_target_pairs={{0,4},{4,8},{8,12},{1,5},{5,9},{9,13},{2,6},{6,10},{10,14},{3,7},{... | collective-permute-start | bytes 393224 | tf_op jit(solution)/shard_map/ppermute | solution.py:174
  164.6 3.5 %collective-permute-start.7 = (f32[32,64,16]{1,2,0:T(8,128)S(1)}, f32[32,64,16]{1,2,0:T(8,128)S(1)}, u32[]{:S(2)}, u32[]{:S(2)}) collective-permute-start(f32[32,64,16]{1,2,0:T(8,128)S(1)} %get-tuple-element.51), channel_id=1, source_target_pairs={{0,8},{4,12},{1,9},{5,13},{2,10},{6,14},{3,11},{7,15},{16,24},{20,... | collective-permute-start | bytes 393224 | tf_op jit(solution)/shard_map/ppermute | solution.py:174
  169.5 3.1 %convolution_bitcast_fusion.4 = f32[386,512]{1,0:T(8,128)S(1)} fusion(bf16[4,512,512]{2,1,0:T(8,128)(2,1)} %bitcast.151, bf16[4,386,512]{2,1,0:T(8,128)(2,1)} %gather_fusion.2, pred[4]{0:T(512)(128)(4,1)S(1)} %copy-done.39), kind=kOutput, calls=%fused_computation.35 | convolution fusion | flops 810291200 | bytes 4468740 | tf_op jit(solution)/shard_map/ktr,krc->tc/dot_general | solution.py:143
  174.0 2.8 %collective-permute-done.7 = f32[32,64,16]{1,2,0:T(8,128)S(1)} collective-permute-done((f32[32,64,16]{1,2,0:T(8,128)S(1)}, f32[32,64,16]{1,2,0:T(8,128)S(1)}, u32[]{:S(2)}, u32[]{:S(2)}) %collective-permute-start.7) | collective-permute-done | bytes 131104 | tf_op jit(solution)/shard_map/ppermute | solution.py:174
  176.8 3.9 %collective-permute-done.8 = f32[32,64,16]{1,2,0:T(8,128)S(1)} collective-permute-done((f32[32,64,16]{1,2,0:T(8,128)S(1)}, f32[32,64,16]{1,2,0:T(8,128)S(1)}, u32[]{:S(2)}, u32[]{:S(2)}) %collective-permute-start.8) | collective-permute-done | bytes 131104 | tf_op jit(solution)/shard_map/ppermute | solution.py:174
  182.4 3.4 %fusion.11 = f32[3,128,32,16]{1,3,0,2:T(8,128)S(1)} fusion(f32[32,3,16,128]{3,2,1,0:T(8,128)S(1)} %fusion.20, f32[32,128,128]{2,1,0:T(8,128)S(1)} %copy-done.18, f32[3,128,32,16]{1,0,3,2:T(4,128)S(1)} %reshape.174), kind=kOutput, calls=%fused_computation.41 | convolution fusion | flops 302186496 | bytes 4456448 | tf_op jit(solution)/shard_map/gij,bjgc->bigc/dot_general | solution.py:162
  186.3 6.3 %collective-permute-done.4 = bf16[3,512,512]{2,1,0:T(8,128)(2,1)} collective-permute-done((bf16[3,512,512]{2,1,0:T(8,128)(2,1)}, bf16[3,512,512]{2,1,0:T(8,128)(2,1)}, u32[]{:S(2)}, u32[]{:S(2)}) %collective-permute-start.4) | collective-permute-done | bytes 1572896 | tf_op jit(solution)/shard_map/ppermute | solution.py:111
  193.7 2.5 %fusion.19 = f32[386,512]{1,0:T(8,128)S(1)} fusion(f32[386,512]{1,0:T(8,128)} %convolution_add_fusion.1, bf16[4,386,512]{2,1,0:T(8,128)(2,1)S(1)} %copy-done.8, bf16[3,512,512]{2,1,0:T(8,128)(2,1)} %collective-permute-done.4), kind=kOutput, calls=%fused_computation.48 | convolution fusion | flops 607520768 | bytes 4734976 | tf_op jit(solution)/shard_map/ktr,krc->tc/dot_general | solution.py:147
  198.1 8.4 %collective-permute-done.9 = bf16[1,384,512]{2,1,0:T(8,128)(2,1)S(1)} collective-permute-done((bf16[1,384,512]{2,1,0:T(8,128)(2,1)S(1)}, bf16[1,384,512]{2,1,0:T(8,128)(2,1)S(1)}, u32[]{:S(2)}, u32[]{:S(2)}) %collective-permute-start.9) | collective-permute-done | bytes 393248 | tf_op jit(solution)/shard_map/ppermute | solution.py:198
  206.6 1.9 fusion.31
  208.6 1.8 fusion.29
  (162 shorter events, 41.2 us)
Async XLA Ops:
  6.5 53.5 %all-gather.7.cloned.1.call-start = ((), (), s32[]{:S(2)}) async-start(), calls=%async_computation | async-start | bytes 2621440 | tf_op jit(solution)/shard_map/all_gather | solution.py:117
  6.5 3.4 %copy-start.37 = (bf16[1024]{0:T(1024)(128)(2,1)S(1)}, bf16[1024]{0:T(1024)(128)(2,1)}, u32[]{:S(2)}) copy-start(bf16[1024]{0:T(1024)(128)(2,1)} %param.13) | copy-start | bytes 6148
  6.5 3.5 %copy-start.12 = (bf16[384,1024]{1,0:T(8,128)(2,1)S(1)}, bf16[384,1024]{1,0:T(8,128)(2,1)}, u32[]{:S(2)}) copy-start(bf16[384,1024]{1,0:T(8,128)(2,1)} %param.12) | copy-start | bytes 2359300
  9.1 4.1 %copy-start = (s32[4]{0:T(128)S(1)}, s32[4]{0:T(128)}, u32[]{:S(2)}) copy-start(s32[4]{0:T(128)} %constant.130.clone) | copy-start | bytes 52
  9.2 94.6 %all-gather.11.cloned.1.call-start = ((), (), s32[]{:S(2)}) async-start(), calls=%async_computation.2 | async-start | bytes 2621440 | tf_op jit(solution)/shard_map/all_gather | solution.py:117
  9.2 6.5 %copy-start.27 = (f32[3,3,512]{2,1,0:T(4,128)S(1)}, f32[3,3,512]{2,1,0:T(4,128)}, u32[]{:S(2)}) copy-start(f32[3,3,512]{2,1,0:T(4,128)} %param.15) | copy-start | bytes 55300
  9.9 139.9 %all-gather.9.cloned.1.call-start = ((), (), s32[]{:S(2)}) async-start(), calls=%async_computation.1 | async-start | bytes 2621440 | tf_op jit(solution)/shard_map/all_gather | solution.py:117
  10.1 20.9 %collective-permute-start = (bf16[1,385,1024]{2,1,0:T(8,128)(2,1)S(1)}, bf16[1,385,1024]{2,1,0:T(8,128)(2,1)S(1)}, u32[]{:S(2)}, u32[]{:S(2)}) collective-permute-start(bf16[1,385,1024]{2,1,0:T(8,128)(2,1)S(1)} %maximum_bitcast_fusion), channel_id=1, source_target_pairs={{0,2},{1,3},{2,0},{3,1},{4,6},{5,7},{6,4},{7,5},{8,10},{9,11},{10,... | collective-permute-start | bytes 2365448 | tf_op jit(solution)/shard_map/ppermute | solution.py:57
  32.8 11.1 %collective-permute-start.1 = (bf16[2,385,1024]{2,0,1:T(2,128)(2,1)S(1)}, bf16[2,385,1024]{2,0,1:T(2,128)(2,1)S(1)}, u32[]{:S(2)}, u32[]{:S(2)}) collective-permute-start(bf16[2,385,1024]{2,0,1:T(2,128)(2,1)S(1)} %copy.40), channel_id=1, source_target_pairs={{0,1},{1,0},{2,3},{3,2},{4,5},{5,4},{6,7},{7,6},{8,9},{9,8},{10,11... | collective-permute-start | bytes 4730888 | tf_op jit(solution)/shard_map/ppermute | solution.py:57
  35.0 7.1 %copy-start.5 = (bf16[1024,3,512]{2,0,1:T(8,128)(2,1)S(1)}, bf16[1024,3,512]{2,0,1:T(8,128)(2,1)}, u32[]{:S(2)}) copy-start(bf16[1024,3,512]{2,0,1:T(8,128)(2,1)} %param.14) | copy-start | bytes 9437188
  51.3 5.1 %collective-permute-start.2 = (bf16[2,4096]{1,0:T(2,128)(2,1)S(1)}, bf16[2,4096]{1,0:T(2,128)(2,1)}, u32[]{:S(2)}, u32[]{:S(2)}) collective-permute-start(bf16[2,4096]{1,0:T(2,128)(2,1)S(1)} %pad_maximum_fusion.3), channel_id=1, source_target_pairs={{0,4},{4,8},{8,12},{1,5},{5,9},{9,13},{2,6},{6,10},{10,14},{3,7},{... | collective-permute-start | bytes 49160 | tf_op jit(solution)/shard_map/ppermute | solution.py:12
  71.7 44.1 %collective-permute-start.3 = (bf16[3,512,512]{2,1,0:T(8,128)(2,1)}, bf16[3,512,512]{2,1,0:T(8,128)(2,1)}, u32[]{:S(2)}, u32[]{:S(2)}) collective-permute-start(bf16[3,512,512]{2,1,0:T(8,128)(2,1)} %fusion.7), channel_id=1, source_target_pairs={{0,16},{16,0},{1,17},{17,1},{2,18},{18,2},{3,19},{19,3},{4,20},{20... | collective-permute-start | bytes 4718600 | tf_op jit(solution)/shard_map/ppermute | solution.py:111
  103.8 4.8 %copy-start.19 = (bf16[2048,1,512]{2,0,1:T(8,128)(2,1)S(1)}, bf16[2048,1,512]{2,0,1:T(8,128)(2,1)}, u32[]{:S(2)}) copy-start(bf16[2048,1,512]{2,0,1:T(8,128)(2,1)} %all-gather.7.cloned.1.call-done) | copy-start | bytes 6291460
  103.8 4.8 %copy-start.39 = (pred[4]{0:T(512)(128)(4,1)S(1)}, pred[4]{0:T(512)(128)(4,1)}, u32[]{:S(2)}) copy-start(pred[4]{0:T(512)(128)(4,1)} %compare_and_fusion.1) | copy-start | bytes 16
  107.0 3.9 %copy-start.6 = (bf16[4,386,512]{2,1,0:T(8,128)(2,1)S(1)}, bf16[4,386,512]{2,1,0:T(8,128)(2,1)}, u32[]{:S(2)}) copy-start(bf16[4,386,512]{2,1,0:T(8,128)(2,1)} %gather_fusion.3) | copy-start | bytes 4743172
  107.0 4.0 %copy-start.38 = (pred[4]{0:T(512)(128)(4,1)S(1)}, pred[4]{0:T(512)(128)(4,1)}, u32[]{:S(2)}) copy-start(pred[4]{0:T(512)(128)(4,1)} %get-tuple-element.109) | copy-start | bytes 16
  107.0 42.8 %collective-permute-start.5 = (bf16[3,512,512]{2,1,0:T(8,128)(2,1)}, bf16[3,512,512]{2,1,0:T(8,128)(2,1)}, u32[]{:S(2)}, u32[]{:S(2)}) collective-permute-start(bf16[3,512,512]{2,1,0:T(8,128)(2,1)} %fusion.5), channel_id=1, source_target_pairs={{0,16},{16,0},{1,17},{17,1},{2,18},{18,2},{3,19},{19,3},{4,20},{20... | collective-permute-start | bytes 4718600 | tf_op jit(solution)/shard_map/ppermute | solution.py:111
  111.2 38.6 %copy-start.7 = (bf16[4,386,512]{2,1,0:T(8,128)(2,1)}, bf16[4,386,512]{2,1,0:T(8,128)(2,1)S(1)}, u32[]{:S(2)}) copy-start(bf16[4,386,512]{2,1,0:T(8,128)(2,1)S(1)} %broadcast_select_fusion.1) | copy-start | bytes 4743172
  153.0 4.8 %copy-start.10 = (f32[32,64,128]{2,1,0:T(8,128)S(1)}, f32[32,64,128]{2,1,0:T(8,128)}, u32[]{:S(2)}) copy-start(f32[32,64,128]{2,1,0:T(8,128)} %multiply_exponential_fusion) | copy-start | bytes 3145732
  156.3 36.3 %collective-permute-start.4 = (bf16[3,512,512]{2,1,0:T(8,128)(2,1)}, bf16[3,512,512]{2,1,0:T(8,128)(2,1)}, u32[]{:S(2)}, u32[]{:S(2)}) collective-permute-start(bf16[3,512,512]{2,1,0:T(8,128)(2,1)} %fusion.6), channel_id=1, source_target_pairs={{0,16},{16,0},{1,17},{17,1},{2,18},{18,2},{3,19},{19,3},{4,20},{20... | collective-permute-start | bytes 4718600 | tf_op jit(solution)/shard_map/ppermute | solution.py:111
  162.3 10.3 %copy-start.8 = (bf16[4,386,512]{2,1,0:T(8,128)(2,1)S(1)}, bf16[4,386,512]{2,1,0:T(8,128)(2,1)}, u32[]{:S(2)}) copy-start(bf16[4,386,512]{2,1,0:T(8,128)(2,1)} %copy-done.7) | copy-start | bytes 4743172
  162.3 10.3 %copy-start.15 = (bf16[1024,1,512]{2,0,1:T(8,128)(2,1)S(1)}, bf16[1024,1,512]{2,0,1:T(8,128)(2,1)}, u32[]{:S(2)}) copy-start(bf16[1024,1,512]{2,0,1:T(8,128)(2,1)} %get-tuple-element.115) | copy-start | bytes 3145732
  162.3 11.6 %collective-permute-start.6 = (f32[32,64,16]{1,2,0:T(8,128)S(1)}, f32[32,64,16]{1,2,0:T(8,128)S(1)}, u32[]{:S(2)}, u32[]{:S(2)}) collective-permute-start(f32[32,64,16]{1,2,0:T(8,128)S(1)} %get-tuple-element.51), channel_id=1, source_target_pairs={{0,4},{4,8},{8,12},{1,5},{5,9},{9,13},{2,6},{6,10},{10,14},{3,7},{... | collective-permute-start | bytes 393224 | tf_op jit(solution)/shard_map/ppermute | solution.py:174
  164.6 12.2 %collective-permute-start.7 = (f32[32,64,16]{1,2,0:T(8,128)S(1)}, f32[32,64,16]{1,2,0:T(8,128)S(1)}, u32[]{:S(2)}, u32[]{:S(2)}) collective-permute-start(f32[32,64,16]{1,2,0:T(8,128)S(1)} %get-tuple-element.51), channel_id=1, source_target_pairs={{0,8},{4,12},{1,9},{5,13},{2,10},{6,14},{3,11},{7,15},{16,24},{20,... | collective-permute-start | bytes 393224 | tf_op jit(solution)/shard_map/ppermute | solution.py:174
  168.1 12.5 %collective-permute-start.8 = (f32[32,64,16]{1,2,0:T(8,128)S(1)}, f32[32,64,16]{1,2,0:T(8,128)S(1)}, u32[]{:S(2)}, u32[]{:S(2)}) collective-permute-start(f32[32,64,16]{1,2,0:T(8,128)S(1)} %get-tuple-element.51), channel_id=1, source_target_pairs={{0,12},{1,13},{2,14},{3,15},{16,28},{17,29},{18,30},{19,31}} | collective-permute-start | bytes 393224 | tf_op jit(solution)/shard_map/ppermute | solution.py:174
  172.6 8.1 %copy-start.23 = (f32[32,64]{1,0:T(8,128)S(1)}, f32[32,64]{1,0:T(8,128)}, u32[]{:S(2)}) copy-start(f32[32,64]{1,0:T(8,128)} %get-tuple-element.132) | copy-start | bytes 24580
  172.6 8.1 %copy-start.24 = (f32[32,64]{1,0:T(8,128)S(1)}, f32[32,64]{1,0:T(8,128)}, u32[]{:S(2)}) copy-start(f32[32,64]{1,0:T(8,128)} %get-tuple-element.133) | copy-start | bytes 24580
  172.6 8.2 %copy-start.11 = (f32[32,128,64]{1,2,0:T(8,128)S(1)}, f32[32,128,64]{1,2,0:T(8,128)}, u32[]{:S(2)}) copy-start(f32[32,128,64]{1,2,0:T(8,128)} %exponential_multiply_fusion) | copy-start | bytes 3145732
  172.6 8.2 %copy-start.22 = (f32[3,32,64,16]{2,3,1,0:T(8,128)S(1)}, f32[3,32,64,16]{2,3,1,0:T(8,128)}, u32[]{:S(2)}) copy-start(f32[3,32,64,16]{2,3,1,0:T(8,128)} %get-tuple-element.52) | copy-start | bytes 1179652
  196.5 9.9 %collective-permute-start.9 = (bf16[1,384,512]{2,1,0:T(8,128)(2,1)S(1)}, bf16[1,384,512]{2,1,0:T(8,128)(2,1)S(1)}, u32[]{:S(2)}, u32[]{:S(2)}) collective-permute-start(bf16[1,384,512]{2,1,0:T(8,128)(2,1)S(1)} %bitcast.147), channel_id=1, source_target_pairs={{0,2},{1,3},{2,0},{3,1},{4,6},{5,7},{6,4},{7,5},{8,10},{9,11},{10,... | collective-permute-start | bytes 1179656 | tf_op jit(solution)/shard_map/ppermute | solution.py:198
  206.5 3.9 %collective-permute-start.10 = (bf16[2,384,512]{2,1,0:T(8,128)(2,1)S(1)}, bf16[2,384,512]{2,1,0:T(8,128)(2,1)S(1)}, u32[]{:S(2)}, u32[]{:S(2)}) collective-permute-start(bf16[2,384,512]{2,1,0:T(8,128)(2,1)S(1)} %pad_maximum_fusion.2), channel_id=1, source_target_pairs={{0,1},{1,0},{2,3},{3,2},{4,5},{5,4},{6,7},{7,6},{8,9},{9,8},{10,11... | collective-permute-start | bytes 2359304 | tf_op jit(solution)/shard_map/ppermute | solution.py:198
  206.6 3.8 %copy-start.9 = (bf16[2048,1024]{1,0:T(8,128)(2,1)S(1)}, bf16[2048,1024]{1,0:T(8,128)(2,1)}, u32[]{:S(2)}) copy-start(bf16[2048,1024]{1,0:T(8,128)(2,1)} %param.18) | copy-start | bytes 12582916
  (22 other events, 43.1 us)
Sparse Core Ops, SparseCore 0:
  9.3 48.3 all-gather.6
  59.3 44.4 all-gather.10
  105.3 44.4 all-gather.8

commit v4 on v3

--- a/solution.py
+++ b/solution.py
@@ -111,19 +111,34 @@
             received.append(lax.ppermute(send, "grp", pairs))
         return received
 
-    order = [0, 2, 1] if streams == 3 else list(range(streams))
+    stream_order = [0, 2, 1] if streams == 3 else list(range(streams))
+    width = streams * local_width
+    own_cat = jnp.concatenate([own[:, s, :] for s in stream_order], axis=1)
+    w_cat = jnp.concatenate([w_in[:, s, :] for s in stream_order], axis=1)
+    taps_cat = jnp.concatenate([short_taps[:, s, :] for s in stream_order], axis=1)
+    if streams == 3:
+        cuts = [0, 5 * width // 12, 10 * width // 12, width]
+    else:
+        cuts = [s * local_width for s in range(streams + 1)]
+    order = [(cuts[c], cuts[c + 1]) for c in range(len(cuts) - 1)]
     relayed = {}
-    for s in order:
-        got = lax.all_gather(own[:, s, :], "ctx", axis=0)
-        if s == order[0]:
+    previous = None
+    for index, chunk in enumerate(order):
+        lo, hi = chunk
+        operand = own_cat[:, lo:hi]
+        if index >= 2:
+            operand, _ = lax.optimization_barrier((operand, previous))
+        got = lax.all_gather(operand, "ctx", axis=0)
+        previous = got
+        if index == 0:
             got, kernel, tail, entry = lax.optimization_barrier((got, kernel, tail, entry))
-        if s == order[-1] and len(order) > 1:
-            relayed[s] = (got, None)
+        if chunk == order[-1] and len(order) > 1:
+            relayed[chunk] = (got, None)
             continue
         send = relay_send(got)
-        if s == order[0]:
+        if index == 0:
             send, gathered = lax.optimization_barrier((send, gathered))
-        relayed[s] = (got, relay(send))
+        relayed[chunk] = (got, relay(send))
 
     ext_rows = tok_rows + halo
     values = gathered[:ext_rows].astype(jnp.float32)
@@ -138,25 +153,27 @@
         src_grp = (me_grp - by) % n_grp
         rolled = ((shard_ids + me_ctx) % n_ctx) * n_grp + src_grp
         others.append((src_grp, jnp.take(blocks, rolled, axis=0)))
-    def project(s, received):
-        got = relayed[s][0]
+    def project(chunk, received):
+        lo, hi = chunk
+        got = relayed[chunk][0]
         acc = jnp.einsum("ktr,krc->tc", mine, got, preferred_element_type=jnp.float32)
         for (src_grp, part), recv in zip(others, received):
-            local = lax.dynamic_slice_in_dim(w_in[:, s, :], src_grp * piece, piece, axis=0)
+            local = lax.dynamic_slice_in_dim(w_cat[:, lo:hi], src_grp * piece, piece, axis=0)
             acc = acc + jnp.dot(part[0], local, preferred_element_type=jnp.float32)
             acc = acc + jnp.einsum(
                 "ktr,krc->tc", part[1:], recv, preferred_element_type=jnp.float32
             )
         rounded = lax.reduce_precision(acc, exponent_bits=8, mantissa_bits=7)
-        return short_filter(rounded, short_taps[:, s, :], tok_rows)
+        return short_filter(rounded, taps_cat[:, lo:hi], tok_rows)
 
     last = order[-1]
-    filtered = {s: project(s, relayed[s][1]) for s in order[:-1]}
+    filtered = {chunk: project(chunk, relayed[chunk][1]) for chunk in order[:-1]}
     first = order[0]
     if relayed[last][1] is None:
         filtered[first], tied = lax.optimization_barrier((filtered[first], relayed[last][0]))
         relayed[last] = (tied, relay(relay_send(tied)))
-    product = filtered[0] * filtered[2]
+    early = jnp.concatenate([filtered[c] for c in order[:-1]], axis=1)
+    product = early[:, :local_width] * early[:, local_width : 2 * local_width]
     blocks = tok_rows // block_rows
     current = product.reshape(blocks, block_rows, local_groups, group_size)
     near = jnp.einsum("gij,bjgc->bigc", kernel, current, precision=highest)
@@ -179,7 +196,8 @@
     distant = jnp.einsum("gin,bgnc->bigc", entry, starts, precision=highest)
     conv_out = (near + distant).reshape(tok_rows, local_width)
     late, conv_out = lax.optimization_barrier((relayed[last][1], conv_out))
-    second = project(last, late)
+    late_part = project(last, late)
+    second = jnp.concatenate([early[:, 2 * local_width :], late_part], axis=1)
     gated = (second * conv_out).astype(jnp.bfloat16)
     count = lax.axis_size("tp")
     me_tp = lax.axis_index("tp")

time: 220 us -> 245 us (1.11)
  waiting for transfers between devices: 99.2 us -> 108 us
  other arithmetic: 27.3 us -> 32.9 us
  matrix products: 33.6 us -> 38.8 us
  local copies, waits for them, and re-layouts: 24.9 us -> 28.5 us
    ppermute x3, waiting for transfers between devices: 6.3 us -> 24.9 us  [relay(): received.append(lax.ppermute(send, 'grp', pairs))]
    all_gather x3, waiting for transfers between devices: 62.1 us -> 56.1 us  [body(): got = lax.all_gather(operand, 'ctx', axis=0)]
    squeeze x0 -> x3, local copies, waits for them, and re-layouts: none -> 3.15 us  [the longest x1 1.69 us: body(): w_cat = jnp.concatenate([w_in[:, s, :] for s in stream_order], axis=1)]
    add x3, other arithmetic: 0.34 us -> 3.24 us  [advance(): return (step_decay * state + end_block, state)]
    slice x2 -> x5, local copies, waits for them, and re-layouts: 4.38 us -> 1.58 us  [the longest x1 0.84 us: project(): w_cat[:, lo:hi]]
    unnamed x82 -> x85, local copies, waits for them, and re-layouts: 6.89 us -> 7.87 us
  transfers between devices with their start and end apart: 14 -> 14, of which waited for: 8 -> 9; matrix products, arithmetic and copies ran while one was open for 30% -> 29% of each run, Pallas kernels for 0% -> 0%
where the time goes in v4:
time: 245 us; the launch traced here: 243 us
  waiting for transfers between devices  108 us (44%)
  matrix products  38.8 us (16%)
  other arithmetic  32.9 us (13%)
  local copies, waits for them, and re-layouts  28.5 us (12%)
  starting transfers between devices  21.2 us (9%)
  between operations  13.9 us (6%)
    all_gather x3, waiting for transfers between devices, body(): got = lax.all_gather(operand, 'ctx', axis=0)  56.1 us
    ppermute x3, waiting for transfers between devices, relay(): received.append(lax.ppermute(send, 'grp', pairs))  24.9 us
    ppermute x2, waiting for transfers between devices, gather_by_swaps(): held = jnp.concatenate([held, lax.ppermute(held, axis, pairs)], axis=0)  14.5 us
    dot_general x3, matrix products, project(): jnp.einsum('ktr,krc->tc', mine, got, preferred_element_type=jnp.float32)  8.65 us
    unnamed x85, local copies, waits for them, and re-layouts  7.87 us
    concatenate x3, other arithmetic, relay_send(): doubled = jnp.concatenate([got, got], axis=0)  7.59 us
    dot_general x3, matrix products, project(): jnp.einsum('ktr,krc->tc', part[1:], recv, preferred_element_type=jnp.floa...  7.33 us
    ppermute x2, waiting for transfers between devices, body(): arrived = lax.ppermute(held, 'tp', pairs)  7.09 us
  transfers between devices with their start and end apart: 14, of which 9 were waited for; matrix products, arithmetic and copies ran while one was open for 29% of the time, Pallas kernels for 0%

profile of v4, /device:TPU:0, one launch (start us, length us, event | category | flops | bytes accessed | tf_op | source)
XLA Modules:
  0.0 243.0 jit_solution(1604326131541683936)
XLA Ops:
  10.2 3.0 %collective-permute-start = (bf16[1,385,1024]{2,1,0:T(8,128)(2,1)S(1)}, bf16[1,385,1024]{2,1,0:T(8,128)(2,1)S(1)}, u32[]{:S(2)}, u32[]{:S(2)}) collective-permute-start(bf16[1,385,1024]{2,1,0:T(8,128)(2,1)S(1)} %maximum_bitcast_fusion), channel_id=1, source_target_pairs={{0,2},{1,3},{2,0},{3,1},{4,6},{5,7},{6,4},{7,5},{8,10},{9,11},{10,... | collective-permute-start | bytes 2365448 | tf_op jit(solution)/shard_map/ppermute | solution.py:57
  16.6 14.5 %collective-permute-done = bf16[1,385,1024]{2,1,0:T(8,128)(2,1)S(1)} collective-permute-done((bf16[1,385,1024]{2,1,0:T(8,128)(2,1)S(1)}, bf16[1,385,1024]{2,1,0:T(8,128)(2,1)S(1)}, u32[]{:S(2)}, u32[]{:S(2)}) %collective-permute-start) | collective-permute-done | bytes 788512 | tf_op jit(solution)/shard_map/ppermute | solution.py:57
  36.7 5.5 %convolution_select_fusion = f32[32,128,128]{2,1,0:T(8,128)} fusion(pred[128,128]{1,0:T(8,128)(4,1)S(1)} %broadcast_compare_fusion, f32[32,64]{1,0:T(8,128)S(1)} %copy-done.34, f32[128]{0:T(128)S(1)} %iota_convert_fusion.1, f32[32,64]{1,0:T(8,128)S(1)} %get-tuple-element.143, f32[32,64]{1,0:T(8,128)S(1)} %get-tuple-element.142), kind=kOutput, calls=%fused_computation.25 | convolution fusion | flops 403963904 | bytes 2138624 | tf_op jit(solution)/shard_map/gin,gjn->gij/dot_general | solution.py:91
  44.3 2.0 pad_maximum_fusion
  46.3 2.7 %gather_fusion.1 = bf16[4,385,1024]{2,1,0:T(8,128)(2,1)S(1)} fusion(bf16[4,385,1024]{2,1,0:T(8,128)(2,1)} %pad_maximum_fusion, s32[1024]{0:T(1024)S(1)} %pad_clamp_fusion.2), kind=kCustom, calls=%fused_computation.3 | custom fusion | bytes 6307856 | tf_op jit(solution)/shard_map/jit(_take)/gather | solution.py:62
  50.9 4.4 %collective-permute-start.2 = (bf16[2,4096]{1,0:T(2,128)(2,1)S(1)}, bf16[2,4096]{1,0:T(2,128)(2,1)}, u32[]{:S(2)}, u32[]{:S(2)}) collective-permute-start(bf16[2,4096]{1,0:T(2,128)(2,1)S(1)} %pad_maximum_fusion.6), channel_id=1, source_target_pairs={{0,4},{4,8},{8,12},{1,5},{5,9},{9,13},{2,6},{6,10},{10,14},{3,7},{... | collective-permute-start | bytes 49160 | tf_op jit(solution)/shard_map/ppermute | solution.py:12
  58.1 3.5 %maximum_maximum_fusion = bf16[387,4096]{1,0:T(8,128)(2,1)S(1)} fusion(bf16[385,1024]{1,0:T(8,128)(2,1)} %copy-done.3, bf16[385,1024]{1,0:T(8,128)(2,1)} %copy-done.4, bf16[385,1024]{1,0:T(8,128)(2,1)} %copy-done.5, bf16[385,1024]{1,0:T(8,128)(2,1)} %copy-done.2, bf16[2,4096]{1,0:T(2,128)(2,1)} %collective-permute-done.2), kind=kLoop, calls=%fused_computation.16 | loop fusion | flops 15851520 | bytes 6340608 | tf_op jit(solution)/shard_map/concatenate | solution.py:100
  61.6 6.1 %all-gather.7.cloned.1.call-done = bf16[2048,640]{1,0:T(8,128)(2,1)} async-done(((bf16[512,640]{1,0:T(8,128)(2,1)}), bf16[2048,640]{1,0:T(8,128)(2,1)}) %all-gather.7.cloned.1.call-update) | async-done | bytes 2621456 | tf_op jit(solution)/shard_map/all_gather | solution.py:131
  67.7 3.6 %fusion.6 = bf16[3,512,640]{2,1,0:T(8,128)(2,1)} fusion(s32[]{:T(128)S(6)} %select_n.106, bf16[4,512,640]{2,1,0:T(8,128)(2,1)} %bitcast.154), kind=kLoop, calls=%fused_computation.24 | loop fusion | flops 983040 | bytes 4587524 | tf_op jit(solution)/shard_map/concatenate | solution.py:104
  77.4 45.6 %all-gather.9.cloned.1.call-done = bf16[2048,640]{1,0:T(8,128)(2,1)} async-done(((bf16[512,640]{1,0:T(8,128)(2,1)}), bf16[2048,640]{1,0:T(8,128)(2,1)}) %all-gather.9.cloned.1.call-update) | async-done | bytes 2621456 | tf_op jit(solution)/shard_map/all_gather | solution.py:131
  123.0 3.7 %fusion.5 = bf16[3,512,640]{2,1,0:T(8,128)(2,1)} fusion(s32[]{:T(128)S(6)} %select_n.106, bf16[4,512,640]{2,1,0:T(8,128)(2,1)} %bitcast.156), kind=kLoop, calls=%fused_computation.23 | loop fusion | flops 983040 | bytes 4587524 | tf_op jit(solution)/shard_map/concatenate | solution.py:104
  128.2 2.0 gather_fusion.2
  130.2 4.8 %convolution_bitcast_fusion.1 = f32[386,640]{1,0:T(8,128)} fusion(bf16[4,512,640]{2,1,0:T(8,128)(2,1)} %bitcast.157, bf16[4,386,512]{2,1,0:T(8,128)(2,1)} %gather_fusion.2, pred[4]{0:T(512)(128)(4,1)} %compare_and_fusion.1), kind=kOutput, calls=%fused_computation.33 | convolution fusion | flops 1012666368 | bytes 5190660 | tf_op jit(solution)/shard_map/ktr,krc->tc/dot_general | solution.py:159
  135.0 1.9 gather_fusion.3
  137.0 1.8 broadcast_select_fusion.1
  143.9 2.7 %fusion.16 = f32[386,640]{1,0:T(8,128)S(1)} fusion(f32[386,640]{1,0:T(8,128)S(1)} %convolution_add_fusion, bf16[4,386,512]{2,1,0:T(8,128)(2,1)S(1)} %broadcast_select_fusion.1, bf16[3,512,640]{2,1,0:T(8,128)(2,1)} %collective-permute-done.4), kind=kOutput, calls=%fused_computation.46 | convolution fusion | flops 759400960 | bytes 5523456 | tf_op jit(solution)/shard_map/ktr,krc->tc/dot_general | solution.py:163
  146.9 4.4 %all-gather.11.cloned.1.call-done = bf16[2048,256]{1,0:T(8,128)(2,1)} async-done(((bf16[512,256]{1,0:T(8,128)(2,1)}), bf16[2048,256]{1,0:T(8,128)(2,1)}) %all-gather.11.cloned.1.call-update) | async-done | bytes 1048592 | tf_op jit(solution)/shard_map/all_gather | solution.py:131
  151.4 20.0 %collective-permute-done.3 = bf16[3,512,640]{2,1,0:T(8,128)(2,1)} collective-permute-done((bf16[3,512,640]{2,1,0:T(8,128)(2,1)}, bf16[3,512,640]{2,1,0:T(8,128)(2,1)}, u32[]{:S(2)}, u32[]{:S(2)}) %collective-permute-start.3) | collective-permute-done | bytes 1966112 | tf_op jit(solution)/shard_map/ppermute | solution.py:111
  171.4 2.9 %fusion.14 = f32[386,640]{1,0:T(8,128)S(1)} fusion(f32[386,640]{1,0:T(8,128)} %convolution_add_fusion.1, bf16[4,386,512]{2,1,0:T(8,128)(2,1)S(1)} %broadcast_select_fusion.1, bf16[3,512,640]{2,1,0:T(8,128)(2,1)} %collective-permute-done.3), kind=kOutput, calls=%fused_computation.44 | convolution fusion | flops 759400960 | bytes 5523456 | tf_op jit(solution)/shard_map/ktr,krc->tc/dot_general | solution.py:163
  176.8 2.3 copy.53
  180.5 3.9 %convolution_bitcast_fusion.4 = f32[3,32,64,16]{2,3,0,1:T(8,128)} fusion(f32[32,64,128]{2,1,0:T(8,128)} %multiply_exponential_fusion, f32[3,128,32,16]{1,0,3,2:T(4,128)S(1)} %reshape.153), kind=kOutput, calls=%fused_computation.42 | convolution fusion | flops 150994944 | bytes 2228224 | tf_op jit(solution)/shard_map/gni,bigc->bgnc/dot_general | solution.py:180
  184.4 5.5 %while.13 = (s32[]{:T(128)}, f32[32,64,16]{1,2,0:T(8,128)S(1)}, f32[3,32,64,16]{2,3,1,0:T(8,128)}, f32[32,64,1]{1,0,2:T(8,128)S(1)}, f32[3,32,64,16]{2,3,0,1:T(8,128)}, /*index=5*/s32[]{:T(128)}, s32[]{:T(128)}) while((s32[]{:T(128)}, f32[32,64,16]{1,2,0:T(8,128)S(1)}, f32[3,32,64,16]{2,3,1,0:T(8,128)}, ...), condition=%wide.region_2.4_spmd.clone, body=%wide.region_1.3_spmd.clone.sunk | while | flops 131075 | bytes 795228 | solution.py:187
  191.3 4.3 %collective-permute-start.7 = (f32[32,64,16]{1,2,0:T(8,128)S(1)}, f32[32,64,16]{1,2,0:T(8,128)S(1)}, u32[]{:S(2)}, u32[]{:S(2)}) collective-permute-start(f32[32,64,16]{1,2,0:T(8,128)S(1)} %get-tuple-element.53), channel_id=1, source_target_pairs={{0,8},{4,12},{1,9},{5,13},{2,10},{6,14},{3,11},{7,15},{16,24},{20,... | collective-permute-start | bytes 393224 | tf_op jit(solution)/shard_map/ppermute | solution.py:191
  196.9 2.3 convolution_bitcast_fusion.6
  199.6 1.7 collective-permute-start.5
  203.3 4.1 %collective-permute-done.8 = f32[32,64,16]{1,2,0:T(8,128)S(1)} collective-permute-done((f32[32,64,16]{1,2,0:T(8,128)S(1)}, f32[32,64,16]{1,2,0:T(8,128)S(1)}, u32[]{:S(2)}, u32[]{:S(2)}) %collective-permute-start.8) | collective-permute-done | bytes 131104 | tf_op jit(solution)/shard_map/ppermute | solution.py:191
  209.0 3.4 %fusion.10 = f32[3,128,32,16]{1,3,0,2:T(8,128)S(1)} fusion(f32[32,3,16,128]{3,2,1,0:T(8,128)S(1)} %fusion.19, f32[32,128,128]{2,1,0:T(8,128)S(1)} %copy-done.18, f32[3,128,32,16]{1,0,3,2:T(4,128)S(1)} %reshape.153), kind=kOutput, calls=%fused_computation.41 | convolution fusion | flops 302186496 | bytes 4456448 | tf_op jit(solution)/shard_map/gij,bjgc->bigc/dot_general | solution.py:179
  212.9 4.9 %collective-permute-done.5 = bf16[3,512,256]{2,1,0:T(8,128)(2,1)S(1)} collective-permute-done((bf16[3,512,256]{2,1,0:T(8,128)(2,1)S(1)}, bf16[3,512,256]{2,1,0:T(8,128)(2,1)S(1)}, u32[]{:S(2)}, u32[]{:S(2)}) %collective-permute-start.5) | collective-permute-done | bytes 786464 | tf_op jit(solution)/shard_map/ppermute | solution.py:111
  218.9 1.8 fusion.18
  222.7 7.1 %collective-permute-done.9 = bf16[1,384,512]{2,1,0:T(8,128)(2,1)S(1)} collective-permute-done((bf16[1,384,512]{2,1,0:T(8,128)(2,1)S(1)}, bf16[1,384,512]{2,1,0:T(8,128)(2,1)S(1)}, u32[]{:S(2)}, u32[]{:S(2)}) %collective-permute-start.9) | collective-permute-done | bytes 393248 | tf_op jit(solution)/shard_map/ppermute | solution.py:216
  230.0 1.9 fusion.30
  232.0 1.8 fusion.28
  (175 shorter events, 54.4 us)
Async XLA Ops:
  6.5 61.2 %all-gather.7.cloned.1.call-start = ((), (), s32[]{:S(2)}) async-start(), calls=%async_computation | async-start | bytes 3276800 | tf_op jit(solution)/shard_map/all_gather | solution.py:131
  10.0 3.3 %copy-start = (s32[4]{0:T(128)S(1)}, s32[4]{0:T(128)}, u32[]{:S(2)}) copy-start(s32[4]{0:T(128)} %constant.127.clone) | copy-start | bytes 52
  10.0 5.2 %copy-start.35 = (f32[3,3,512]{2,1,0:T(4,128)S(1)}, f32[3,3,512]{2,1,0:T(4,128)}, u32[]{:S(2)}) copy-start(f32[3,3,512]{2,1,0:T(4,128)} %param.15) | copy-start | bytes 55300
  10.1 112.9 %all-gather.9.cloned.1.call-start = ((), (), s32[]{:S(2)}) async-start(), calls=%async_computation.1 | async-start | bytes 3276800 | tf_op jit(solution)/shard_map/all_gather | solution.py:131
  10.2 20.9 %collective-permute-start = (bf16[1,385,1024]{2,1,0:T(8,128)(2,1)S(1)}, bf16[1,385,1024]{2,1,0:T(8,128)(2,1)S(1)}, u32[]{:S(2)}, u32[]{:S(2)}) collective-permute-start(bf16[1,385,1024]{2,1,0:T(8,128)(2,1)S(1)} %maximum_bitcast_fusion), channel_id=1, source_target_pairs={{0,2},{1,3},{2,0},{3,1},{4,6},{5,7},{6,4},{7,5},{8,10},{9,11},{10,... | collective-permute-start | bytes 2365448 | tf_op jit(solution)/shard_map/ppermute | solution.py:57
  13.3 138.1 %all-gather.11.cloned.1.call-start = ((), (), s32[]{:S(2)}) async-start(), calls=%async_computation.2 | async-start | bytes 1310720 | tf_op jit(solution)/shard_map/all_gather | solution.py:131
  32.9 10.9 %collective-permute-start.1 = (bf16[2,385,1024]{2,0,1:T(2,128)(2,1)S(1)}, bf16[2,385,1024]{2,0,1:T(2,128)(2,1)S(1)}, u32[]{:S(2)}, u32[]{:S(2)}) collective-permute-start(bf16[2,385,1024]{2,0,1:T(2,128)(2,1)S(1)} %copy.49), channel_id=1, source_target_pairs={{0,1},{1,0},{2,3},{3,2},{4,5},{5,4},{6,7},{7,6},{8,9},{9,8},{10,11... | collective-permute-start | bytes 4730888 | tf_op jit(solution)/shard_map/ppermute | solution.py:57
  35.1 7.1 %copy-start.6 = (bf16[1024,3,512]{2,0,1:T(8,128)(2,1)S(1)}, bf16[1024,3,512]{2,0,1:T(8,128)(2,1)}, u32[]{:S(2)}) copy-start(bf16[1024,3,512]{2,0,1:T(8,128)(2,1)} %param.14) | copy-start | bytes 9437188
  49.7 5.6 %copy-start.4 = (bf16[385,1024]{1,0:T(8,128)(2,1)}, bf16[385,1024]{1,0:T(8,128)(2,1)S(1)}, u32[]{:S(2)}) copy-start(bf16[385,1024]{1,0:T(8,128)(2,1)S(1)} %get-tuple-element.124) | copy-start | bytes 2365444
  49.7 5.6 %copy-start.5 = (bf16[385,1024]{1,0:T(8,128)(2,1)}, bf16[385,1024]{1,0:T(8,128)(2,1)S(1)}, u32[]{:S(2)}) copy-start(bf16[385,1024]{1,0:T(8,128)(2,1)S(1)} %get-tuple-element.125) | copy-start | bytes 2365444
  49.7 6.1 %copy-start.14 = (bf16[512,512]{1,0:T(8,128)(2,1)S(1)}, bf16[512,512]{1,0:T(8,128)(2,1)}, u32[]{:S(2)}) copy-start(bf16[512,512]{1,0:T(8,128)(2,1)} %copy-done.13) | copy-start | bytes 1572868
  49.8 6.9 %copy-start.7 = (bf16[1024,512]{1,0:T(8,128)(2,1)S(1)}, bf16[1024,512]{1,0:T(8,128)(2,1)}, u32[]{:S(2)}) copy-start(bf16[1024,512]{1,0:T(8,128)(2,1)} %get-tuple-element.126) | copy-start | bytes 3145732
  50.9 7.2 %collective-permute-start.2 = (bf16[2,4096]{1,0:T(2,128)(2,1)S(1)}, bf16[2,4096]{1,0:T(2,128)(2,1)}, u32[]{:S(2)}, u32[]{:S(2)}) collective-permute-start(bf16[2,4096]{1,0:T(2,128)(2,1)S(1)} %pad_maximum_fusion.6), channel_id=1, source_target_pairs={{0,4},{4,8},{8,12},{1,5},{5,9},{9,13},{2,6},{6,10},{10,14},{3,7},{... | collective-permute-start | bytes 49160 | tf_op jit(solution)/shard_map/ppermute | solution.py:12
  71.3 72.6 %collective-permute-start.4 = (bf16[3,512,640]{2,1,0:T(8,128)(2,1)}, bf16[3,512,640]{2,1,0:T(8,128)(2,1)}, u32[]{:S(2)}, u32[]{:S(2)}) collective-permute-start(bf16[3,512,640]{2,1,0:T(8,128)(2,1)} %fusion.6), channel_id=1, source_target_pairs={{0,16},{16,0},{1,17},{17,1},{2,18},{18,2},{3,19},{19,3},{4,20},{20... | collective-permute-start | bytes 5898248 | tf_op jit(solution)/shard_map/ppermute | solution.py:111
  126.7 44.7 %collective-permute-start.3 = (bf16[3,512,640]{2,1,0:T(8,128)(2,1)}, bf16[3,512,640]{2,1,0:T(8,128)(2,1)}, u32[]{:S(2)}, u32[]{:S(2)}) collective-permute-start(bf16[3,512,640]{2,1,0:T(8,128)(2,1)} %fusion.5), channel_id=1, source_target_pairs={{0,16},{16,0},{1,17},{17,1},{2,18},{18,2},{3,19},{19,3},{4,20},{20... | collective-permute-start | bytes 5898248 | tf_op jit(solution)/shard_map/ppermute | solution.py:111
  143.9 2.7 %copy-start.30 = (f32[640]{0:T(1024)S(1)}, f32[640]{0:T(1024)}, u32[]{:S(2)}) copy-start(f32[640]{0:T(1024)} %get-tuple-element.107) | copy-start | bytes 7684
  143.9 2.7 %copy-start.31 = (f32[640]{0:T(1024)S(1)}, f32[640]{0:T(1024)}, u32[]{:S(2)}) copy-start(f32[640]{0:T(1024)} %get-tuple-element.108) | copy-start | bytes 7684
  151.4 22.9 %copy-start.27 = (f32[640]{0:T(1024)S(1)}, f32[640]{0:T(1024)}, u32[]{:S(2)}) copy-start(f32[640]{0:T(1024)} %get-tuple-element.101) | copy-start | bytes 7684
  151.4 22.9 %copy-start.28 = (f32[640]{0:T(1024)S(1)}, f32[640]{0:T(1024)}, u32[]{:S(2)}) copy-start(f32[640]{0:T(1024)} %get-tuple-element.102) | copy-start | bytes 7684
  151.4 23.0 %copy-start.29 = (f32[640]{0:T(1024)S(1)}, f32[640]{0:T(1024)}, u32[]{:S(2)}) copy-start(f32[640]{0:T(1024)} %get-tuple-element.103) | copy-start | bytes 7684
  189.9 9.4 %copy-start.21 = (bf16[2048,256]{1,0:T(8,128)(2,1)S(1)}, bf16[2048,256]{1,0:T(8,128)(2,1)}, u32[]{:S(2)}) copy-start(bf16[2048,256]{1,0:T(8,128)(2,1)} %all-gather.11.cloned.1.call-done) | copy-start | bytes 3145732
  189.9 12.5 %collective-permute-start.6 = (f32[32,64,16]{1,2,0:T(8,128)S(1)}, f32[32,64,16]{1,2,0:T(8,128)S(1)}, u32[]{:S(2)}, u32[]{:S(2)}) collective-permute-start(f32[32,64,16]{1,2,0:T(8,128)S(1)} %get-tuple-element.53), channel_id=1, source_target_pairs={{0,4},{4,8},{8,12},{1,5},{5,9},{9,13},{2,6},{6,10},{10,14},{3,7},{... | collective-permute-start | bytes 393224 | tf_op jit(solution)/shard_map/ppermute | solution.py:191
  191.3 12.0 %collective-permute-start.7 = (f32[32,64,16]{1,2,0:T(8,128)S(1)}, f32[32,64,16]{1,2,0:T(8,128)S(1)}, u32[]{:S(2)}, u32[]{:S(2)}) collective-permute-start(f32[32,64,16]{1,2,0:T(8,128)S(1)} %get-tuple-element.53), channel_id=1, source_target_pairs={{0,8},{4,12},{1,9},{5,13},{2,10},{6,14},{3,11},{7,15},{16,24},{20,... | collective-permute-start | bytes 393224 | tf_op jit(solution)/shard_map/ppermute | solution.py:191
  195.6 11.8 %collective-permute-start.8 = (f32[32,64,16]{1,2,0:T(8,128)S(1)}, f32[32,64,16]{1,2,0:T(8,128)S(1)}, u32[]{:S(2)}, u32[]{:S(2)}) collective-permute-start(f32[32,64,16]{1,2,0:T(8,128)S(1)} %get-tuple-element.53), channel_id=1, source_target_pairs={{0,12},{1,13},{2,14},{3,15},{16,28},{17,29},{18,30},{19,31}} | collective-permute-start | bytes 393224 | tf_op jit(solution)/shard_map/ppermute | solution.py:191
  199.3 8.1 %copy-start.25 = (f32[32,64]{1,0:T(8,128)S(1)}, f32[32,64]{1,0:T(8,128)}, u32[]{:S(2)}) copy-start(f32[32,64]{1,0:T(8,128)} %get-tuple-element.139) | copy-start | bytes 24580
  199.3 8.1 %copy-start.26 = (f32[32,64]{1,0:T(8,128)S(1)}, f32[32,64]{1,0:T(8,128)}, u32[]{:S(2)}) copy-start(f32[32,64]{1,0:T(8,128)} %get-tuple-element.140) | copy-start | bytes 24580
  199.6 7.9 %copy-start.12 = (f32[32,128,64]{1,2,0:T(8,128)S(1)}, f32[32,128,64]{1,2,0:T(8,128)}, u32[]{:S(2)}) copy-start(f32[32,128,64]{1,2,0:T(8,128)} %exponential_multiply_fusion) | copy-start | bytes 3145732
  199.6 7.9 %copy-start.23 = (f32[3,32,64,16]{2,3,1,0:T(8,128)S(1)}, f32[3,32,64,16]{2,3,1,0:T(8,128)}, u32[]{:S(2)}) copy-start(f32[3,32,64,16]{2,3,1,0:T(8,128)} %get-tuple-element.54) | copy-start | bytes 1179652
  199.6 18.1 %collective-permute-start.5 = (bf16[3,512,256]{2,1,0:T(8,128)(2,1)S(1)}, bf16[3,512,256]{2,1,0:T(8,128)(2,1)S(1)}, u32[]{:S(2)}, u32[]{:S(2)}) collective-permute-start(bf16[3,512,256]{2,1,0:T(8,128)(2,1)S(1)} %fusion.41), channel_id=1, source_target_pairs={{0,16},{16,0},{1,17},{17,1},{2,18},{18,2},{3,19},{19,3},{4,20},{20... | collective-permute-start | bytes 2359304 | tf_op jit(solution)/shard_map/ppermute | solution.py:111
  221.0 8.8 %collective-permute-start.9 = (bf16[1,384,512]{2,1,0:T(8,128)(2,1)S(1)}, bf16[1,384,512]{2,1,0:T(8,128)(2,1)S(1)}, u32[]{:S(2)}, u32[]{:S(2)}) collective-permute-start(bf16[1,384,512]{2,1,0:T(8,128)(2,1)S(1)} %bitcast.151), channel_id=1, source_target_pairs={{0,2},{1,3},{2,0},{3,1},{4,6},{5,7},{6,4},{7,5},{8,10},{9,11},{10,... | collective-permute-start | bytes 1179656 | tf_op jit(solution)/shard_map/ppermute | solution.py:216
  229.9 3.9 %collective-permute-start.10 = (bf16[2,384,512]{2,1,0:T(8,128)(2,1)S(1)}, bf16[2,384,512]{2,1,0:T(8,128)(2,1)S(1)}, u32[]{:S(2)}, u32[]{:S(2)}) collective-permute-start(bf16[2,384,512]{2,1,0:T(8,128)(2,1)S(1)} %pad_maximum_fusion.3), channel_id=1, source_target_pairs={{0,1},{1,0},{2,3},{3,2},{4,5},{5,4},{6,7},{7,6},{8,9},{9,8},{10,11... | collective-permute-start | bytes 2359304 | tf_op jit(solution)/shard_map/ppermute | solution.py:216
  230.0 3.8 %copy-start.10 = (bf16[2048,1024]{1,0:T(8,128)(2,1)S(1)}, bf16[2048,1024]{1,0:T(8,128)(2,1)}, u32[]{:S(2)}) copy-start(bf16[2048,1024]{1,0:T(8,128)(2,1)} %param.18) | copy-start | bytes 12582916
  (24 other events, 43.1 us)
Sparse Core Ops, SparseCore 0:
  10.2 57.4 all-gather.6
  69.3 53.6 all-gather.8
  124.6 26.7 all-gather.10

commit v5 on v3

--- a/solution.py
+++ b/solution.py
@@ -113,13 +113,16 @@
 
     order = [0, 2, 1] if streams == 3 else list(range(streams))
     relayed = {}
+    previous = None
     for s in order:
+        if s == order[-1] and len(order) > 1:
+            operand, _ = lax.optimization_barrier((w_in[:, s, :], previous))
+            relayed[s] = (lax.all_gather(operand, "ctx", axis=0, tiled=True), None)
+            continue
         got = lax.all_gather(own[:, s, :], "ctx", axis=0)
+        previous = got
         if s == order[0]:
             got, kernel, tail, entry = lax.optimization_barrier((got, kernel, tail, entry))
-        if s == order[-1] and len(order) > 1:
-            relayed[s] = (got, None)
-            continue
         send = relay_send(got)
         if s == order[0]:
             send, gathered = lax.optimization_barrier((send, gathered))
@@ -155,7 +158,7 @@
     first = order[0]
     if relayed[last][1] is None:
         filtered[first], tied = lax.optimization_barrier((filtered[first], relayed[last][0]))
-        relayed[last] = (tied, relay(relay_send(tied)))
+        relayed[last] = (tied, None)
     product = filtered[0] * filtered[2]
     blocks = tok_rows // block_rows
     current = product.reshape(blocks, block_rows, local_groups, group_size)
@@ -178,8 +181,14 @@
     starts = lead * incoming[None] + local_starts
     distant = jnp.einsum("gin,bgnc->bigc", entry, starts, precision=highest)
     conv_out = (near + distant).reshape(tok_rows, local_width)
-    late, conv_out = lax.optimization_barrier((relayed[last][1], conv_out))
-    second = project(last, late)
+    if relayed[last][1] is None:
+        whole_w, conv_out = lax.optimization_barrier((relayed[last][0], conv_out))
+        acc = jnp.dot(normed, whole_w, preferred_element_type=jnp.float32)
+        rounded = lax.reduce_precision(acc, exponent_bits=8, mantissa_bits=7)
+        second = short_filter(rounded, short_taps[:, last, :], tok_rows)
+    else:
+        late, conv_out = lax.optimization_barrier((relayed[last][1], conv_out))
+        second = project(last, late)
     gated = (second * conv_out).astype(jnp.bfloat16)
     count = lax.axis_size("tp")
     me_tp = lax.axis_index("tp")

time: 220 us -> 258 us (1.17)
  the two profiles are of different devices: /device:TPU:0 before, /device:TPU:17 now
where the time goes in v5:
time: 258 us; the launch traced here: 257 us
  waiting for transfers between devices  150 us (58%)
  matrix products  28.8 us (11%)
  local copies, waits for them, and re-layouts  25.7 us (10%)
  other arithmetic  23.5 us (9%)
  starting transfers between devices  15.7 us (6%)
  between operations  13.9 us (5%)
    ppermute x2, waiting for transfers between devices, relay(): received.append(lax.ppermute(send, 'grp', pairs))  57.7 us
    all_gather x2, waiting for transfers between devices, body(): got = lax.all_gather(own[:, s, :], 'ctx', axis=0)  43.7 us
    ppermute x3, waiting for transfers between devices, body(): arrived = lax.ppermute(own_state, 'ctx', pairs)  22.8 us
    ppermute x2, waiting for transfers between devices, gather_by_swaps(): held = jnp.concatenate([held, lax.ppermute(held, axis, pairs)], axis=0)  14.9 us
    ppermute x2, waiting for transfers between devices, body(): arrived = lax.ppermute(held, 'tp', pairs)  9.32 us
    dot_general x4, matrix products, contribution(): return jnp.dot(block, rows, preferred_element_type=jnp.float32)  5.93 us
    ppermute x3, starting transfers between devices, body(): arrived = lax.ppermute(own_state, 'ctx', pairs)  5.89 us
    dot_general x1, matrix products, body(): square = jnp.einsum('gin,gjn->gij', falling, rising, precision=highest)  5.51 us
  transfers between devices with their start and end apart: 13, of which 9 were waited for; matrix products, arithmetic and copies ran while one was open for 19% of the time, Pallas kernels for 0%

profile of v5, /device:TPU:17, one launch (start us, length us, event | category | flops | bytes accessed | tf_op | source)
XLA Modules:
  0.0 257.5 jit_solution(17854723088514794937)
XLA Ops:
  6.5 2.3 constant_dynamic-slice_fusion.1
  13.0 14.9 %collective-permute-done = bf16[1,385,1024]{2,1,0:T(8,128)(2,1)S(1)} collective-permute-done((bf16[1,385,1024]{2,1,0:T(8,128)(2,1)S(1)}, bf16[1,385,1024]{2,1,0:T(8,128)(2,1)S(1)}, u32[]{:S(2)}, u32[]{:S(2)}) %collective-permute-start) | collective-permute-done | bytes 788512 | tf_op jit(solution)/shard_map/ppermute | solution.py:57
  28.1 1.6 copy.39
  33.9 1.6 exponential_multiply_fusion
  35.5 5.5 %convolution_select_fusion = f32[32,128,128]{2,1,0:T(8,128)} fusion(pred[128,128]{1,0:T(8,128)(4,1)S(1)} %broadcast_compare_fusion, f32[32,64]{1,0:T(8,128)S(1)} %copy-done.22, f32[128]{0:T(128)S(1)} %iota_convert_fusion.1, f32[32,64]{1,0:T(8,128)S(1)} %get-tuple-element.137, f32[32,64]{1,0:T(8,128)S(1)} %get-tuple-element.136), kind=kOutput, calls=%fused_computation.21 | convolution fusion | flops 403963904 | bytes 2138624 | tf_op jit(solution)/shard_map/gin,gjn->gij/dot_general | solution.py:91
  41.0 1.8 fusion.69
  43.2 2.0 pad_maximum_fusion
  45.2 2.7 %gather_fusion.1 = bf16[4,385,1024]{2,1,0:T(8,128)(2,1)S(1)} fusion(bf16[4,385,1024]{2,1,0:T(8,128)(2,1)} %pad_maximum_fusion, s32[1024]{0:T(1024)S(1)} %pad_clamp_fusion.2), kind=kCustom, calls=%fused_computation.3 | custom fusion | bytes 6307856 | tf_op jit(solution)/shard_map/jit(_take)/gather | solution.py:62
  48.6 5.8 %all-gather.10.cloned.1.call-done = bf16[2048,1,512]{2,0,1:T(8,128)(2,1)} async-done(((bf16[512,1,512]{2,0,1:T(8,128)(2,1)}), bf16[2048,1,512]{2,0,1:T(8,128)(2,1)}) %all-gather.10.cloned.1.call-update) | async-done | bytes 2097168 | tf_op jit(solution)/shard_map/all_gather | solution.py:122
  54.5 2.7 %collective-permute-start.2 = (bf16[2,4096]{1,0:T(2,128)(2,1)S(1)}, bf16[2,4096]{1,0:T(2,128)(2,1)}, u32[]{:S(2)}, u32[]{:S(2)}) collective-permute-start(bf16[2,4096]{1,0:T(2,128)(2,1)S(1)} %pad_maximum_fusion.3), channel_id=1, source_target_pairs={{0,4},{4,8},{8,12},{1,5},{5,9},{9,13},{2,6},{6,10},{10,14},{3,7},{... | collective-permute-start | bytes 49160 | tf_op jit(solution)/shard_map/ppermute | solution.py:12
  59.1 3.5 %maximum_maximum_fusion = bf16[387,4096]{1,0:T(8,128)(2,1)S(1)} fusion(bf16[385,1024]{1,0:T(8,128)(2,1)} %copy-done.4, bf16[385,1024]{1,0:T(8,128)(2,1)} %copy-done.5, bf16[385,1024]{1,0:T(8,128)(2,1)} %copy-done.6, bf16[385,1024]{1,0:T(8,128)(2,1)} %copy-done.3, bf16[2,4096]{1,0:T(2,128)(2,1)} %collective-permute-done.2), kind=kLoop, calls=%fused_computation.16 | loop fusion | flops 15851520 | bytes 6340608 | tf_op jit(solution)/shard_map/concatenate | solution.py:100
  62.6 37.9 %all-gather.8.cloned.1.call-done = bf16[2048,1,512]{2,0,1:T(8,128)(2,1)} async-done(((bf16[512,1,512]{2,0,1:T(8,128)(2,1)}), bf16[2048,1,512]{2,0,1:T(8,128)(2,1)}) %all-gather.8.cloned.1.call-update) | async-done | bytes 2097168 | tf_op jit(solution)/shard_map/all_gather | solution.py:122
  100.5 3.1 %fusion.6 = bf16[3,512,512]{2,1,0:T(8,128)(2,1)} fusion(s32[]{:T(128)S(6)} %select_n.104, bf16[4,512,512]{2,1,0:T(8,128)(2,1)} %bitcast.140), kind=kLoop, calls=%fused_computation.26 | loop fusion | flops 786432 | bytes 3670020 | tf_op jit(solution)/shard_map/concatenate | solution.py:104
  108.5 1.9 gather_fusion.2
  110.4 1.9 gather_fusion.3
  113.5 1.9 fusion.5
  116.1 2.5 convolution_bitcast_fusion.3
  122.7 25.1 %collective-permute-done.3 = bf16[3,512,512]{2,1,0:T(8,128)(2,1)S(1)} collective-permute-done((bf16[3,512,512]{2,1,0:T(8,128)(2,1)}, bf16[3,512,512]{2,1,0:T(8,128)(2,1)S(1)}, u32[]{:S(2)}, u32[]{:S(2)}) %collective-permute-start.3) | collective-permute-done | bytes 1572896 | tf_op jit(solution)/shard_map/ppermute | solution.py:111
  148.9 32.6 %collective-permute-done.4 = bf16[3,512,512]{2,1,0:T(8,128)(2,1)S(1)} collective-permute-done((bf16[3,512,512]{2,1,0:T(8,128)(2,1)S(1)}, bf16[3,512,512]{2,1,0:T(8,128)(2,1)S(1)}, u32[]{:S(2)}, u32[]{:S(2)}) %collective-permute-start.4) | collective-permute-done | bytes 1572896 | tf_op jit(solution)/shard_map/ppermute | solution.py:111
  185.3 1.7 convolution_bitcast_fusion.4
  187.1 2.6 %while.13 = (s32[]{:T(128)}, f32[32,64,16]{1,2,0:T(8,128)S(1)}, f32[3,32,64,16]{2,3,1,0:T(8,128)}, f32[32,64,1]{1,0,2:T(8,128)S(1)}, f32[3,32,64,16]{2,3,0,1:T(8,128)S(1)}, /*index=5*/s32[]{:T(128)}, s32[]{:T(128)}) while((s32[]{:T(128)}, f32[32,64,16]{1,2,0:T(8,128)S(1)}, f32[3,32,64,16]{2,3,1,0:T(8,128)}, ...), condition=%wide.region_2.4_spmd.clone, body=%wide.region_1.3_spmd.clone.sunk | while | flops 131075 | bytes 794728 | solution.py:173
  191.8 3.8 %collective-permute-start.5 = (f32[32,64,16]{1,2,0:T(8,128)S(1)}, f32[32,64,16]{1,2,0:T(8,128)S(1)}, u32[]{:S(2)}, u32[]{:S(2)}) collective-permute-start(f32[32,64,16]{1,2,0:T(8,128)S(1)} %get-tuple-element.53), channel_id=1, source_target_pairs={{0,4},{4,8},{8,12},{1,5},{5,9},{9,13},{2,6},{6,10},{10,14},{3,7},{... | collective-permute-start | bytes 393224 | tf_op jit(solution)/shard_map/ppermute | solution.py:177
  195.7 9.9 %collective-permute-done.6 = f32[32,64,16]{1,2,0:T(8,128)S(1)} collective-permute-done((f32[32,64,16]{1,2,0:T(8,128)S(1)}, f32[32,64,16]{1,2,0:T(8,128)S(1)}, u32[]{:S(2)}, u32[]{:S(2)}) %collective-permute-start.6) | collective-permute-done | bytes 131104 | tf_op jit(solution)/shard_map/ppermute | solution.py:177
  205.5 12.9 %collective-permute-done.5 = f32[32,64,16]{1,2,0:T(8,128)S(1)} collective-permute-done((f32[32,64,16]{1,2,0:T(8,128)S(1)}, f32[32,64,16]{1,2,0:T(8,128)S(1)}, u32[]{:S(2)}, u32[]{:S(2)}) %collective-permute-start.5) | collective-permute-done | bytes 131104 | tf_op jit(solution)/shard_map/ppermute | solution.py:177
  218.6 2.3 fusion.17
  220.9 3.4 %fusion.10 = f32[3,128,32,16]{1,3,0,2:T(8,128)S(1)} fusion(f32[32,3,16,128]{3,2,1,0:T(8,128)S(1)} %fusion.17, f32[32,128,128]{2,1,0:T(8,128)S(1)} %copy-done.17, f32[3,128,32,16]{1,0,3,2:T(4,128)S(1)} %reshape.173), kind=kOutput, calls=%fused_computation.36 | convolution fusion | flops 302186496 | bytes 4456448 | tf_op jit(solution)/shard_map/gij,bjgc->bigc/dot_general | solution.py:165
  225.6 2.6 %copy.48 = f32[384,512]{1,0:T(8,128)} copy(f32[384,512]{0,1:T(8,128)} %bitcast.137) | data formatting | bytes 1572864 | tf_op jit(solution)/shard_map/optimization_barrier | solution.py:185
  228.3 4.1 %convolution_reduce-precision_fusion = f32[386,512]{1,0:T(8,128)S(1)} fusion(bf16[386,4096]{1,0:T(8,128)(2,1)S(1)} %copy-done.2, bf16[4096,512]{1,0:T(8,128)(2,1)} %all-gather.6.cloned.1.call-done), kind=kOutput, calls=%fused_computation.30 | convolution fusion | flops 1619198976 | bytes 8146944 | tf_op jit(solution)/shard_map/dot_general | solution.py:186
  233.6 9.3 %collective-permute-done.8 = bf16[1,384,512]{2,1,0:T(8,128)(2,1)S(1)} collective-permute-done((bf16[1,384,512]{2,1,0:T(8,128)(2,1)S(1)}, bf16[1,384,512]{2,1,0:T(8,128)(2,1)S(1)}, u32[]{:S(2)}, u32[]{:S(2)}) %collective-permute-start.8) | collective-permute-done | bytes 393248 | tf_op jit(solution)/shard_map/ppermute | solution.py:207
  244.4 1.9 fusion.28
  246.4 1.8 fusion.26
  249.3 1.6 add_convert_fusion
  (151 shorter events, 36.8 us)
Async XLA Ops:
  6.5 47.9 %all-gather.10.cloned.1.call-start = ((), (), s32[]{:S(2)}) async-start(), calls=%async_computation.2 | async-start | bytes 2621440 | tf_op jit(solution)/shard_map/all_gather | solution.py:122
  8.9 91.6 %all-gather.8.cloned.1.call-start = ((), (), s32[]{:S(2)}) async-start(), calls=%async_computation.1 | async-start | bytes 2621440 | tf_op jit(solution)/shard_map/all_gather | solution.py:122
  9.1 18.8 %collective-permute-start = (bf16[1,385,1024]{2,1,0:T(8,128)(2,1)S(1)}, bf16[1,385,1024]{2,1,0:T(8,128)(2,1)S(1)}, u32[]{:S(2)}, u32[]{:S(2)}) collective-permute-start(bf16[1,385,1024]{2,1,0:T(8,128)(2,1)S(1)} %maximum_bitcast_fusion), channel_id=1, source_target_pairs={{0,2},{1,3},{2,0},{3,1},{4,6},{5,7},{6,4},{7,5},{8,10},{9,11},{10,... | collective-permute-start | bytes 2365448 | tf_op jit(solution)/shard_map/ppermute | solution.py:57
  10.4 171.9 %all-gather.6.cloned.1.call-start = ((), (), s32[]{:S(2)}) async-start(), calls=%async_computation | async-start | bytes 5242880 | tf_op jit(solution)/shard_map/all_gather | solution.py:120
  28.1 4.5 %copy-start.21 = (f32[32,64]{1,0:T(8,128)S(1)}, f32[32,64]{1,0:T(8,128)}, u32[]{:S(2)}) copy-start(f32[32,64]{1,0:T(8,128)} %param.17) | copy-start | bytes 24580
  28.1 4.5 %copy-start.22 = (f32[32,64]{1,0:T(8,128)S(1)}, f32[32,64]{1,0:T(8,128)}, u32[]{:S(2)}) copy-start(f32[32,64]{1,0:T(8,128)} %param.16) | copy-start | bytes 24580
  29.7 13.1 %collective-permute-start.1 = (bf16[2,385,1024]{2,0,1:T(2,128)(2,1)S(1)}, bf16[2,385,1024]{2,0,1:T(2,128)(2,1)S(1)}, u32[]{:S(2)}, u32[]{:S(2)}) collective-permute-start(bf16[2,385,1024]{2,0,1:T(2,128)(2,1)S(1)} %copy.39), channel_id=1, source_target_pairs={{0,1},{1,0},{2,3},{3,2},{4,5},{5,4},{6,7},{7,6},{8,9},{9,8},{10,11... | collective-permute-start | bytes 4730888 | tf_op jit(solution)/shard_map/ppermute | solution.py:57
  33.9 7.1 %copy-start.8 = (bf16[1024,3,512]{2,0,1:T(8,128)(2,1)S(1)}, bf16[1024,3,512]{2,0,1:T(8,128)(2,1)}, u32[]{:S(2)}) copy-start(bf16[1024,3,512]{2,0,1:T(8,128)(2,1)} %param.14) | copy-start | bytes 9437188
  48.6 5.9 %copy-start.3 = (bf16[385,1024]{1,0:T(8,128)(2,1)}, bf16[385,1024]{1,0:T(8,128)(2,1)S(1)}, u32[]{:S(2)}) copy-start(bf16[385,1024]{1,0:T(8,128)(2,1)S(1)} %get-tuple-element.113) | copy-start | bytes 2365444
  48.6 5.9 %copy-start.4 = (bf16[385,1024]{1,0:T(8,128)(2,1)}, bf16[385,1024]{1,0:T(8,128)(2,1)S(1)}, u32[]{:S(2)}) copy-start(bf16[385,1024]{1,0:T(8,128)(2,1)S(1)} %get-tuple-element.114) | copy-start | bytes 2365444
  48.6 5.9 %copy-start.5 = (bf16[385,1024]{1,0:T(8,128)(2,1)}, bf16[385,1024]{1,0:T(8,128)(2,1)S(1)}, u32[]{:S(2)}) copy-start(bf16[385,1024]{1,0:T(8,128)(2,1)S(1)} %get-tuple-element.115) | copy-start | bytes 2365444
  48.6 5.9 %copy-start.6 = (bf16[385,1024]{1,0:T(8,128)(2,1)}, bf16[385,1024]{1,0:T(8,128)(2,1)S(1)}, u32[]{:S(2)}) copy-start(bf16[385,1024]{1,0:T(8,128)(2,1)S(1)} %get-tuple-element.116) | copy-start | bytes 2365444
  54.5 4.6 %collective-permute-start.2 = (bf16[2,4096]{1,0:T(2,128)(2,1)S(1)}, bf16[2,4096]{1,0:T(2,128)(2,1)}, u32[]{:S(2)}, u32[]{:S(2)}) collective-permute-start(bf16[2,4096]{1,0:T(2,128)(2,1)S(1)} %pad_maximum_fusion.3), channel_id=1, source_target_pairs={{0,4},{4,8},{8,12},{1,5},{5,9},{9,13},{2,6},{6,10},{10,14},{3,7},{... | collective-permute-start | bytes 49160 | tf_op jit(solution)/shard_map/ppermute | solution.py:12
  112.3 35.4 %collective-permute-start.3 = (bf16[3,512,512]{2,1,0:T(8,128)(2,1)}, bf16[3,512,512]{2,1,0:T(8,128)(2,1)S(1)}, u32[]{:S(2)}, u32[]{:S(2)}) collective-permute-start(bf16[3,512,512]{2,1,0:T(8,128)(2,1)} %fusion.6), channel_id=1, source_target_pairs={{0,16},{16,0},{1,17},{17,1},{2,18},{18,2},{3,19},{19,3},{4,20},{20... | collective-permute-start | bytes 4718600 | tf_op jit(solution)/shard_map/ppermute | solution.py:111
  115.5 65.9 %collective-permute-start.4 = (bf16[3,512,512]{2,1,0:T(8,128)(2,1)S(1)}, bf16[3,512,512]{2,1,0:T(8,128)(2,1)S(1)}, u32[]{:S(2)}, u32[]{:S(2)}) collective-permute-start(bf16[3,512,512]{2,1,0:T(8,128)(2,1)S(1)} %fusion.5), channel_id=1, source_target_pairs={{0,16},{16,0},{1,17},{17,1},{2,18},{18,2},{3,19},{19,3},{4,20},{20... | collective-permute-start | bytes 4718600 | tf_op jit(solution)/shard_map/ppermute | solution.py:111
  122.6 25.9 %copy-start.30 = (f32[1,1,512]{2,1,0:T(1,128)S(1)}, f32[1,1,512]{2,1,0:T(1,128)}, u32[]{:S(2)}) copy-start(f32[1,1,512]{2,1,0:T(1,128)} %get-tuple-element.126) | copy-start | bytes 6148
  122.7 25.9 %copy-start.31 = (f32[1,1,512]{2,1,0:T(1,128)S(1)}, f32[1,1,512]{2,1,0:T(1,128)}, u32[]{:S(2)}) copy-start(f32[1,1,512]{2,1,0:T(1,128)} %get-tuple-element.127) | copy-start | bytes 6148
  122.7 25.9 %copy-start.32 = (f32[1,1,512]{2,1,0:T(1,128)S(1)}, f32[1,1,512]{2,1,0:T(1,128)}, u32[]{:S(2)}) copy-start(f32[1,1,512]{2,1,0:T(1,128)} %get-tuple-element.128) | copy-start | bytes 6148
  148.8 33.5 %copy-start.27 = (f32[1,1,512]{2,1,0:T(1,128)S(1)}, f32[1,1,512]{2,1,0:T(1,128)}, u32[]{:S(2)}) copy-start(f32[1,1,512]{2,1,0:T(1,128)} %get-tuple-element.123) | copy-start | bytes 6148
  148.8 33.5 %copy-start.28 = (f32[1,1,512]{2,1,0:T(1,128)S(1)}, f32[1,1,512]{2,1,0:T(1,128)}, u32[]{:S(2)}) copy-start(f32[1,1,512]{2,1,0:T(1,128)} %get-tuple-element.124) | copy-start | bytes 6148
  148.8 33.5 %copy-start.29 = (f32[1,1,512]{2,1,0:T(1,128)S(1)}, f32[1,1,512]{2,1,0:T(1,128)}, u32[]{:S(2)}) copy-start(f32[1,1,512]{2,1,0:T(1,128)} %get-tuple-element.125) | copy-start | bytes 6148
  187.0 8.5 %copy-start.35 = (f32[3]{0:T(128)S(1)}, f32[3]{0:T(128)}, u32[]{:S(2)}) copy-start(f32[3]{0:T(128)} %iota_convert_fusion) | copy-start | bytes 40
  187.0 31.5 %copy-start.11 = (f32[32,128,64]{1,2,0:T(8,128)S(1)}, f32[32,128,64]{1,2,0:T(8,128)}, u32[]{:S(2)}) copy-start(f32[32,128,64]{1,2,0:T(8,128)} %exponential_multiply_fusion) | copy-start | bytes 3145732
  189.6 31.2 %copy-start.17 = (f32[32,128,128]{2,1,0:T(8,128)S(1)}, f32[32,128,128]{2,1,0:T(8,128)}, u32[]{:S(2)}) copy-start(f32[32,128,128]{2,1,0:T(8,128)} %convolution_select_fusion) | copy-start | bytes 6291460
  189.7 6.0 %collective-permute-start.7 = (f32[32,64,16]{1,2,0:T(8,128)S(1)}, f32[32,64,16]{1,2,0:T(8,128)S(1)}, u32[]{:S(2)}, u32[]{:S(2)}) collective-permute-start(f32[32,64,16]{1,2,0:T(8,128)S(1)} %get-tuple-element.53), channel_id=1, source_target_pairs={{0,12},{1,13},{2,14},{3,15},{16,28},{17,29},{18,30},{19,31}} | collective-permute-start | bytes 393224 | tf_op jit(solution)/shard_map/ppermute | solution.py:177
  190.5 15.1 %collective-permute-start.6 = (f32[32,64,16]{1,2,0:T(8,128)S(1)}, f32[32,64,16]{1,2,0:T(8,128)S(1)}, u32[]{:S(2)}, u32[]{:S(2)}) collective-permute-start(f32[32,64,16]{1,2,0:T(8,128)S(1)} %get-tuple-element.53), channel_id=1, source_target_pairs={{0,8},{4,12},{1,9},{5,13},{2,10},{6,14},{3,11},{7,15},{16,24},{20,... | collective-permute-start | bytes 393224 | tf_op jit(solution)/shard_map/ppermute | solution.py:177
  191.8 26.7 %collective-permute-start.5 = (f32[32,64,16]{1,2,0:T(8,128)S(1)}, f32[32,64,16]{1,2,0:T(8,128)S(1)}, u32[]{:S(2)}, u32[]{:S(2)}) collective-permute-start(f32[32,64,16]{1,2,0:T(8,128)S(1)} %get-tuple-element.53), channel_id=1, source_target_pairs={{0,4},{4,8},{8,12},{1,5},{5,9},{9,13},{2,6},{6,10},{10,14},{3,7},{... | collective-permute-start | bytes 393224 | tf_op jit(solution)/shard_map/ppermute | solution.py:177
  228.3 4.1 %copy-start.24 = (f32[1,1,512]{2,1,0:T(1,128)S(1)}, f32[1,1,512]{2,1,0:T(1,128)}, u32[]{:S(2)}) copy-start(f32[1,1,512]{2,1,0:T(1,128)} %get-tuple-element.122) | copy-start | bytes 6148
  228.3 4.1 %copy-start.25 = (f32[1,1,512]{2,1,0:T(1,128)S(1)}, f32[1,1,512]{2,1,0:T(1,128)}, u32[]{:S(2)}) copy-start(f32[1,1,512]{2,1,0:T(1,128)} %get-tuple-element.129) | copy-start | bytes 6148
  228.3 4.1 %copy-start.26 = (f32[1,1,512]{2,1,0:T(1,128)S(1)}, f32[1,1,512]{2,1,0:T(1,128)}, u32[]{:S(2)}) copy-start(f32[1,1,512]{2,1,0:T(1,128)} %get-tuple-element.130) | copy-start | bytes 6148
  232.7 10.3 %collective-permute-start.8 = (bf16[1,384,512]{2,1,0:T(8,128)(2,1)S(1)}, bf16[1,384,512]{2,1,0:T(8,128)(2,1)S(1)}, u32[]{:S(2)}, u32[]{:S(2)}) collective-permute-start(bf16[1,384,512]{2,1,0:T(8,128)(2,1)S(1)} %bitcast.135), channel_id=1, source_target_pairs={{0,2},{1,3},{2,0},{3,1},{4,6},{5,7},{6,4},{7,5},{8,10},{9,11},{10,... | collective-permute-start | bytes 1179656 | tf_op jit(solution)/shard_map/ppermute | solution.py:207
  243.0 5.2 %collective-permute-start.9 = (bf16[2,384,512]{2,1,0:T(8,128)(2,1)S(1)}, bf16[2,384,512]{2,1,0:T(8,128)(2,1)S(1)}, u32[]{:S(2)}, u32[]{:S(2)}) collective-permute-start(bf16[2,384,512]{2,1,0:T(8,128)(2,1)S(1)} %pad_maximum_fusion.2), channel_id=1, source_target_pairs={{0,1},{1,0},{2,3},{3,2},{4,5},{5,4},{6,7},{7,6},{8,9},{9,8},{10,11... | collective-permute-start | bytes 2359304 | tf_op jit(solution)/shard_map/ppermute | solution.py:207
  (18 other events, 49.5 us)
Sparse Core Ops, SparseCore 0:
  9.0 45.3 all-gather.9
  56.0 44.4 all-gather.7
  102.1 79.2 all-gather.5

commit v6 on v3

--- a/solution.py
+++ b/solution.py
@@ -154,7 +154,10 @@
     filtered = {s: project(s, relayed[s][1]) for s in order[:-1]}
     first = order[0]
     if relayed[last][1] is None:
-        filtered[first], tied = lax.optimization_barrier((filtered[first], relayed[last][0]))
+        early = [s for s in order[:-1]]
+        held, tied = lax.optimization_barrier(([filtered[s] for s in early], relayed[last][0]))
+        for s, value in zip(early, held):
+            filtered[s] = value
         relayed[last] = (tied, relay(relay_send(tied)))
     product = filtered[0] * filtered[2]
     blocks = tok_rows // block_rows

time: 220 us -> 221 us (level); the launches traced: 220 us -> 216 us
    all_gather x3, waiting for transfers between devices: 62.1 us -> 37.3 us  [body(): got = lax.all_gather(own[:, s, :], 'ctx', axis=0)]
    ppermute x3, waiting for transfers between devices: 6.3 us -> 27.9 us  [relay(): received.append(lax.ppermute(send, 'grp', pairs))]
  transfers between devices with their start and end apart: 14 -> 14, of which waited for: 8 -> 9; matrix products, arithmetic and copies ran while one was open for 30% -> 31% of each run, Pallas kernels for 0% -> 0%
where the time goes in v6:
time: 221 us; the launch traced here: 216 us
  waiting for transfers between devices  97.7 us (44%)
  matrix products  32.1 us (15%)
  other arithmetic  26.3 us (12%)
  local copies, waits for them, and re-layouts  25.6 us (12%)
  starting transfers between devices  20.7 us (9%)
  between operations  14 us (6%)
    all_gather x3, waiting for transfers between devices, body(): got = lax.all_gather(own[:, s, :], 'ctx', axis=0)  37.3 us
    ppermute x3, waiting for transfers between devices, relay(): received.append(lax.ppermute(send, 'grp', pairs))  27.9 us
    ppermute x2, waiting for transfers between devices, gather_by_swaps(): held = jnp.concatenate([held, lax.ppermute(held, axis, pairs)], axis=0)  14.6 us
    concatenate x3, other arithmetic, relay_send(): doubled = jnp.concatenate([got, got], axis=0)  8.49 us
    ppermute x3, waiting for transfers between devices, body(): arrived = lax.ppermute(own_state, 'ctx', pairs)  8.46 us
    ppermute x2, waiting for transfers between devices, body(): arrived = lax.ppermute(held, 'tp', pairs)  8.38 us
    unnamed x82, local copies, waits for them, and re-layouts  7.59 us
    ppermute x3, starting transfers between devices, body(): arrived = lax.ppermute(own_state, 'ctx', pairs)  7.11 us
  transfers between devices with their start and end apart: 14, of which 9 were waited for; matrix products, arithmetic and copies ran while one was open for 31% of the time, Pallas kernels for 0%

profile of v6, /device:TPU:0, one launch (start us, length us, event | category | flops | bytes accessed | tf_op | source)
XLA Modules:
  0.0 216.4 jit_solution(15410819846927851009)
XLA Ops:
  6.5 2.6 %constant_dynamic-slice_fusion.2 = (bf16[512,1,512]{2,0,1:T(8,128)(2,1)}, bf16[512,1,512]{2,0,1:T(8,128)(2,1)}, bf16[512,1,512]{2,0,1:T(8,128)(2,1)}) fusion(bf16[1024,3,512]{2,0,1:T(8,128)(2,1)} %param.14, s32[]{:T(128)S(6)} %select_n.104, s32[]{:T(128)S(6)} %add.242, s32[]{:T(128)S(6)} %add.241), kind=kLoop, calls=%fused_computation.135 | loop fusion | bytes 3145740 | tf_op jit(solution)/shard_map/slice | solution.py:117
  10.1 3.0 %collective-permute-start = (bf16[1,385,1024]{2,1,0:T(8,128)(2,1)S(1)}, bf16[1,385,1024]{2,1,0:T(8,128)(2,1)S(1)}, u32[]{:S(2)}, u32[]{:S(2)}) collective-permute-start(bf16[1,385,1024]{2,1,0:T(8,128)(2,1)S(1)} %maximum_bitcast_fusion), channel_id=1, source_target_pairs={{0,2},{1,3},{2,0},{3,1},{4,6},{5,7},{6,4},{7,5},{8,10},{9,11},{10,... | collective-permute-start | bytes 2365448 | tf_op jit(solution)/shard_map/ppermute | solution.py:57
  16.4 14.6 %collective-permute-done = bf16[1,385,1024]{2,1,0:T(8,128)(2,1)S(1)} collective-permute-done((bf16[1,385,1024]{2,1,0:T(8,128)(2,1)S(1)}, bf16[1,385,1024]{2,1,0:T(8,128)(2,1)S(1)}, u32[]{:S(2)}, u32[]{:S(2)}) %collective-permute-start) | collective-permute-done | bytes 788512 | tf_op jit(solution)/shard_map/ppermute | solution.py:57
  36.6 5.5 %convolution_select_fusion = f32[32,128,128]{2,1,0:T(8,128)} fusion(pred[128,128]{1,0:T(8,128)(4,1)S(1)} %broadcast_compare_fusion, f32[32,64]{1,0:T(8,128)S(1)} %copy-done.26, f32[128]{0:T(128)S(1)} %iota_convert_fusion.1, f32[32,64]{1,0:T(8,128)S(1)} %get-tuple-element.138, f32[32,64]{1,0:T(8,128)S(1)} %get-tuple-element.137), kind=kOutput, calls=%fused_computation.23 | convolution fusion | flops 403963904 | bytes 2138624 | tf_op jit(solution)/shard_map/gin,gjn->gij/dot_general | solution.py:91
  42.1 1.8 fusion.72
  44.3 2.0 pad_maximum_fusion
  46.3 2.7 %gather_fusion.1 = bf16[4,385,1024]{2,1,0:T(8,128)(2,1)S(1)} fusion(bf16[4,385,1024]{2,1,0:T(8,128)(2,1)} %pad_maximum_fusion, s32[1024]{0:T(1024)S(1)} %pad_clamp_fusion.2), kind=kCustom, calls=%fused_computation.3 | custom fusion | bytes 6307856 | tf_op jit(solution)/shard_map/jit(_take)/gather | solution.py:62
  51.4 4.3 %collective-permute-start.2 = (bf16[2,4096]{1,0:T(2,128)(2,1)S(1)}, bf16[2,4096]{1,0:T(2,128)(2,1)}, u32[]{:S(2)}, u32[]{:S(2)}) collective-permute-start(bf16[2,4096]{1,0:T(2,128)(2,1)S(1)} %pad_maximum_fusion.3), channel_id=1, source_target_pairs={{0,4},{4,8},{8,12},{1,5},{5,9},{9,13},{2,6},{6,10},{10,14},{3,7},{... | collective-permute-start | bytes 49160 | tf_op jit(solution)/shard_map/ppermute | solution.py:12
  56.5 3.5 %maximum_maximum_fusion = bf16[387,4096]{1,0:T(8,128)(2,1)S(1)} fusion(bf16[385,1024]{1,0:T(8,128)(2,1)} %copy-done.2, bf16[385,1024]{1,0:T(8,128)(2,1)} %copy-done.3, bf16[385,1024]{1,0:T(8,128)(2,1)} %copy-done.4, bf16[385,1024]{1,0:T(8,128)(2,1)} %copy-done.1, bf16[2,4096]{1,0:T(2,128)(2,1)} %collective-permute-done.2), kind=kLoop, calls=%fused_computation.18 | loop fusion | flops 15851520 | bytes 6340608 | tf_op jit(solution)/shard_map/concatenate | solution.py:100
  60.1 3.2 %fusion.7 = bf16[3,512,512]{2,1,0:T(8,128)(2,1)} fusion(s32[]{:T(128)S(6)} %select_n.106, bf16[4,512,512]{2,1,0:T(8,128)(2,1)} %bitcast.152), kind=kLoop, calls=%fused_computation.29 | loop fusion | flops 786432 | bytes 3670020 | tf_op jit(solution)/shard_map/concatenate | solution.py:104
  67.9 2.0 gather_fusion.2
  69.8 1.9 gather_fusion.3
  73.3 30.5 %all-gather.9.cloned.1.call-done = bf16[2048,1,512]{2,0,1:T(8,128)(2,1)} async-done(((bf16[512,1,512]{2,0,1:T(8,128)(2,1)}), bf16[2048,1,512]{2,0,1:T(8,128)(2,1)}) %all-gather.9.cloned.1.call-update) | async-done | bytes 2097168 | tf_op jit(solution)/shard_map/all_gather | solution.py:117
  103.8 2.1 fusion.6
  107.5 2.5 %convolution_bitcast_fusion.5 = f32[386,512]{1,0:T(8,128)S(1)} fusion(bf16[4,512,512]{2,1,0:T(8,128)(2,1)S(1)} %bitcast.153, bf16[4,386,512]{2,1,0:T(8,128)(2,1)} %gather_fusion.2, pred[4]{0:T(512)(128)(4,1)S(1)} %copy-done.39), kind=kOutput, calls=%fused_computation.36 | convolution fusion | flops 810291200 | bytes 4468740 | tf_op jit(solution)/shard_map/ktr,krc->tc/dot_general | solution.py:143
  114.8 2.2 %fusion.15 = f32[386,512]{1,0:T(8,128)S(1)} fusion(f32[386,512]{1,0:T(8,128)S(1)} %convolution_add_fusion.2, bf16[4,386,512]{2,1,0:T(8,128)(2,1)S(1)} %broadcast_select_fusion.1, bf16[3,512,512]{2,1,0:T(8,128)(2,1)} %collective-permute-done.3), kind=kOutput, calls=%fused_computation.44 | convolution fusion | flops 607520768 | bytes 4734976 | tf_op jit(solution)/shard_map/ktr,krc->tc/dot_general | solution.py:147
  117.3 24.7 %collective-permute-done.4 = bf16[3,512,512]{2,1,0:T(8,128)(2,1)S(1)} collective-permute-done((bf16[3,512,512]{2,1,0:T(8,128)(2,1)S(1)}, bf16[3,512,512]{2,1,0:T(8,128)(2,1)S(1)}, u32[]{:S(2)}, u32[]{:S(2)}) %collective-permute-start.4) | collective-permute-done | bytes 1572896 | tf_op jit(solution)/shard_map/ppermute | solution.py:111
  143.0 6.8 %all-gather.11.cloned.1.call-done = bf16[2048,1,512]{2,0,1:T(8,128)(2,1)} async-done(((bf16[512,1,512]{2,0,1:T(8,128)(2,1)}), bf16[2048,1,512]{2,0,1:T(8,128)(2,1)}) %all-gather.11.cloned.1.call-update) | async-done | bytes 2097168 | tf_op jit(solution)/shard_map/all_gather | solution.py:117
  149.8 3.2 %fusion.5 = bf16[3,512,512]{2,1,0:T(8,128)(2,1)} fusion(s32[]{:T(128)S(6)} %select_n.106, bf16[4,512,512]{2,1,0:T(8,128)(2,1)} %bitcast.150), kind=kLoop, calls=%fused_computation.27 | loop fusion | flops 786432 | bytes 3670020 | tf_op jit(solution)/shard_map/concatenate | solution.py:104
  155.9 2.0 convolution_bitcast_fusion.6
  157.8 2.6 %while.13 = (s32[]{:T(128)}, f32[32,64,16]{1,2,0:T(8,128)S(1)}, f32[3,32,64,16]{2,3,1,0:T(8,128)}, f32[32,64,1]{1,0,2:T(8,128)S(1)}, f32[3,32,64,16]{2,3,0,1:T(8,128)S(1)}, /*index=5*/s32[]{:T(128)}, s32[]{:T(128)}) while((s32[]{:T(128)}, f32[32,64,16]{1,2,0:T(8,128)S(1)}, f32[3,32,64,16]{2,3,1,0:T(8,128)}, ...), condition=%wide.region_2.4_spmd.clone, body=%wide.region_1.3_spmd.clone.sunk | while | flops 131075 | bytes 794728 | solution.py:173
  160.4 3.3 %collective-permute-start.8 = (f32[32,64,16]{1,2,0:T(8,128)S(1)}, f32[32,64,16]{1,2,0:T(8,128)S(1)}, u32[]{:S(2)}, u32[]{:S(2)}) collective-permute-start(f32[32,64,16]{1,2,0:T(8,128)S(1)} %get-tuple-element.53), channel_id=1, source_target_pairs={{0,12},{1,13},{2,14},{3,15},{16,28},{17,29},{18,30},{19,31}} | collective-permute-start | bytes 393224 | tf_op jit(solution)/shard_map/ppermute | solution.py:177
  165.1 2.5 %collective-permute-start.6 = (f32[32,64,16]{1,2,0:T(8,128)S(1)}, f32[32,64,16]{1,2,0:T(8,128)S(1)}, u32[]{:S(2)}, u32[]{:S(2)}) collective-permute-start(f32[32,64,16]{1,2,0:T(8,128)S(1)} %get-tuple-element.53), channel_id=1, source_target_pairs={{0,4},{4,8},{8,12},{1,5},{5,9},{9,13},{2,6},{6,10},{10,14},{3,7},{... | collective-permute-start | bytes 393224 | tf_op jit(solution)/shard_map/ppermute | solution.py:177
  167.6 3.1 %convolution_bitcast_fusion.3 = f32[386,512]{1,0:T(8,128)S(1)} fusion(bf16[4,512,512]{2,1,0:T(8,128)(2,1)} %bitcast.151, bf16[4,386,512]{2,1,0:T(8,128)(2,1)} %gather_fusion.2, pred[4]{0:T(512)(128)(4,1)S(1)} %copy-done.39), kind=kOutput, calls=%fused_computation.34 | convolution fusion | flops 810291200 | bytes 4468740 | tf_op jit(solution)/shard_map/ktr,krc->tc/dot_general | solution.py:143
  172.0 4.1 %collective-permute-done.7 = f32[32,64,16]{1,2,0:T(8,128)S(1)} collective-permute-done((f32[32,64,16]{1,2,0:T(8,128)S(1)}, f32[32,64,16]{1,2,0:T(8,128)S(1)}, u32[]{:S(2)}, u32[]{:S(2)}) %collective-permute-start.7) | collective-permute-done | bytes 131104 | tf_op jit(solution)/shard_map/ppermute | solution.py:177
  176.1 4.3 %collective-permute-done.6 = f32[32,64,16]{1,2,0:T(8,128)S(1)} collective-permute-done((f32[32,64,16]{1,2,0:T(8,128)S(1)}, f32[32,64,16]{1,2,0:T(8,128)S(1)}, u32[]{:S(2)}, u32[]{:S(2)}) %collective-permute-start.6) | collective-permute-done | bytes 131104 | tf_op jit(solution)/shard_map/ppermute | solution.py:177
  182.2 3.4 %fusion.11 = f32[3,128,32,16]{1,3,0,2:T(8,128)S(1)} fusion(f32[32,3,16,128]{3,2,1,0:T(8,128)S(1)} %fusion.20, f32[32,128,128]{2,1,0:T(8,128)S(1)} %copy-done.18, f32[3,128,32,16]{1,0,3,2:T(4,128)S(1)} %reshape.174), kind=kOutput, calls=%fused_computation.41 | convolution fusion | flops 302186496 | bytes 4456448 | tf_op jit(solution)/shard_map/gij,bjgc->bigc/dot_general | solution.py:165
  186.1 3.3 %collective-permute-done.5 = bf16[3,512,512]{2,1,0:T(8,128)(2,1)} collective-permute-done((bf16[3,512,512]{2,1,0:T(8,128)(2,1)}, bf16[3,512,512]{2,1,0:T(8,128)(2,1)}, u32[]{:S(2)}, u32[]{:S(2)}) %collective-permute-start.5) | collective-permute-done | bytes 1572896 | tf_op jit(solution)/shard_map/ppermute | solution.py:111
  190.5 2.5 %fusion.19 = f32[386,512]{1,0:T(8,128)S(1)} fusion(f32[386,512]{1,0:T(8,128)} %convolution_add_fusion, bf16[4,386,512]{2,1,0:T(8,128)(2,1)S(1)} %copy-done.8, bf16[3,512,512]{2,1,0:T(8,128)(2,1)} %collective-permute-done.5), kind=kOutput, calls=%fused_computation.48 | convolution fusion | flops 607520768 | bytes 4734976 | tf_op jit(solution)/shard_map/ktr,krc->tc/dot_general | solution.py:147
  194.8 8.4 %collective-permute-done.9 = bf16[1,384,512]{2,1,0:T(8,128)(2,1)S(1)} collective-permute-done((bf16[1,384,512]{2,1,0:T(8,128)(2,1)S(1)}, bf16[1,384,512]{2,1,0:T(8,128)(2,1)S(1)}, u32[]{:S(2)}, u32[]{:S(2)}) %collective-permute-start.9) | collective-permute-done | bytes 393248 | tf_op jit(solution)/shard_map/ppermute | solution.py:201
  203.4 1.9 fusion.31
  205.3 1.8 fusion.29
  (163 shorter events, 42.9 us)
Async XLA Ops:
  6.5 53.5 %all-gather.7.cloned.1.call-start = ((), (), s32[]{:S(2)}) async-start(), calls=%async_computation | async-start | bytes 2621440 | tf_op jit(solution)/shard_map/all_gather | solution.py:117
  9.1 4.1 %copy-start = (s32[4]{0:T(128)S(1)}, s32[4]{0:T(128)}, u32[]{:S(2)}) copy-start(s32[4]{0:T(128)} %constant.130.clone) | copy-start | bytes 52
  9.2 94.6 %all-gather.9.cloned.1.call-start = ((), (), s32[]{:S(2)}) async-start(), calls=%async_computation.1 | async-start | bytes 2621440 | tf_op jit(solution)/shard_map/all_gather | solution.py:117
  9.2 6.6 %copy-start.27 = (f32[3,3,512]{2,1,0:T(4,128)S(1)}, f32[3,3,512]{2,1,0:T(4,128)}, u32[]{:S(2)}) copy-start(f32[3,3,512]{2,1,0:T(4,128)} %param.15) | copy-start | bytes 55300
  9.9 139.9 %all-gather.11.cloned.1.call-start = ((), (), s32[]{:S(2)}) async-start(), calls=%async_computation.2 | async-start | bytes 2621440 | tf_op jit(solution)/shard_map/all_gather | solution.py:117
  10.1 20.9 %collective-permute-start = (bf16[1,385,1024]{2,1,0:T(8,128)(2,1)S(1)}, bf16[1,385,1024]{2,1,0:T(8,128)(2,1)S(1)}, u32[]{:S(2)}, u32[]{:S(2)}) collective-permute-start(bf16[1,385,1024]{2,1,0:T(8,128)(2,1)S(1)} %maximum_bitcast_fusion), channel_id=1, source_target_pairs={{0,2},{1,3},{2,0},{3,1},{4,6},{5,7},{6,4},{7,5},{8,10},{9,11},{10,... | collective-permute-start | bytes 2365448 | tf_op jit(solution)/shard_map/ppermute | solution.py:57
  32.8 11.1 %collective-permute-start.1 = (bf16[2,385,1024]{2,0,1:T(2,128)(2,1)S(1)}, bf16[2,385,1024]{2,0,1:T(2,128)(2,1)S(1)}, u32[]{:S(2)}, u32[]{:S(2)}) collective-permute-start(bf16[2,385,1024]{2,0,1:T(2,128)(2,1)S(1)} %copy.40), channel_id=1, source_target_pairs={{0,1},{1,0},{2,3},{3,2},{4,5},{5,4},{6,7},{7,6},{8,9},{9,8},{10,11... | collective-permute-start | bytes 4730888 | tf_op jit(solution)/shard_map/ppermute | solution.py:57
  35.0 7.1 %copy-start.5 = (bf16[1024,3,512]{2,0,1:T(8,128)(2,1)S(1)}, bf16[1024,3,512]{2,0,1:T(8,128)(2,1)}, u32[]{:S(2)}) copy-start(bf16[1024,3,512]{2,0,1:T(8,128)(2,1)} %param.14) | copy-start | bytes 9437188
  51.4 5.1 %collective-permute-start.2 = (bf16[2,4096]{1,0:T(2,128)(2,1)S(1)}, bf16[2,4096]{1,0:T(2,128)(2,1)}, u32[]{:S(2)}, u32[]{:S(2)}) collective-permute-start(bf16[2,4096]{1,0:T(2,128)(2,1)S(1)} %pad_maximum_fusion.3), channel_id=1, source_target_pairs={{0,4},{4,8},{8,12},{1,5},{5,9},{9,13},{2,6},{6,10},{10,14},{3,7},{... | collective-permute-start | bytes 49160 | tf_op jit(solution)/shard_map/ppermute | solution.py:12
  71.8 43.0 %collective-permute-start.3 = (bf16[3,512,512]{2,1,0:T(8,128)(2,1)}, bf16[3,512,512]{2,1,0:T(8,128)(2,1)}, u32[]{:S(2)}, u32[]{:S(2)}) collective-permute-start(bf16[3,512,512]{2,1,0:T(8,128)(2,1)} %fusion.7), channel_id=1, source_target_pairs={{0,16},{16,0},{1,17},{17,1},{2,18},{18,2},{3,19},{19,3},{4,20},{20... | collective-permute-start | bytes 4718600 | tf_op jit(solution)/shard_map/ppermute | solution.py:111
  103.8 3.7 %copy-start.19 = (bf16[2048,1,512]{2,0,1:T(8,128)(2,1)S(1)}, bf16[2048,1,512]{2,0,1:T(8,128)(2,1)}, u32[]{:S(2)}) copy-start(bf16[2048,1,512]{2,0,1:T(8,128)(2,1)} %all-gather.7.cloned.1.call-done) | copy-start | bytes 6291460
  103.8 3.7 %copy-start.39 = (pred[4]{0:T(512)(128)(4,1)S(1)}, pred[4]{0:T(512)(128)(4,1)}, u32[]{:S(2)}) copy-start(pred[4]{0:T(512)(128)(4,1)} %compare_and_fusion.1) | copy-start | bytes 16
  105.9 4.0 %copy-start.6 = (bf16[4,386,512]{2,1,0:T(8,128)(2,1)S(1)}, bf16[4,386,512]{2,1,0:T(8,128)(2,1)}, u32[]{:S(2)}) copy-start(bf16[4,386,512]{2,1,0:T(8,128)(2,1)} %gather_fusion.3) | copy-start | bytes 4743172
  105.9 4.0 %copy-start.38 = (pred[4]{0:T(512)(128)(4,1)S(1)}, pred[4]{0:T(512)(128)(4,1)}, u32[]{:S(2)}) copy-start(pred[4]{0:T(512)(128)(4,1)} %get-tuple-element.111) | copy-start | bytes 16
  105.9 36.0 %collective-permute-start.4 = (bf16[3,512,512]{2,1,0:T(8,128)(2,1)S(1)}, bf16[3,512,512]{2,1,0:T(8,128)(2,1)S(1)}, u32[]{:S(2)}, u32[]{:S(2)}) collective-permute-start(bf16[3,512,512]{2,1,0:T(8,128)(2,1)S(1)} %fusion.6), channel_id=1, source_target_pairs={{0,16},{16,0},{1,17},{17,1},{2,18},{18,2},{3,19},{19,3},{4,20},{20... | collective-permute-start | bytes 4718600 | tf_op jit(solution)/shard_map/ppermute | solution.py:111
  110.2 31.8 %copy-start.7 = (bf16[4,386,512]{2,1,0:T(8,128)(2,1)}, bf16[4,386,512]{2,1,0:T(8,128)(2,1)S(1)}, u32[]{:S(2)}) copy-start(bf16[4,386,512]{2,1,0:T(8,128)(2,1)S(1)} %broadcast_select_fusion.1) | copy-start | bytes 4743172
  117.3 25.5 %copy-start.31 = (f32[1,1,512]{2,1,0:T(1,128)S(1)}, f32[1,1,512]{2,1,0:T(1,128)}, u32[]{:S(2)}) copy-start(f32[1,1,512]{2,1,0:T(1,128)} %get-tuple-element.124) | copy-start | bytes 6148
  117.3 25.5 %copy-start.32 = (f32[1,1,512]{2,1,0:T(1,128)S(1)}, f32[1,1,512]{2,1,0:T(1,128)}, u32[]{:S(2)}) copy-start(f32[1,1,512]{2,1,0:T(1,128)} %get-tuple-element.125) | copy-start | bytes 6148
  117.3 25.5 %copy-start.33 = (f32[1,1,512]{2,1,0:T(1,128)S(1)}, f32[1,1,512]{2,1,0:T(1,128)}, u32[]{:S(2)}) copy-start(f32[1,1,512]{2,1,0:T(1,128)} %get-tuple-element.126) | copy-start | bytes 6148
  153.0 36.3 %collective-permute-start.5 = (bf16[3,512,512]{2,1,0:T(8,128)(2,1)}, bf16[3,512,512]{2,1,0:T(8,128)(2,1)}, u32[]{:S(2)}, u32[]{:S(2)}) collective-permute-start(bf16[3,512,512]{2,1,0:T(8,128)(2,1)} %fusion.5), channel_id=1, source_target_pairs={{0,16},{16,0},{1,17},{17,1},{2,18},{18,2},{3,19},{19,3},{4,20},{20... | collective-permute-start | bytes 4718600 | tf_op jit(solution)/shard_map/ppermute | solution.py:111
  160.4 10.3 %copy-start.8 = (bf16[4,386,512]{2,1,0:T(8,128)(2,1)S(1)}, bf16[4,386,512]{2,1,0:T(8,128)(2,1)}, u32[]{:S(2)}) copy-start(bf16[4,386,512]{2,1,0:T(8,128)(2,1)} %copy-done.7) | copy-start | bytes 4743172
  160.4 10.3 %copy-start.15 = (bf16[1024,1,512]{2,0,1:T(8,128)(2,1)S(1)}, bf16[1024,1,512]{2,0,1:T(8,128)(2,1)}, u32[]{:S(2)}) copy-start(bf16[1024,1,512]{2,0,1:T(8,128)(2,1)} %get-tuple-element.117) | copy-start | bytes 3145732
  160.4 11.6 %collective-permute-start.8 = (f32[32,64,16]{1,2,0:T(8,128)S(1)}, f32[32,64,16]{1,2,0:T(8,128)S(1)}, u32[]{:S(2)}, u32[]{:S(2)}) collective-permute-start(f32[32,64,16]{1,2,0:T(8,128)S(1)} %get-tuple-element.53), channel_id=1, source_target_pairs={{0,12},{1,13},{2,14},{3,15},{16,28},{17,29},{18,30},{19,31}} | collective-permute-start | bytes 393224 | tf_op jit(solution)/shard_map/ppermute | solution.py:177
  163.8 12.4 %collective-permute-start.7 = (f32[32,64,16]{1,2,0:T(8,128)S(1)}, f32[32,64,16]{1,2,0:T(8,128)S(1)}, u32[]{:S(2)}, u32[]{:S(2)}) collective-permute-start(f32[32,64,16]{1,2,0:T(8,128)S(1)} %get-tuple-element.53), channel_id=1, source_target_pairs={{0,8},{4,12},{1,9},{5,13},{2,10},{6,14},{3,11},{7,15},{16,24},{20,... | collective-permute-start | bytes 393224 | tf_op jit(solution)/shard_map/ppermute | solution.py:177
  165.1 15.4 %collective-permute-start.6 = (f32[32,64,16]{1,2,0:T(8,128)S(1)}, f32[32,64,16]{1,2,0:T(8,128)S(1)}, u32[]{:S(2)}, u32[]{:S(2)}) collective-permute-start(f32[32,64,16]{1,2,0:T(8,128)S(1)} %get-tuple-element.53), channel_id=1, source_target_pairs={{0,4},{4,8},{8,12},{1,5},{5,9},{9,13},{2,6},{6,10},{10,14},{3,7},{... | collective-permute-start | bytes 393224 | tf_op jit(solution)/shard_map/ppermute | solution.py:177
  170.7 9.8 %copy-start.23 = (f32[32,64]{1,0:T(8,128)S(1)}, f32[32,64]{1,0:T(8,128)}, u32[]{:S(2)}) copy-start(f32[32,64]{1,0:T(8,128)} %get-tuple-element.134) | copy-start | bytes 24580
  170.7 9.8 %copy-start.24 = (f32[32,64]{1,0:T(8,128)S(1)}, f32[32,64]{1,0:T(8,128)}, u32[]{:S(2)}) copy-start(f32[32,64]{1,0:T(8,128)} %get-tuple-element.135) | copy-start | bytes 24580
  170.7 9.9 %copy-start.11 = (f32[32,128,64]{1,2,0:T(8,128)S(1)}, f32[32,128,64]{1,2,0:T(8,128)}, u32[]{:S(2)}) copy-start(f32[32,128,64]{1,2,0:T(8,128)} %exponential_multiply_fusion) | copy-start | bytes 3145732
  170.7 9.9 %copy-start.22 = (f32[3,32,64,16]{2,3,1,0:T(8,128)S(1)}, f32[3,32,64,16]{2,3,1,0:T(8,128)}, u32[]{:S(2)}) copy-start(f32[3,32,64,16]{2,3,1,0:T(8,128)} %get-tuple-element.54) | copy-start | bytes 1179652
  193.3 9.9 %collective-permute-start.9 = (bf16[1,384,512]{2,1,0:T(8,128)(2,1)S(1)}, bf16[1,384,512]{2,1,0:T(8,128)(2,1)S(1)}, u32[]{:S(2)}, u32[]{:S(2)}) collective-permute-start(bf16[1,384,512]{2,1,0:T(8,128)(2,1)S(1)} %bitcast.147), channel_id=1, source_target_pairs={{0,2},{1,3},{2,0},{3,1},{4,6},{5,7},{6,4},{7,5},{8,10},{9,11},{10,... | collective-permute-start | bytes 1179656 | tf_op jit(solution)/shard_map/ppermute | solution.py:201
  203.3 3.9 %collective-permute-start.10 = (bf16[2,384,512]{2,1,0:T(8,128)(2,1)S(1)}, bf16[2,384,512]{2,1,0:T(8,128)(2,1)S(1)}, u32[]{:S(2)}, u32[]{:S(2)}) collective-permute-start(bf16[2,384,512]{2,1,0:T(8,128)(2,1)S(1)} %pad_maximum_fusion.2), channel_id=1, source_target_pairs={{0,1},{1,0},{2,3},{3,2},{4,5},{5,4},{6,7},{7,6},{8,9},{9,8},{10,11... | collective-permute-start | bytes 2359304 | tf_op jit(solution)/shard_map/ppermute | solution.py:201
  203.4 3.8 %copy-start.9 = (bf16[2048,1024]{1,0:T(8,128)(2,1)S(1)}, bf16[2048,1024]{1,0:T(8,128)(2,1)}, u32[]{:S(2)}) copy-start(bf16[2048,1024]{1,0:T(8,128)(2,1)} %param.18) | copy-start | bytes 12582916
  (22 other events, 44.6 us)
Sparse Core Ops, SparseCore 0:
  9.3 48.3 all-gather.6
  59.3 44.4 all-gather.8
  105.3 44.4 all-gather.10

commit v7 on v6

--- a/solution.py
+++ b/solution.py
@@ -153,12 +153,18 @@
     last = order[-1]
     filtered = {s: project(s, relayed[s][1]) for s in order[:-1]}
     first = order[0]
+    count_is_pow2 = lax.axis_size("tp") & (lax.axis_size("tp") - 1) == 0
     if relayed[last][1] is None:
         early = [s for s in order[:-1]]
         held, tied = lax.optimization_barrier(([filtered[s] for s in early], relayed[last][0]))
         for s, value in zip(early, held):
             filtered[s] = value
-        relayed[last] = (tied, relay(relay_send(tied)))
+        send = relay_send(tied)
+        if local_width % 256 == 0 and count_is_pow2:
+            cut = local_width // 2
+            relayed[last] = (tied, (relay(send[..., :cut]), relay(send[..., cut:])))
+        else:
+            relayed[last] = (tied, relay(send))
     product = filtered[0] * filtered[2]
     blocks = tok_rows // block_rows
     current = product.reshape(blocks, block_rows, local_groups, group_size)
@@ -181,33 +187,59 @@
     starts = lead * incoming[None] + local_starts
     distant = jnp.einsum("gin,bgnc->bigc", entry, starts, precision=highest)
     conv_out = (near + distant).reshape(tok_rows, local_width)
-    late, conv_out = lax.optimization_barrier((relayed[last][1], conv_out))
-    second = project(last, late)
-    gated = (second * conv_out).astype(jnp.bfloat16)
     count = lax.axis_size("tp")
     me_tp = lax.axis_index("tp")
 
-    def contribution(block, source):
-        rows = lax.dynamic_slice_in_dim(w_out, source * local_width, local_width, axis=0)
+    def project_cols(received, lo, hi):
+        got = relayed[last][0][..., lo:hi]
+        acc = jnp.einsum("ktr,krc->tc", mine, got, preferred_element_type=jnp.float32)
+        for (src_grp, part), recv in zip(others, received):
+            local = lax.dynamic_slice_in_dim(w_in[:, last, lo:hi], src_grp * piece, piece, axis=0)
+            acc = acc + jnp.dot(part[0], local, preferred_element_type=jnp.float32)
+            acc = acc + jnp.einsum(
+                "ktr,krc->tc", part[1:], recv, preferred_element_type=jnp.float32
+            )
+        rounded = lax.reduce_precision(acc, exponent_bits=8, mantissa_bits=7)
+        return short_filter(rounded, short_taps[:, last, lo:hi], tok_rows)
+
+    def contribution(block, source, lo):
+        width = block.shape[1]
+        rows = lax.dynamic_slice_in_dim(w_out, source * local_width + lo, width, axis=0)
         return jnp.dot(block, rows, preferred_element_type=jnp.float32)
 
-    if count & (count - 1) == 0:
-        mixed = contribution(gated, me_tp)
-        held = gated[None]
+    def swap_project(gated_part, lo):
+        mixed = contribution(gated_part, me_tp, lo)
+        held = gated_part[None]
         masks = [0]
         bit = count // 2
         while bit >= 1:
             pairs = [(q, q ^ bit) for q in range(count)]
             arrived = lax.ppermute(held, "tp", pairs)
             for q, m in enumerate(masks):
-                mixed = mixed + contribution(arrived[q], jnp.bitwise_xor(me_tp, m ^ bit))
+                mixed = mixed + contribution(arrived[q], jnp.bitwise_xor(me_tp, m ^ bit), lo)
             held = jnp.concatenate([held, arrived], axis=0)
             masks = masks + [m ^ bit for m in masks]
             bit //= 2
+        return mixed
+
+    if isinstance(relayed[last][1], tuple):
+        first_half, second_half = relayed[last][1]
+        cut = local_width // 2
+        late_a, conv_out = lax.optimization_barrier((first_half, conv_out))
+        gated_a = (project_cols(late_a, 0, cut) * conv_out[:, :cut]).astype(jnp.bfloat16)
+        late_b, gated_a = lax.optimization_barrier((second_half, gated_a))
+        gated_b = (project_cols(late_b, cut, local_width) * conv_out[:, cut:]).astype(jnp.bfloat16)
+        mixed = swap_project(gated_a, 0) + swap_project(gated_b, cut)
     else:
-        pieces = gather_by_swaps(gated, "tp")
-        mixed = jnp.einsum("qtc,qcf->tf", pieces, w_out.reshape(pieces.shape[0], local_width, -1),
-                           preferred_element_type=jnp.float32)
+        late, conv_out = lax.optimization_barrier((relayed[last][1], conv_out))
+        second = project(last, late)
+        gated = (second * conv_out).astype(jnp.bfloat16)
+        if count_is_pow2:
+            mixed = swap_project(gated, 0)
+        else:
+            pieces = gather_by_swaps(gated, "tp")
+            mixed = jnp.einsum("qtc,qcf->tf", pieces, w_out.reshape(pieces.shape[0], local_width, -1),
+                               preferred_element_type=jnp.float32)
     return (tokens.astype(jnp.float32) + mixed).astype(jnp.bfloat16)
 
 

time: 221 us -> 236 us (1.068); the launches traced: 216 us -> 236 us
  waiting for transfers between devices: 97.7 us -> 107 us
  local copies, waits for them, and re-layouts: 25.6 us -> 29.4 us
  other arithmetic: 26.3 us -> 29.7 us
    ppermute x3 -> x4, waiting for transfers between devices: 27.9 us -> 44.8 us  [relay(): received.append(lax.ppermute(send, 'grp', pairs))]
    dot_general x0 -> x6, matrix products: none -> 8.21 us  [the longest x2 3.38 us: project_cols(): jnp.einsum('ktr,krc->tc', part[1:], recv, preferred_element_type=jnp.floa...]
    ppermute x3, waiting for transfers between devices: 8.46 us -> 3.32 us  [body(): arrived = lax.ppermute(own_state, 'ctx', pairs)]
    dot_general x3 -> x2, matrix products: 6.64 us -> 3.52 us  [project(): jnp.einsum('ktr,krc->tc', mine, got, preferred_element_type=jnp.float32)]
    add x3, other arithmetic: 0.34 us -> 3.24 us  [advance(): return (step_decay * state + end_block, state)]
    dot_general x3 -> x2, matrix products: 5.46 us -> 2.98 us  [project(): jnp.einsum('ktr,krc->tc', part[1:], recv, preferred_element_type=jnp.floa...]
    dot_general x4 -> x8, matrix products: 5.94 us -> 4.28 us  [contribution(): return jnp.dot(block, rows, preferred_element_type=jnp.float32)]
    ppermute x2 -> x4, waiting for transfers between devices: 8.38 us -> 7.63 us  [swap_project(): arrived = lax.ppermute(held, 'tp', pairs)]
  transfers between devices with their start and end apart: 14 -> 17, of which waited for: 9 -> 11; matrix products, arithmetic and copies ran while one was open for 31% -> 28% of each run, Pallas kernels for 0% -> 0%
where the time goes in v7:
time: 236 us
  waiting for transfers between devices  107 us (45%)
  matrix products  33.7 us (14%)
  other arithmetic  29.7 us (13%)
  local copies, waits for them, and re-layouts  29.4 us (12%)
  starting transfers between devices  22 us (9%)
  between operations  14 us (6%)
    ppermute x4, waiting for transfers between devices, relay(): received.append(lax.ppermute(send, 'grp', pairs))  44.8 us
    all_gather x3, waiting for transfers between devices, body(): got = lax.all_gather(own[:, s, :], 'ctx', axis=0)  36.6 us
    ppermute x2, waiting for transfers between devices, gather_by_swaps(): held = jnp.concatenate([held, lax.ppermute(held, axis, pairs)], axis=0)  13.4 us
    ppermute x4, waiting for transfers between devices, swap_project(): arrived = lax.ppermute(held, 'tp', pairs)  7.63 us
    unnamed x90, local copies, waits for them, and re-layouts  7.59 us
    concatenate x3, other arithmetic, relay_send(): doubled = jnp.concatenate([got, got], axis=0)  7.26 us
    ppermute x3, starting transfers between devices, body(): arrived = lax.ppermute(own_state, 'ctx', pairs)  7.21 us
    dot_general x1, matrix products, body(): square = jnp.einsum('gin,gjn->gij', falling, rising, precision=highest)  5.56 us
  transfers between devices with their start and end apart: 17, of which 11 were waited for; matrix products, arithmetic and copies ran while one was open for 28% of the time, Pallas kernels for 0%

profile of v7, /device:TPU:0, one launch (start us, length us, event | category | flops | bytes accessed | tf_op | source)
XLA Modules:
  0.0 235.6 jit_solution(13714249316630226857)
XLA Ops:
  6.5 2.7 %constant_dynamic-slice_fusion.2 = (bf16[512,1,512]{2,0,1:T(8,128)(2,1)}, bf16[512,1,512]{2,0,1:T(8,128)(2,1)}, bf16[512,1,512]{2,0,1:T(8,128)(2,1)}) fusion(bf16[1024,3,512]{2,0,1:T(8,128)(2,1)} %param.14, s32[]{:T(128)S(6)} %select_n.117, s32[]{:T(128)S(6)} %add.315, s32[]{:T(128)S(6)} %add.314), kind=kLoop, calls=%fused_computation.164 | loop fusion | bytes 3145740 | tf_op jit(solution)/shard_map/slice | solution.py:117
  10.1 3.0 %collective-permute-start = (bf16[1,385,1024]{2,1,0:T(8,128)(2,1)S(1)}, bf16[1,385,1024]{2,1,0:T(8,128)(2,1)S(1)}, u32[]{:S(2)}, u32[]{:S(2)}) collective-permute-start(bf16[1,385,1024]{2,1,0:T(8,128)(2,1)S(1)} %maximum_bitcast_fusion), channel_id=1, source_target_pairs={{0,2},{1,3},{2,0},{3,1},{4,6},{5,7},{6,4},{7,5},{8,10},{9,11},{10,... | collective-permute-start | bytes 2365448 | tf_op jit(solution)/shard_map/ppermute | solution.py:57
  17.6 13.4 %collective-permute-done = bf16[1,385,1024]{2,1,0:T(8,128)(2,1)S(1)} collective-permute-done((bf16[1,385,1024]{2,1,0:T(8,128)(2,1)S(1)}, bf16[1,385,1024]{2,1,0:T(8,128)(2,1)S(1)}, u32[]{:S(2)}, u32[]{:S(2)}) %collective-permute-start) | collective-permute-done | bytes 788512 | tf_op jit(solution)/shard_map/ppermute | solution.py:57
  37.0 5.6 %convolution_select_fusion = f32[32,128,128]{2,1,0:T(8,128)} fusion(pred[128,128]{1,0:T(8,128)(4,1)S(1)} %broadcast_compare_fusion, f32[32,64]{1,0:T(8,128)S(1)} %copy-done.27, f32[128]{0:T(128)S(1)} %iota_convert_fusion.1, f32[32,64]{1,0:T(8,128)S(1)} %get-tuple-element.148, f32[32,64]{1,0:T(8,128)S(1)} %get-tuple-element.147), kind=kOutput, calls=%fused_computation.23 | convolution fusion | flops 403963904 | bytes 2138624 | tf_op jit(solution)/shard_map/gin,gjn->gij/dot_general | solution.py:91
  44.4 2.0 pad_maximum_fusion
  46.4 2.7 %gather_fusion.1 = bf16[4,385,1024]{2,1,0:T(8,128)(2,1)S(1)} fusion(bf16[4,385,1024]{2,1,0:T(8,128)(2,1)} %pad_maximum_fusion, s32[1024]{0:T(1024)S(1)} %pad_clamp_fusion.2), kind=kCustom, calls=%fused_computation.3 | custom fusion | bytes 6307856 | tf_op jit(solution)/shard_map/jit(_take)/gather | solution.py:62
  51.5 4.3 %collective-permute-start.2 = (bf16[2,4096]{1,0:T(2,128)(2,1)S(1)}, bf16[2,4096]{1,0:T(2,128)(2,1)}, u32[]{:S(2)}, u32[]{:S(2)}) collective-permute-start(bf16[2,4096]{1,0:T(2,128)(2,1)S(1)} %pad_maximum_fusion.4), channel_id=1, source_target_pairs={{0,4},{4,8},{8,12},{1,5},{5,9},{9,13},{2,6},{6,10},{10,14},{3,7},{... | collective-permute-start | bytes 49160 | tf_op jit(solution)/shard_map/ppermute | solution.py:12
  56.6 3.3 %maximum_maximum_fusion = bf16[387,4096]{1,0:T(8,128)(2,1)S(1)} fusion(bf16[385,1024]{1,0:T(8,128)(2,1)} %copy-done.2, bf16[385,1024]{1,0:T(8,128)(2,1)} %copy-done.3, bf16[385,1024]{1,0:T(8,128)(2,1)} %copy-done.4, bf16[385,1024]{1,0:T(8,128)(2,1)} %copy-done.1, bf16[2,4096]{1,0:T(2,128)(2,1)} %collective-permute-done.2), kind=kLoop, calls=%fused_computation.18 | loop fusion | flops 15851520 | bytes 6340608 | tf_op jit(solution)/shard_map/concatenate | solution.py:100
  60.0 3.2 %fusion.7 = bf16[3,512,512]{2,1,0:T(8,128)(2,1)} fusion(s32[]{:T(128)S(6)} %select_n.119, bf16[4,512,512]{2,1,0:T(8,128)(2,1)} %bitcast.178), kind=kLoop, calls=%fused_computation.29 | loop fusion | flops 786432 | bytes 3670020 | tf_op jit(solution)/shard_map/concatenate | solution.py:104
  67.8 2.0 gather_fusion.2
  69.7 1.9 gather_fusion.3
  73.2 30.6 %all-gather.9.cloned.1.call-done = bf16[2048,1,512]{2,0,1:T(8,128)(2,1)} async-done(((bf16[512,1,512]{2,0,1:T(8,128)(2,1)}), bf16[2048,1,512]{2,0,1:T(8,128)(2,1)}) %all-gather.9.cloned.1.call-update) | async-done | bytes 2097168 | tf_op jit(solution)/shard_map/all_gather | solution.py:117
  103.8 2.1 fusion.6
  107.5 2.5 %convolution_bitcast_fusion.3 = f32[386,512]{1,0:T(8,128)S(1)} fusion(bf16[4,512,512]{2,1,0:T(8,128)(2,1)S(1)} %bitcast.179, bf16[4,386,512]{2,1,0:T(8,128)(2,1)} %gather_fusion.2, pred[4]{0:T(512)(128)(4,1)S(1)} %copy-done.43), kind=kOutput, calls=%fused_computation.34 | convolution fusion | flops 810291200 | bytes 4468740 | tf_op jit(solution)/shard_map/ktr,krc->tc/dot_general | solution.py:143
  114.4 2.2 fusion.15
  116.9 25.1 %collective-permute-done.4 = bf16[3,512,512]{2,1,0:T(8,128)(2,1)S(1)} collective-permute-done((bf16[3,512,512]{2,1,0:T(8,128)(2,1)S(1)}, bf16[3,512,512]{2,1,0:T(8,128)(2,1)S(1)}, u32[]{:S(2)}, u32[]{:S(2)}) %collective-permute-start.4) | collective-permute-done | bytes 1572896 | tf_op jit(solution)/shard_map/ppermute | solution.py:111
  144.0 5.9 %all-gather.11.cloned.1.call-done = bf16[2048,1,512]{2,0,1:T(8,128)(2,1)} async-done(((bf16[512,1,512]{2,0,1:T(8,128)(2,1)}), bf16[2048,1,512]{2,0,1:T(8,128)(2,1)}) %all-gather.11.cloned.1.call-update) | async-done | bytes 2097168 | tf_op jit(solution)/shard_map/all_gather | solution.py:117
  152.3 1.6 reshape.181
  154.0 3.9 %convolution_bitcast_fusion.4 = f32[3,32,64,16]{2,3,0,1:T(8,128)} fusion(f32[32,64,128]{2,1,0:T(8,128)} %multiply_exponential_fusion, f32[3,128,32,16]{1,0,3,2:T(4,128)S(1)} %reshape.181), kind=kOutput, calls=%fused_computation.39 | convolution fusion | flops 150994944 | bytes 2228224 | tf_op jit(solution)/shard_map/gni,bigc->bgnc/dot_general | solution.py:172
  157.8 5.5 %while.13 = (s32[]{:T(128)}, f32[32,64,16]{1,2,0:T(8,128)S(1)}, f32[3,32,64,16]{2,3,1,0:T(8,128)}, f32[32,64,1]{1,0,2:T(8,128)S(1)}, f32[3,32,64,16]{2,3,0,1:T(8,128)}, /*index=5*/s32[]{:T(128)}, s32[]{:T(128)}) while((s32[]{:T(128)}, f32[32,64,16]{1,2,0:T(8,128)S(1)}, f32[3,32,64,16]{2,3,1,0:T(8,128)}, ...), condition=%wide.region_2.4_spmd.clone, body=%wide.region_1.3_spmd.clone.sunk | while | flops 131075 | bytes 794728 | solution.py:179
  163.3 3.4 %collective-permute-start.9 = (f32[32,64,16]{1,2,0:T(8,128)S(1)}, f32[32,64,16]{1,2,0:T(8,128)S(1)}, u32[]{:S(2)}, u32[]{:S(2)}) collective-permute-start(f32[32,64,16]{1,2,0:T(8,128)S(1)} %get-tuple-element.55), channel_id=1, source_target_pairs={{0,12},{1,13},{2,14},{3,15},{16,28},{17,29},{18,30},{19,31}} | collective-permute-start | bytes 393224 | tf_op jit(solution)/shard_map/ppermute | solution.py:183
  168.1 2.5 %collective-permute-start.7 = (f32[32,64,16]{1,2,0:T(8,128)S(1)}, f32[32,64,16]{1,2,0:T(8,128)S(1)}, u32[]{:S(2)}, u32[]{:S(2)}) collective-permute-start(f32[32,64,16]{1,2,0:T(8,128)S(1)} %get-tuple-element.55), channel_id=1, source_target_pairs={{0,4},{4,8},{8,12},{1,5},{5,9},{9,13},{2,6},{6,10},{10,14},{3,7},{... | collective-permute-start | bytes 393224 | tf_op jit(solution)/shard_map/ppermute | solution.py:183
  170.6 2.0 fusion.5
  172.6 2.2 convolution_bitcast_fusion.7
  180.5 3.3 %collective-permute-done.7 = f32[32,64,16]{1,2,0:T(8,128)S(1)} collective-permute-done((f32[32,64,16]{1,2,0:T(8,128)S(1)}, f32[32,64,16]{1,2,0:T(8,128)S(1)}, u32[]{:S(2)}, u32[]{:S(2)}) %collective-permute-start.7) | collective-permute-done | bytes 131104 | tf_op jit(solution)/shard_map/ppermute | solution.py:183
  185.5 3.4 %fusion.11 = f32[3,128,32,16]{1,3,0,2:T(8,128)S(1)} fusion(f32[32,3,16,128]{3,2,1,0:T(8,128)S(1)} %fusion.22, f32[32,128,128]{2,1,0:T(8,128)S(1)} %copy-done.14, f32[3,128,32,16]{1,0,3,2:T(4,128)S(1)} %reshape.181), kind=kOutput, calls=%fused_computation.38 | convolution fusion | flops 302186496 | bytes 4456448 | tf_op jit(solution)/shard_map/gij,bjgc->bigc/dot_general | solution.py:171
  189.4 7.4 %collective-permute-done.6 = bf16[3,512,256]{2,1,0:T(8,128)(2,1)S(1)} collective-permute-done((bf16[3,512,256]{2,1,0:T(8,128)(2,1)S(1)}, bf16[3,512,256]{2,1,0:T(8,128)(2,1)S(1)}, u32[]{:S(2)}, u32[]{:S(2)}) %collective-permute-start.6) | collective-permute-done | bytes 786464 | tf_op jit(solution)/shard_map/ppermute | solution.py:111
  198.0 1.8 fusion.19
  200.0 12.3 %collective-permute-done.5 = bf16[3,512,256]{2,1,0:T(8,128)(2,1)} collective-permute-done((bf16[3,512,256]{2,1,0:T(8,128)(2,1)}, bf16[3,512,256]{2,1,0:T(8,128)(2,1)}, u32[]{:S(2)}, u32[]{:S(2)}) %collective-permute-start.5) | collective-permute-done | bytes 786464 | tf_op jit(solution)/shard_map/ppermute | solution.py:111
  216.9 4.7 %collective-permute-done.12 = bf16[1,384,256]{2,1,0:T(8,128)(2,1)S(1)} collective-permute-done((bf16[1,384,256]{2,1,0:T(8,128)(2,1)S(1)}, bf16[1,384,256]{2,1,0:T(8,128)(2,1)S(1)}, u32[]{:S(2)}, u32[]{:S(2)}) %collective-permute-start.12) | collective-permute-done | bytes 196640 | tf_op jit(solution)/shard_map/ppermute | solution.py:217
  221.7 2.0 collective-permute-done.10
  227.5 1.6 add_convert_fusion
  (189 shorter events, 57.1 us)
Async XLA Ops:
  6.5 53.4 %all-gather.7.cloned.1.call-start = ((), (), s32[]{:S(2)}) async-start(), calls=%async_computation | async-start | bytes 2621440 | tf_op jit(solution)/shard_map/all_gather | solution.py:117
  9.2 94.6 %all-gather.9.cloned.1.call-start = ((), (), s32[]{:S(2)}) async-start(), calls=%async_computation.1 | async-start | bytes 2621440 | tf_op jit(solution)/shard_map/all_gather | solution.py:117
  9.3 6.4 %copy-start.28 = (f32[3,3,512]{2,1,0:T(4,128)S(1)}, f32[3,3,512]{2,1,0:T(4,128)}, u32[]{:S(2)}) copy-start(f32[3,3,512]{2,1,0:T(4,128)} %param.15) | copy-start | bytes 55300
  9.3 7.7 %copy-start.26 = (f32[32,64]{1,0:T(8,128)S(1)}, f32[32,64]{1,0:T(8,128)}, u32[]{:S(2)}) copy-start(f32[32,64]{1,0:T(8,128)} %param.17) | copy-start | bytes 24580
  9.3 7.7 %copy-start.27 = (f32[32,64]{1,0:T(8,128)S(1)}, f32[32,64]{1,0:T(8,128)}, u32[]{:S(2)}) copy-start(f32[32,64]{1,0:T(8,128)} %param.16) | copy-start | bytes 24580
  10.0 139.9 %all-gather.11.cloned.1.call-start = ((), (), s32[]{:S(2)}) async-start(), calls=%async_computation.2 | async-start | bytes 2621440 | tf_op jit(solution)/shard_map/all_gather | solution.py:117
  10.1 20.9 %collective-permute-start = (bf16[1,385,1024]{2,1,0:T(8,128)(2,1)S(1)}, bf16[1,385,1024]{2,1,0:T(8,128)(2,1)S(1)}, u32[]{:S(2)}, u32[]{:S(2)}) collective-permute-start(bf16[1,385,1024]{2,1,0:T(8,128)(2,1)S(1)} %maximum_bitcast_fusion), channel_id=1, source_target_pairs={{0,2},{1,3},{2,0},{3,1},{4,6},{5,7},{6,4},{7,5},{8,10},{9,11},{10,... | collective-permute-start | bytes 2365448 | tf_op jit(solution)/shard_map/ppermute | solution.py:57
  31.2 4.7 %copy-start.5 = (bf16[1024,3,512]{2,0,1:T(8,128)(2,1)S(1)}, bf16[1024,3,512]{2,0,1:T(8,128)(2,1)}, u32[]{:S(2)}) copy-start(bf16[1024,3,512]{2,0,1:T(8,128)(2,1)} %param.14) | copy-start | bytes 9437188
  32.8 11.2 %collective-permute-start.1 = (bf16[2,385,1024]{2,0,1:T(2,128)(2,1)S(1)}, bf16[2,385,1024]{2,0,1:T(2,128)(2,1)S(1)}, u32[]{:S(2)}, u32[]{:S(2)}) collective-permute-start(bf16[2,385,1024]{2,0,1:T(2,128)(2,1)S(1)} %copy.43), channel_id=1, source_target_pairs={{0,1},{1,0},{2,3},{3,2},{4,5},{5,4},{6,7},{7,6},{8,9},{9,8},{10,11... | collective-permute-start | bytes 4730888 | tf_op jit(solution)/shard_map/ppermute | solution.py:57
  51.5 5.1 %collective-permute-start.2 = (bf16[2,4096]{1,0:T(2,128)(2,1)S(1)}, bf16[2,4096]{1,0:T(2,128)(2,1)}, u32[]{:S(2)}, u32[]{:S(2)}) collective-permute-start(bf16[2,4096]{1,0:T(2,128)(2,1)S(1)} %pad_maximum_fusion.4), channel_id=1, source_target_pairs={{0,4},{4,8},{8,12},{1,5},{5,9},{9,13},{2,6},{6,10},{10,14},{3,7},{... | collective-permute-start | bytes 49160 | tf_op jit(solution)/shard_map/ppermute | solution.py:12
  71.7 42.7 %collective-permute-start.3 = (bf16[3,512,512]{2,1,0:T(8,128)(2,1)}, bf16[3,512,512]{2,1,0:T(8,128)(2,1)}, u32[]{:S(2)}, u32[]{:S(2)}) collective-permute-start(bf16[3,512,512]{2,1,0:T(8,128)(2,1)} %fusion.7), channel_id=1, source_target_pairs={{0,16},{16,0},{1,17},{17,1},{2,18},{18,2},{3,19},{19,3},{4,20},{20... | collective-permute-start | bytes 4718600 | tf_op jit(solution)/shard_map/ppermute | solution.py:111
  106.0 36.0 %collective-permute-start.4 = (bf16[3,512,512]{2,1,0:T(8,128)(2,1)S(1)}, bf16[3,512,512]{2,1,0:T(8,128)(2,1)S(1)}, u32[]{:S(2)}, u32[]{:S(2)}) collective-permute-start(bf16[3,512,512]{2,1,0:T(8,128)(2,1)S(1)} %fusion.6), channel_id=1, source_target_pairs={{0,16},{16,0},{1,17},{17,1},{2,18},{18,2},{3,19},{19,3},{4,20},{20... | collective-permute-start | bytes 4718600 | tf_op jit(solution)/shard_map/ppermute | solution.py:111
  116.9 25.9 %copy-start.29 = (f32[1,1,512]{2,1,0:T(1,128)S(1)}, f32[1,1,512]{2,1,0:T(1,128)}, u32[]{:S(2)}) copy-start(f32[1,1,512]{2,1,0:T(1,128)} %get-tuple-element.136) | copy-start | bytes 6148
  116.9 25.9 %copy-start.30 = (f32[1,1,512]{2,1,0:T(1,128)S(1)}, f32[1,1,512]{2,1,0:T(1,128)}, u32[]{:S(2)}) copy-start(f32[1,1,512]{2,1,0:T(1,128)} %get-tuple-element.137) | copy-start | bytes 6148
  116.9 25.9 %copy-start.31 = (f32[1,1,512]{2,1,0:T(1,128)S(1)}, f32[1,1,512]{2,1,0:T(1,128)}, u32[]{:S(2)}) copy-start(f32[1,1,512]{2,1,0:T(1,128)} %get-tuple-element.138) | copy-start | bytes 6148
  163.3 9.2 %copy-start.13 = (bf16[2048,1,512]{2,0,1:T(8,128)(2,1)S(1)}, bf16[2048,1,512]{2,0,1:T(8,128)(2,1)}, u32[]{:S(2)}) copy-start(bf16[2048,1,512]{2,0,1:T(8,128)(2,1)} %all-gather.11.cloned.1.call-done) | copy-start | bytes 6291460
  163.3 17.2 %collective-permute-start.9 = (f32[32,64,16]{1,2,0:T(8,128)S(1)}, f32[32,64,16]{1,2,0:T(8,128)S(1)}, u32[]{:S(2)}, u32[]{:S(2)}) collective-permute-start(f32[32,64,16]{1,2,0:T(8,128)S(1)} %get-tuple-element.55), channel_id=1, source_target_pairs={{0,12},{1,13},{2,14},{3,15},{16,28},{17,29},{18,30},{19,31}} | collective-permute-start | bytes 393224 | tf_op jit(solution)/shard_map/ppermute | solution.py:183
  166.8 13.7 %collective-permute-start.8 = (f32[32,64,16]{1,2,0:T(8,128)S(1)}, f32[32,64,16]{1,2,0:T(8,128)S(1)}, u32[]{:S(2)}, u32[]{:S(2)}) collective-permute-start(f32[32,64,16]{1,2,0:T(8,128)S(1)} %get-tuple-element.55), channel_id=1, source_target_pairs={{0,8},{4,12},{1,9},{5,13},{2,10},{6,14},{3,11},{7,15},{16,24},{20,... | collective-permute-start | bytes 393224 | tf_op jit(solution)/shard_map/ppermute | solution.py:183
  168.1 15.7 %collective-permute-start.7 = (f32[32,64,16]{1,2,0:T(8,128)S(1)}, f32[32,64,16]{1,2,0:T(8,128)S(1)}, u32[]{:S(2)}, u32[]{:S(2)}) collective-permute-start(f32[32,64,16]{1,2,0:T(8,128)S(1)} %get-tuple-element.55), channel_id=1, source_target_pairs={{0,4},{4,8},{8,12},{1,5},{5,9},{9,13},{2,6},{6,10},{10,14},{3,7},{... | collective-permute-start | bytes 393224 | tf_op jit(solution)/shard_map/ppermute | solution.py:183
  176.4 7.4 %copy-start.24 = (f32[32,64]{1,0:T(8,128)S(1)}, f32[32,64]{1,0:T(8,128)}, u32[]{:S(2)}) copy-start(f32[32,64]{1,0:T(8,128)} %get-tuple-element.144) | copy-start | bytes 24580
  176.4 7.4 %copy-start.25 = (f32[32,64]{1,0:T(8,128)S(1)}, f32[32,64]{1,0:T(8,128)}, u32[]{:S(2)}) copy-start(f32[32,64]{1,0:T(8,128)} %get-tuple-element.145) | copy-start | bytes 24580
  176.4 20.4 %collective-permute-start.6 = (bf16[3,512,256]{2,1,0:T(8,128)(2,1)S(1)}, bf16[3,512,256]{2,1,0:T(8,128)(2,1)S(1)}, u32[]{:S(2)}, u32[]{:S(2)}) collective-permute-start(bf16[3,512,256]{2,1,0:T(8,128)(2,1)S(1)} %get-tuple-element.129), channel_id=1, source_target_pairs={{0,16},{16,0},{1,17},{17,1},{2,18},{18,2},{3,19},{19,3},{4,20},{20... | collective-permute-start | bytes 2359304 | tf_op jit(solution)/shard_map/ppermute | solution.py:111
  177.6 34.6 %collective-permute-start.5 = (bf16[3,512,256]{2,1,0:T(8,128)(2,1)}, bf16[3,512,256]{2,1,0:T(8,128)(2,1)}, u32[]{:S(2)}, u32[]{:S(2)}) collective-permute-start(bf16[3,512,256]{2,1,0:T(8,128)(2,1)} %get-tuple-element.128), channel_id=1, source_target_pairs={{0,16},{16,0},{1,17},{17,1},{2,18},{18,2},{3,19},{19,3},{4,20},{20... | collective-permute-start | bytes 2359304 | tf_op jit(solution)/shard_map/ppermute | solution.py:111
  198.0 14.3 %copy-start.19 = (f32[386,256]{1,0:T(8,128)S(1)}, f32[386,256]{1,0:T(8,128)}, u32[]{:S(2)}) copy-start(f32[386,256]{1,0:T(8,128)} %convolution_add_fusion.2) | copy-start | bytes 1185796
  199.8 14.1 %copy-start.35 = (f32[1,1,256]{2,1,0:T(1,128)S(1)}, f32[1,1,256]{2,1,0:T(1,128)}, u32[]{:S(2)}) copy-start(f32[1,1,256]{2,1,0:T(1,128)} %get-tuple-element.130) | copy-start | bytes 3076
  199.8 14.1 %copy-start.36 = (f32[1,1,256]{2,1,0:T(1,128)S(1)}, f32[1,1,256]{2,1,0:T(1,128)}, u32[]{:S(2)}) copy-start(f32[1,1,256]{2,1,0:T(1,128)} %get-tuple-element.134) | copy-start | bytes 3076
  199.8 14.1 %copy-start.37 = (f32[1,1,256]{2,1,0:T(1,128)S(1)}, f32[1,1,256]{2,1,0:T(1,128)}, u32[]{:S(2)}) copy-start(f32[1,1,256]{2,1,0:T(1,128)} %get-tuple-element.135) | copy-start | bytes 3076
  200.0 16.2 %copy-start.7 = (bf16[2048,1024]{1,0:T(8,128)(2,1)S(1)}, bf16[2048,1024]{1,0:T(8,128)(2,1)}, u32[]{:S(2)}) copy-start(bf16[2048,1024]{1,0:T(8,128)(2,1)} %param.18) | copy-start | bytes 12582916
  214.1 7.6 %collective-permute-start.12 = (bf16[1,384,256]{2,1,0:T(8,128)(2,1)S(1)}, bf16[1,384,256]{2,1,0:T(8,128)(2,1)S(1)}, u32[]{:S(2)}, u32[]{:S(2)}) collective-permute-start(bf16[1,384,256]{2,1,0:T(8,128)(2,1)S(1)} %bitcast.184), channel_id=1, source_target_pairs={{0,2},{1,3},{2,0},{3,1},{4,6},{5,7},{6,4},{7,5},{8,10},{9,11},{10,... | collective-permute-start | bytes 589832 | tf_op jit(solution)/shard_map/ppermute | solution.py:217
  215.3 8.4 %collective-permute-start.10 = (bf16[1,384,256]{2,1,0:T(8,128)(2,1)S(1)}, bf16[1,384,256]{2,1,0:T(8,128)(2,1)S(1)}, u32[]{:S(2)}, u32[]{:S(2)}) collective-permute-start(bf16[1,384,256]{2,1,0:T(8,128)(2,1)S(1)} %bitcast.182), channel_id=1, source_target_pairs={{0,2},{1,3},{2,0},{3,1},{4,6},{5,7},{6,4},{7,5},{8,10},{9,11},{10,... | collective-permute-start | bytes 589832 | tf_op jit(solution)/shard_map/ppermute | solution.py:217
  221.7 4.7 %collective-permute-start.13 = (bf16[2,384,256]{2,1,0:T(8,128)(2,1)S(1)}, bf16[2,384,256]{2,1,0:T(8,128)(2,1)S(1)}, u32[]{:S(2)}, u32[]{:S(2)}) collective-permute-start(bf16[2,384,256]{2,1,0:T(8,128)(2,1)S(1)} %pad_maximum_fusion.3), channel_id=1, source_target_pairs={{0,1},{1,0},{2,3},{3,2},{4,5},{5,4},{6,7},{7,6},{8,9},{9,8},{10,11... | collective-permute-start | bytes 1179656 | tf_op jit(solution)/shard_map/ppermute | solution.py:217
  223.8 1.8 collective-permute-start.11
  (29 other events, 72.6 us)
Sparse Core Ops, SparseCore 0:
  9.3 48.3 all-gather.6
  59.3 44.4 all-gather.8
  105.4 44.4 all-gather.10

commit v8 on v6

--- a/solution.py
+++ b/solution.py
@@ -101,8 +101,8 @@
     own = lax.dynamic_slice_in_dim(w_in, me_grp * piece, piece, axis=0)
 
     def relay_send(got):
-        doubled = jnp.concatenate([got, got], axis=0)
-        return lax.dynamic_slice_in_dim(doubled, me_ctx + 1, n_ctx - 1, axis=0)
+        picks = (me_ctx + 1 + jnp.arange(n_ctx - 1, dtype=jnp.int32)) % n_ctx
+        return jnp.take(got, picks, axis=0)
 
     def relay(send):
         received = []

time: 221 us -> 258 us (1.17); the launches traced: 216 us -> 257 us
  waiting for transfers between devices: 97.7 us -> 133 us
  local copies, waits for them, and re-layouts: 25.6 us -> 34.3 us
    ppermute x3, waiting for transfers between devices: 27.9 us -> 65.7 us  [relay(): received.append(lax.ppermute(send, 'grp', pairs))]
    gather x0 -> x3, local copies, waits for them, and re-layouts: none -> 9.53 us  [relay_send(): return jnp.take(got, picks, axis=0)]
    concatenate x3 -> x0, other arithmetic: 8.49 us -> none  [relay_send(): doubled = jnp.concatenate([got, got], axis=0)]
    select_n x0 -> x3, other arithmetic: none -> 5.38 us  [relay_send(): return jnp.take(got, picks, axis=0)]
    ppermute x3, waiting for transfers between devices: 8.46 us -> 5.15 us  [body(): arrived = lax.ppermute(own_state, 'ctx', pairs)]
    all_gather x3, waiting for transfers between devices: 37.3 us -> 40.2 us  [body(): got = lax.all_gather(own[:, s, :], 'ctx', axis=0)]
  transfers between devices with their start and end apart: 14 -> 14, of which waited for: 9 -> 9; matrix products, arithmetic and copies ran while one was open for 31% -> 28% of each run, Pallas kernels for 0% -> 0%
where the time goes in v8:
time: 258 us; the launch traced here: 257 us
  waiting for transfers between devices  133 us (52%)
  local copies, waits for them, and re-layouts  34.3 us (13%)
  matrix products  31.2 us (12%)
  other arithmetic  24.3 us (9%)
  starting transfers between devices  20.2 us (8%)
  between operations  14 us (5%)
    ppermute x3, waiting for transfers between devices, relay(): received.append(lax.ppermute(send, 'grp', pairs))  65.7 us
    all_gather x3, waiting for transfers between devices, body(): got = lax.all_gather(own[:, s, :], 'ctx', axis=0)  40.2 us
    ppermute x2, waiting for transfers between devices, gather_by_swaps(): held = jnp.concatenate([held, lax.ppermute(held, axis, pairs)], axis=0)  13.4 us
    gather x3, local copies, waits for them, and re-layouts, relay_send(): return jnp.take(got, picks, axis=0)  9.53 us
    ppermute x3, starting transfers between devices, body(): arrived = lax.ppermute(own_state, 'ctx', pairs)  7.6 us
    ppermute x2, waiting for transfers between devices, body(): arrived = lax.ppermute(held, 'tp', pairs)  7.53 us
    dot_general x3, matrix products, project(): jnp.einsum('ktr,krc->tc', mine, got, preferred_element_type=jnp.float32)  7.32 us
    unnamed x82, local copies, waits for them, and re-layouts  6.75 us
  transfers between devices with their start and end apart: 14, of which 9 were waited for; matrix products, arithmetic and copies ran while one was open for 28% of the time, Pallas kernels for 0%

profile of v8, /device:TPU:0, one launch (start us, length us, event | category | flops | bytes accessed | tf_op | source)
XLA Modules:
  0.0 257.1 jit_solution(10757829321129062605)
XLA Ops:
  6.5 2.6 %constant_dynamic-slice_fusion.2 = (bf16[512,1,512]{2,0,1:T(8,128)(2,1)}, bf16[512,1,512]{2,0,1:T(8,128)(2,1)}, bf16[512,1,512]{2,0,1:T(8,128)(2,1)}) fusion(bf16[1024,3,512]{2,0,1:T(8,128)(2,1)} %param.16, s32[]{:T(128)S(6)} %select_n.116, s32[]{:T(128)S(6)} %add.265, s32[]{:T(128)S(6)} %add.264), kind=kLoop, calls=%fused_computation.140 | loop fusion | bytes 3145740 | tf_op jit(solution)/shard_map/slice | solution.py:117
  10.1 3.0 %collective-permute-start = (bf16[1,385,1024]{2,1,0:T(8,128)(2,1)S(1)}, bf16[1,385,1024]{2,1,0:T(8,128)(2,1)S(1)}, u32[]{:S(2)}, u32[]{:S(2)}) collective-permute-start(bf16[1,385,1024]{2,1,0:T(8,128)(2,1)S(1)} %maximum_bitcast_fusion), channel_id=1, source_target_pairs={{0,2},{1,3},{2,0},{3,1},{4,6},{5,7},{6,4},{7,5},{8,10},{9,11},{10,... | collective-permute-start | bytes 2365448 | tf_op jit(solution)/shard_map/ppermute | solution.py:57
  17.6 13.4 %collective-permute-done = bf16[1,385,1024]{2,1,0:T(8,128)(2,1)S(1)} collective-permute-done((bf16[1,385,1024]{2,1,0:T(8,128)(2,1)S(1)}, bf16[1,385,1024]{2,1,0:T(8,128)(2,1)S(1)}, u32[]{:S(2)}, u32[]{:S(2)}) %collective-permute-start) | collective-permute-done | bytes 788512 | tf_op jit(solution)/shard_map/ppermute | solution.py:57
  31.2 1.6 copy.40
  36.6 5.6 %convolution_select_fusion = f32[32,128,128]{2,1,0:T(8,128)} fusion(pred[128,128]{1,0:T(8,128)(4,1)S(1)} %broadcast_compare_fusion, f32[32,64]{1,0:T(8,128)S(1)} %copy-done.25, f32[128]{0:T(128)S(1)} %iota_convert_fusion.1, f32[32,64]{1,0:T(8,128)S(1)} %get-tuple-element.139, f32[32,64]{1,0:T(8,128)S(1)} %get-tuple-element.138), kind=kOutput, calls=%fused_computation.20 | convolution fusion | flops 403963904 | bytes 2138624 | tf_op jit(solution)/shard_map/gin,gjn->gij/dot_general | solution.py:91
  42.2 1.7 fusion.70
  44.3 2.0 pad_maximum_fusion
  46.3 2.7 %gather_fusion.1 = bf16[4,385,1024]{2,1,0:T(8,128)(2,1)S(1)} fusion(bf16[4,385,1024]{2,1,0:T(8,128)(2,1)} %pad_maximum_fusion, s32[1024]{0:T(1024)S(1)} %pad_clamp_fusion.2), kind=kCustom, calls=%fused_computation.6 | custom fusion | bytes 6307856 | tf_op jit(solution)/shard_map/jit(_take)/gather | solution.py:62
  51.4 4.3 %collective-permute-start.2 = (bf16[2,4096]{1,0:T(2,128)(2,1)S(1)}, bf16[2,4096]{1,0:T(2,128)(2,1)}, u32[]{:S(2)}, u32[]{:S(2)}) collective-permute-start(bf16[2,4096]{1,0:T(2,128)(2,1)S(1)} %pad_maximum_fusion.3), channel_id=1, source_target_pairs={{0,4},{4,8},{8,12},{1,5},{5,9},{9,13},{2,6},{6,10},{10,14},{3,7},{... | collective-permute-start | bytes 49160 | tf_op jit(solution)/shard_map/ppermute | solution.py:12
  56.5 3.5 %maximum_maximum_fusion = bf16[387,4096]{1,0:T(8,128)(2,1)S(1)} fusion(bf16[385,1024]{1,0:T(8,128)(2,1)} %copy-done.2, bf16[385,1024]{1,0:T(8,128)(2,1)} %copy-done.3, bf16[385,1024]{1,0:T(8,128)(2,1)} %copy-done.4, bf16[385,1024]{1,0:T(8,128)(2,1)} %copy-done.1, bf16[2,4096]{1,0:T(2,128)(2,1)} %collective-permute-done.2), kind=kLoop, calls=%fused_computation.15 | loop fusion | flops 15851520 | bytes 6340608 | tf_op jit(solution)/shard_map/concatenate | solution.py:100
  60.1 3.6 %gather_fusion.2 = bf16[3,512,512]{2,1,0:T(8,128)(2,1)} fusion(bf16[4,512,512]{2,1,0:T(8,128)(2,1)} %bitcast.152, s32[1024]{0:T(1024)} %pad_clamp_fusion.4), kind=kCustom, calls=%fused_computation.clone | custom fusion | bytes 3145740 | tf_op jit(solution)/shard_map/jit(_take)/gather | solution.py:105
  63.7 40.1 %all-gather.9.cloned.1.call-done = bf16[2048,1,512]{2,0,1:T(8,128)(2,1)} async-done(((bf16[512,1,512]{2,0,1:T(8,128)(2,1)}), bf16[2048,1,512]{2,0,1:T(8,128)(2,1)}) %all-gather.9.cloned.1.call-update) | async-done | bytes 2097168 | tf_op jit(solution)/shard_map/all_gather | solution.py:117
  103.8 3.6 %gather_fusion.5 = bf16[3,512,512]{2,1,0:T(8,128)(2,1)} fusion(bf16[4,512,512]{2,1,0:T(8,128)(2,1)} %bitcast.154, s32[1024]{0:T(1024)} %pad_clamp_fusion.4), kind=kCustom, calls=%fused_computation.2.clone | custom fusion | bytes 3145740 | tf_op jit(solution)/shard_map/jit(_take)/gather | solution.py:105
  107.4 3.9 %broadcast_select_fusion.4 = (bf16[3,512,512]{2,1,0:T(8,128)(2,1)}, bf16[3,512,512]{2,1,0:T(8,128)(2,1)}) fusion(bf16[3,512,512]{2,1,0:T(8,128)(2,1)} %gather_fusion.5, pred[3]{0:T(512)(128)(4,1)} %compare_and_fusion.2, bf16[3,512,512]{2,1,0:T(8,128)(2,1)} %gather_fusion.2), kind=kLoop, calls=%fused_computation.26 | loop fusion | flops 1572864 | bytes 6291459 | tf_op jit(solution)/shard_map/jit(_take)/select_n | solution.py:105
  115.9 2.0 gather_fusion.3
  117.9 1.9 gather_fusion.4
  121.8 3.1 %convolution_bitcast_fusion.4 = f32[386,512]{1,0:T(8,128)S(1)} fusion(bf16[4,512,512]{2,1,0:T(8,128)(2,1)} %bitcast.155, bf16[4,386,512]{2,1,0:T(8,128)(2,1)} %gather_fusion.3, pred[4]{0:T(512)(128)(4,1)} %compare_and_fusion.1), kind=kOutput, calls=%fused_computation.32 | convolution fusion | flops 810291200 | bytes 4468740 | tf_op jit(solution)/shard_map/ktr,krc->tc/dot_general | solution.py:143
  129.7 27.6 %collective-permute-done.4 = bf16[3,512,512]{2,1,0:T(8,128)(2,1)S(1)} collective-permute-done((bf16[3,512,512]{2,1,0:T(8,128)(2,1)}, bf16[3,512,512]{2,1,0:T(8,128)(2,1)S(1)}, u32[]{:S(2)}, u32[]{:S(2)}) %collective-permute-start.4) | collective-permute-done | bytes 1572896 | tf_op jit(solution)/shard_map/ppermute | solution.py:111
  158.4 31.3 %collective-permute-done.3 = bf16[3,512,512]{2,1,0:T(8,128)(2,1)S(1)} collective-permute-done((bf16[3,512,512]{2,1,0:T(8,128)(2,1)}, bf16[3,512,512]{2,1,0:T(8,128)(2,1)S(1)}, u32[]{:S(2)}, u32[]{:S(2)}) %collective-permute-start.3) | collective-permute-done | bytes 1572896 | tf_op jit(solution)/shard_map/ppermute | solution.py:111
  191.6 2.4 gather_fusion.6
  196.8 1.8 convolution_bitcast_fusion.6
  198.6 2.6 %while.13 = (s32[]{:T(128)}, f32[32,64,16]{1,2,0:T(8,128)S(1)}, f32[3,32,64,16]{2,3,1,0:T(8,128)}, f32[32,64,1]{1,0,2:T(8,128)S(1)}, f32[3,32,64,16]{2,3,0,1:T(8,128)S(1)}, /*index=5*/s32[]{:T(128)}, s32[]{:T(128)}) while((s32[]{:T(128)}, f32[32,64,16]{1,2,0:T(8,128)S(1)}, f32[3,32,64,16]{2,3,1,0:T(8,128)}, ...), condition=%wide.region_2.5_spmd.clone, body=%wide.region_1.4_spmd.clone.sunk | while | flops 131075 | bytes 795228 | solution.py:173
  201.2 2.0 collective-permute-start.6
  203.2 4.1 %collective-permute-start.7 = (f32[32,64,16]{1,2,0:T(8,128)S(1)}, f32[32,64,16]{1,2,0:T(8,128)S(1)}, u32[]{:S(2)}, u32[]{:S(2)}) collective-permute-start(f32[32,64,16]{1,2,0:T(8,128)S(1)} %get-tuple-element.54), channel_id=1, source_target_pairs={{0,8},{4,12},{1,9},{5,13},{2,10},{6,14},{3,11},{7,15},{16,24},{20,... | collective-permute-start | bytes 393224 | tf_op jit(solution)/shard_map/ppermute | solution.py:177
  208.8 3.1 %convolution_bitcast_fusion.3 = f32[386,512]{1,0:T(8,128)S(1)} fusion(bf16[4,512,512]{2,1,0:T(8,128)(2,1)} %bitcast.151, bf16[4,386,512]{2,1,0:T(8,128)(2,1)} %gather_fusion.3, pred[4]{0:T(512)(128)(4,1)S(1)} %copy-done.39), kind=kOutput, calls=%fused_computation.31 | convolution fusion | flops 810291200 | bytes 4468740 | tf_op jit(solution)/shard_map/ktr,krc->tc/dot_general | solution.py:143
  214.1 4.4 %collective-permute-done.8 = f32[32,64,16]{1,2,0:T(8,128)S(1)} collective-permute-done((f32[32,64,16]{1,2,0:T(8,128)S(1)}, f32[32,64,16]{1,2,0:T(8,128)S(1)}, u32[]{:S(2)}, u32[]{:S(2)}) %collective-permute-start.8) | collective-permute-done | bytes 131104 | tf_op jit(solution)/shard_map/ppermute | solution.py:177
  220.1 3.4 %fusion.8 = f32[3,128,32,16]{1,3,0,2:T(8,128)S(1)} fusion(f32[32,3,16,128]{3,2,1,0:T(8,128)S(1)} %fusion.17, f32[32,128,128]{2,1,0:T(8,128)S(1)} %copy-done.18, f32[3,128,32,16]{1,0,3,2:T(4,128)S(1)} %reshape.179), kind=kOutput, calls=%fused_computation.38 | convolution fusion | flops 302186496 | bytes 4456448 | tf_op jit(solution)/shard_map/gij,bjgc->bigc/dot_general | solution.py:165
  224.0 6.8 %collective-permute-done.5 = bf16[3,512,512]{2,1,0:T(8,128)(2,1)} collective-permute-done((bf16[3,512,512]{2,1,0:T(8,128)(2,1)}, bf16[3,512,512]{2,1,0:T(8,128)(2,1)}, u32[]{:S(2)}, u32[]{:S(2)}) %collective-permute-start.5) | collective-permute-done | bytes 1572896 | tf_op jit(solution)/shard_map/ppermute | solution.py:111
  232.0 2.5 fusion.16
  236.3 7.5 %collective-permute-done.9 = bf16[1,384,512]{2,1,0:T(8,128)(2,1)S(1)} collective-permute-done((bf16[1,384,512]{2,1,0:T(8,128)(2,1)S(1)}, bf16[1,384,512]{2,1,0:T(8,128)(2,1)S(1)}, u32[]{:S(2)}, u32[]{:S(2)}) %collective-permute-start.9) | collective-permute-done | bytes 393248 | tf_op jit(solution)/shard_map/ppermute | solution.py:201
  244.0 1.9 fusion.28
  246.0 1.8 fusion.26
  (168 shorter events, 43.8 us)
Async XLA Ops:
  6.5 53.5 %all-gather.7.cloned.1.call-start = ((), (), s32[]{:S(2)}) async-start(), calls=%async_computation | async-start | bytes 2621440 | tf_op jit(solution)/shard_map/all_gather | solution.py:117
  9.2 4.1 %copy-start = (s32[4]{0:T(128)S(1)}, s32[4]{0:T(128)}, u32[]{:S(2)}) copy-start(s32[4]{0:T(128)} %constant.151.clone) | copy-start | bytes 52
  9.2 94.6 %all-gather.9.cloned.1.call-start = ((), (), s32[]{:S(2)}) async-start(), calls=%async_computation.1 | async-start | bytes 2621440 | tf_op jit(solution)/shard_map/all_gather | solution.py:117
  9.2 7.7 %copy-start.26 = (f32[3,3,512]{2,1,0:T(4,128)S(1)}, f32[3,3,512]{2,1,0:T(4,128)}, u32[]{:S(2)}) copy-start(f32[3,3,512]{2,1,0:T(4,128)} %param.17) | copy-start | bytes 55300
  9.9 180.8 %all-gather.11.cloned.1.call-start = ((), (), s32[]{:S(2)}) async-start(), calls=%async_computation.2 | async-start | bytes 2621440 | tf_op jit(solution)/shard_map/all_gather | solution.py:117
  10.1 20.9 %collective-permute-start = (bf16[1,385,1024]{2,1,0:T(8,128)(2,1)S(1)}, bf16[1,385,1024]{2,1,0:T(8,128)(2,1)S(1)}, u32[]{:S(2)}, u32[]{:S(2)}) collective-permute-start(bf16[1,385,1024]{2,1,0:T(8,128)(2,1)S(1)} %maximum_bitcast_fusion), channel_id=1, source_target_pairs={{0,2},{1,3},{2,0},{3,1},{4,6},{5,7},{6,4},{7,5},{8,10},{9,11},{10,... | collective-permute-start | bytes 2365448 | tf_op jit(solution)/shard_map/ppermute | solution.py:57
  32.8 11.1 %collective-permute-start.1 = (bf16[2,385,1024]{2,0,1:T(2,128)(2,1)S(1)}, bf16[2,385,1024]{2,0,1:T(2,128)(2,1)S(1)}, u32[]{:S(2)}, u32[]{:S(2)}) collective-permute-start(bf16[2,385,1024]{2,0,1:T(2,128)(2,1)S(1)} %copy.40), channel_id=1, source_target_pairs={{0,1},{1,0},{2,3},{3,2},{4,5},{5,4},{6,7},{7,6},{8,9},{9,8},{10,11... | collective-permute-start | bytes 4730888 | tf_op jit(solution)/shard_map/ppermute | solution.py:57
  35.0 7.2 %copy-start.5 = (bf16[1024,3,512]{2,0,1:T(8,128)(2,1)S(1)}, bf16[1024,3,512]{2,0,1:T(8,128)(2,1)}, u32[]{:S(2)}) copy-start(bf16[1024,3,512]{2,0,1:T(8,128)(2,1)} %param.16) | copy-start | bytes 9437188
  51.4 5.1 %collective-permute-start.2 = (bf16[2,4096]{1,0:T(2,128)(2,1)S(1)}, bf16[2,4096]{1,0:T(2,128)(2,1)}, u32[]{:S(2)}, u32[]{:S(2)}) collective-permute-start(bf16[2,4096]{1,0:T(2,128)(2,1)S(1)} %pad_maximum_fusion.3), channel_id=1, source_target_pairs={{0,4},{4,8},{8,12},{1,5},{5,9},{9,13},{2,6},{6,10},{10,14},{3,7},{... | collective-permute-start | bytes 49160 | tf_op jit(solution)/shard_map/ppermute | solution.py:12
  119.8 5.2 %copy-start.6 = (bf16[4,386,512]{2,1,0:T(8,128)(2,1)S(1)}, bf16[4,386,512]{2,1,0:T(8,128)(2,1)}, u32[]{:S(2)}) copy-start(bf16[4,386,512]{2,1,0:T(8,128)(2,1)} %gather_fusion.4) | copy-start | bytes 4743172
  119.8 5.2 %copy-start.38 = (pred[4]{0:T(512)(128)(4,1)S(1)}, pred[4]{0:T(512)(128)(4,1)}, u32[]{:S(2)}) copy-start(pred[4]{0:T(512)(128)(4,1)} %get-tuple-element.112) | copy-start | bytes 16
  119.8 37.5 %collective-permute-start.4 = (bf16[3,512,512]{2,1,0:T(8,128)(2,1)}, bf16[3,512,512]{2,1,0:T(8,128)(2,1)S(1)}, u32[]{:S(2)}, u32[]{:S(2)}) collective-permute-start(bf16[3,512,512]{2,1,0:T(8,128)(2,1)} %get-tuple-element.140), channel_id=1, source_target_pairs={{0,16},{16,0},{1,17},{17,1},{2,18},{18,2},{3,19},{19,3},{4,20},{20... | collective-permute-start | bytes 4718600 | tf_op jit(solution)/shard_map/ppermute | solution.py:111
  121.3 68.4 %collective-permute-start.3 = (bf16[3,512,512]{2,1,0:T(8,128)(2,1)}, bf16[3,512,512]{2,1,0:T(8,128)(2,1)S(1)}, u32[]{:S(2)}, u32[]{:S(2)}) collective-permute-start(bf16[3,512,512]{2,1,0:T(8,128)(2,1)} %get-tuple-element.48), channel_id=1, source_target_pairs={{0,16},{16,0},{1,17},{17,1},{2,18},{18,2},{3,19},{19,3},{4,20},{20... | collective-permute-start | bytes 4718600 | tf_op jit(solution)/shard_map/ppermute | solution.py:111
  125.2 64.5 %copy-start.7 = (bf16[4,386,512]{2,1,0:T(8,128)(2,1)}, bf16[4,386,512]{2,1,0:T(8,128)(2,1)S(1)}, u32[]{:S(2)}) copy-start(bf16[4,386,512]{2,1,0:T(8,128)(2,1)S(1)} %broadcast_select_fusion.1) | copy-start | bytes 4743172
  129.6 28.5 %copy-start.33 = (f32[1,1,512]{2,1,0:T(1,128)S(1)}, f32[1,1,512]{2,1,0:T(1,128)}, u32[]{:S(2)}) copy-start(f32[1,1,512]{2,1,0:T(1,128)} %get-tuple-element.125) | copy-start | bytes 6148
  129.6 28.5 %copy-start.34 = (f32[1,1,512]{2,1,0:T(1,128)S(1)}, f32[1,1,512]{2,1,0:T(1,128)}, u32[]{:S(2)}) copy-start(f32[1,1,512]{2,1,0:T(1,128)} %get-tuple-element.126) | copy-start | bytes 6148
  129.6 28.5 %copy-start.35 = (f32[1,1,512]{2,1,0:T(1,128)S(1)}, f32[1,1,512]{2,1,0:T(1,128)}, u32[]{:S(2)}) copy-start(f32[1,1,512]{2,1,0:T(1,128)} %get-tuple-element.127) | copy-start | bytes 6148
  158.4 32.1 %copy-start.30 = (f32[1,1,512]{2,1,0:T(1,128)S(1)}, f32[1,1,512]{2,1,0:T(1,128)}, u32[]{:S(2)}) copy-start(f32[1,1,512]{2,1,0:T(1,128)} %get-tuple-element.128) | copy-start | bytes 6148
  158.4 32.1 %copy-start.31 = (f32[1,1,512]{2,1,0:T(1,128)S(1)}, f32[1,1,512]{2,1,0:T(1,128)}, u32[]{:S(2)}) copy-start(f32[1,1,512]{2,1,0:T(1,128)} %get-tuple-element.129) | copy-start | bytes 6148
  158.4 32.1 %copy-start.32 = (f32[1,1,512]{2,1,0:T(1,128)S(1)}, f32[1,1,512]{2,1,0:T(1,128)}, u32[]{:S(2)}) copy-start(f32[1,1,512]{2,1,0:T(1,128)} %get-tuple-element.130) | copy-start | bytes 6148
  195.4 35.4 %collective-permute-start.5 = (bf16[3,512,512]{2,1,0:T(8,128)(2,1)}, bf16[3,512,512]{2,1,0:T(8,128)(2,1)}, u32[]{:S(2)}, u32[]{:S(2)}) collective-permute-start(bf16[3,512,512]{2,1,0:T(8,128)(2,1)} %broadcast_select_fusion.3), channel_id=1, source_target_pairs={{0,16},{16,0},{1,17},{17,1},{2,18},{18,2},{3,19},{19,3},{4,20},{20... | collective-permute-start | bytes 4718600 | tf_op jit(solution)/shard_map/ppermute | solution.py:111
  201.2 10.8 %copy-start.8 = (bf16[4,386,512]{2,1,0:T(8,128)(2,1)S(1)}, bf16[4,386,512]{2,1,0:T(8,128)(2,1)}, u32[]{:S(2)}) copy-start(bf16[4,386,512]{2,1,0:T(8,128)(2,1)} %copy-done.7) | copy-start | bytes 4743172
  201.2 10.8 %copy-start.15 = (bf16[1024,1,512]{2,0,1:T(8,128)(2,1)S(1)}, bf16[1024,1,512]{2,0,1:T(8,128)(2,1)}, u32[]{:S(2)}) copy-start(bf16[1024,1,512]{2,0,1:T(8,128)(2,1)} %get-tuple-element.118) | copy-start | bytes 3145732
  201.2 12.1 %collective-permute-start.6 = (f32[32,64,16]{1,2,0:T(8,128)S(1)}, f32[32,64,16]{1,2,0:T(8,128)S(1)}, u32[]{:S(2)}, u32[]{:S(2)}) collective-permute-start(f32[32,64,16]{1,2,0:T(8,128)S(1)} %get-tuple-element.54), channel_id=1, source_target_pairs={{0,4},{4,8},{8,12},{1,5},{5,9},{9,13},{2,6},{6,10},{10,14},{3,7},{... | collective-permute-start | bytes 393224 | tf_op jit(solution)/shard_map/ppermute | solution.py:177
  203.2 10.8 %collective-permute-start.7 = (f32[32,64,16]{1,2,0:T(8,128)S(1)}, f32[32,64,16]{1,2,0:T(8,128)S(1)}, u32[]{:S(2)}, u32[]{:S(2)}) collective-permute-start(f32[32,64,16]{1,2,0:T(8,128)S(1)} %get-tuple-element.54), channel_id=1, source_target_pairs={{0,8},{4,12},{1,9},{5,13},{2,10},{6,14},{3,11},{7,15},{16,24},{20,... | collective-permute-start | bytes 393224 | tf_op jit(solution)/shard_map/ppermute | solution.py:177
  207.3 11.1 %collective-permute-start.8 = (f32[32,64,16]{1,2,0:T(8,128)S(1)}, f32[32,64,16]{1,2,0:T(8,128)S(1)}, u32[]{:S(2)}, u32[]{:S(2)}) collective-permute-start(f32[32,64,16]{1,2,0:T(8,128)S(1)} %get-tuple-element.54), channel_id=1, source_target_pairs={{0,12},{1,13},{2,14},{3,15},{16,28},{17,29},{18,30},{19,31}} | collective-permute-start | bytes 393224 | tf_op jit(solution)/shard_map/ppermute | solution.py:177
  212.0 6.5 %copy-start.22 = (f32[32,64]{1,0:T(8,128)S(1)}, f32[32,64]{1,0:T(8,128)}, u32[]{:S(2)}) copy-start(f32[32,64]{1,0:T(8,128)} %get-tuple-element.135) | copy-start | bytes 24580
  212.0 6.5 %copy-start.23 = (f32[32,64]{1,0:T(8,128)S(1)}, f32[32,64]{1,0:T(8,128)}, u32[]{:S(2)}) copy-start(f32[32,64]{1,0:T(8,128)} %get-tuple-element.136) | copy-start | bytes 24580
  212.0 6.6 %copy-start.11 = (f32[32,128,64]{1,2,0:T(8,128)S(1)}, f32[32,128,64]{1,2,0:T(8,128)}, u32[]{:S(2)}) copy-start(f32[32,128,64]{1,2,0:T(8,128)} %exponential_multiply_fusion) | copy-start | bytes 3145732
  212.0 6.6 %copy-start.21 = (f32[3,32,64,16]{2,3,1,0:T(8,128)S(1)}, f32[3,32,64,16]{2,3,1,0:T(8,128)}, u32[]{:S(2)}) copy-start(f32[3,32,64,16]{2,3,1,0:T(8,128)} %get-tuple-element.55) | copy-start | bytes 1179652
  234.8 9.0 %collective-permute-start.9 = (bf16[1,384,512]{2,1,0:T(8,128)(2,1)S(1)}, bf16[1,384,512]{2,1,0:T(8,128)(2,1)S(1)}, u32[]{:S(2)}, u32[]{:S(2)}) collective-permute-start(bf16[1,384,512]{2,1,0:T(8,128)(2,1)S(1)} %bitcast.147), channel_id=1, source_target_pairs={{0,2},{1,3},{2,0},{3,1},{4,6},{5,7},{6,4},{7,5},{8,10},{9,11},{10,... | collective-permute-start | bytes 1179656 | tf_op jit(solution)/shard_map/ppermute | solution.py:201
  243.9 3.9 %collective-permute-start.10 = (bf16[2,384,512]{2,1,0:T(8,128)(2,1)S(1)}, bf16[2,384,512]{2,1,0:T(8,128)(2,1)S(1)}, u32[]{:S(2)}, u32[]{:S(2)}) collective-permute-start(bf16[2,384,512]{2,1,0:T(8,128)(2,1)S(1)} %pad_maximum_fusion.2), channel_id=1, source_target_pairs={{0,1},{1,0},{2,3},{3,2},{4,5},{5,4},{6,7},{7,6},{8,9},{9,8},{10,11... | collective-permute-start | bytes 2359304 | tf_op jit(solution)/shard_map/ppermute | solution.py:201
  (22 other events, 48.2 us)
Sparse Core Ops, SparseCore 0:
  9.3 48.3 all-gather.6
  59.3 44.4 all-gather.8
  105.4 44.4 all-gather.10

commit v9 on v6

--- a/solution.py
+++ b/solution.py
@@ -170,7 +170,7 @@
         return (step_decay * state + end_block, state)
 
     zero_state = jnp.zeros((local_groups, mode_count, group_size), jnp.float32)
-    own_state, local_starts = lax.scan(advance, zero_state, ends)
+    own_state, local_starts = lax.scan(advance, zero_state, ends, unroll=True)
     incoming = jnp.zeros_like(own_state)
     for by in range(1, n_ctx):
         pairs = [(k, k + by) for k in range(n_ctx - by)]

time: 221 us -> 226 us (1.023); the launches traced: 216 us -> 226 us
  waiting for transfers between devices: 97.7 us -> 115 us
  other arithmetic: 26.3 us -> 21 us
    ppermute x3, waiting for transfers between devices: 27.9 us -> 42.9 us  [relay(): received.append(lax.ppermute(send, 'grp', pairs))]
    concatenate x3, other arithmetic: 8.49 us -> 5.88 us  [relay_send(): doubled = jnp.concatenate([got, got], axis=0)]
    unnamed x82 -> x78, local copies, waits for them, and re-layouts: 7.59 us -> 7.67 us
  transfers between devices with their start and end apart: 14 -> 14, of which waited for: 9 -> 9; matrix products, arithmetic and copies ran while one was open for 31% -> 26% of each run, Pallas kernels for 0% -> 0%
where the time goes in v9:
time: 226 us
  waiting for transfers between devices  115 us (51%)
  matrix products  31.2 us (14%)
  local copies, waits for them, and re-layouts  25.1 us (11%)
  other arithmetic  21 us (9%)
  starting transfers between devices  20 us (9%)
  between operations  14 us (6%)
    ppermute x3, waiting for transfers between devices, relay(): received.append(lax.ppermute(send, 'grp', pairs))  42.9 us
    all_gather x3, waiting for transfers between devices, body(): got = lax.all_gather(own[:, s, :], 'ctx', axis=0)  36.7 us
    ppermute x2, waiting for transfers between devices, gather_by_swaps(): held = jnp.concatenate([held, lax.ppermute(held, axis, pairs)], axis=0)  16.3 us
    ppermute x3, waiting for transfers between devices, body(): arrived = lax.ppermute(own_state, 'ctx', pairs)  8.68 us
    ppermute x2, waiting for transfers between devices, body(): arrived = lax.ppermute(held, 'tp', pairs)  8.42 us
    unnamed x78, local copies, waits for them, and re-layouts  7.67 us
    ppermute x3, starting transfers between devices, body(): arrived = lax.ppermute(own_state, 'ctx', pairs)  7.44 us
    dot_general x4, matrix products, contribution(): return jnp.dot(block, rows, preferred_element_type=jnp.float32)  5.94 us
  transfers between devices with their start and end apart: 14, of which 9 were waited for; matrix products, arithmetic and copies ran while one was open for 26% of the time, Pallas kernels for 0%

profile of v9, /device:TPU:0, one launch (start us, length us, event | category | flops | bytes accessed | tf_op | source)
XLA Modules:
  0.0 225.9 jit_solution(9507087871073447188)
XLA Ops:
  6.5 2.6 %constant_dynamic-slice_fusion.2 = (bf16[512,1,512]{2,0,1:T(8,128)(2,1)}, bf16[512,1,512]{2,0,1:T(8,128)(2,1)}, bf16[512,1,512]{2,0,1:T(8,128)(2,1)}) fusion(bf16[1024,3,512]{2,0,1:T(8,128)(2,1)} %param.12, s32[]{:T(128)S(6)} %select_n.104, s32[]{:T(128)S(6)} %add.255, s32[]{:T(128)S(6)} %add.254), kind=kLoop, calls=%fused_computation.141 | loop fusion | bytes 3145740 | tf_op jit(solution)/shard_map/slice | solution.py:117
  10.1 3.0 %collective-permute-start = (bf16[1,385,1024]{2,1,0:T(8,128)(2,1)S(1)}, bf16[1,385,1024]{2,1,0:T(8,128)(2,1)S(1)}, u32[]{:S(2)}, u32[]{:S(2)}) collective-permute-start(bf16[1,385,1024]{2,1,0:T(8,128)(2,1)S(1)} %maximum_bitcast_fusion), channel_id=1, source_target_pairs={{0,2},{1,3},{2,0},{3,1},{4,6},{5,7},{6,4},{7,5},{8,10},{9,11},{10,... | collective-permute-start | bytes 2365448 | tf_op jit(solution)/shard_map/ppermute | solution.py:57
  14.7 16.3 %collective-permute-done = bf16[1,385,1024]{2,1,0:T(8,128)(2,1)S(1)} collective-permute-done((bf16[1,385,1024]{2,1,0:T(8,128)(2,1)S(1)}, bf16[1,385,1024]{2,1,0:T(8,128)(2,1)S(1)}, u32[]{:S(2)}, u32[]{:S(2)}) %collective-permute-start) | collective-permute-done | bytes 788512 | tf_op jit(solution)/shard_map/ppermute | solution.py:57
  31.2 1.6 copy.44
  34.9 1.6 exponential_multiply_fusion
  36.5 5.5 %convolution_select_fusion = f32[32,128,128]{2,1,0:T(8,128)} fusion(pred[128,128]{1,0:T(8,128)(4,1)S(1)} %broadcast_compare_fusion, f32[32,64]{1,0:T(8,128)S(1)} %copy-done.22, f32[128]{0:T(128)S(1)} %iota_convert_fusion.1, f32[32,64]{1,0:T(8,128)S(1)} %get-tuple-element.58, f32[32,64]{1,0:T(8,128)S(1)} %get-tuple-element.57), kind=kOutput, calls=%fused_computation.21 | convolution fusion | flops 403963904 | bytes 2138624 | tf_op jit(solution)/shard_map/gin,gjn->gij/dot_general | solution.py:91
  42.1 1.7 fusion.76
  44.3 2.0 pad_maximum_fusion
  46.2 2.7 %gather_fusion.1 = bf16[4,385,1024]{2,1,0:T(8,128)(2,1)S(1)} fusion(bf16[4,385,1024]{2,1,0:T(8,128)(2,1)} %pad_maximum_fusion, s32[1024]{0:T(1024)S(1)} %pad_clamp_fusion.2), kind=kCustom, calls=%fused_computation.3 | custom fusion | bytes 6307856 | tf_op jit(solution)/shard_map/jit(_take)/gather | solution.py:62
  51.3 3.7 %collective-permute-start.2 = (bf16[2,4096]{1,0:T(2,128)(2,1)S(1)}, bf16[2,4096]{1,0:T(2,128)(2,1)S(1)}, u32[]{:S(2)}, u32[]{:S(2)}) collective-permute-start(bf16[2,4096]{1,0:T(2,128)(2,1)S(1)} %pad_maximum_fusion.3), channel_id=1, source_target_pairs={{0,4},{4,8},{8,12},{1,5},{5,9},{9,13},{2,6},{6,10},{10,14},{3,7},{... | collective-permute-start | bytes 49160 | tf_op jit(solution)/shard_map/ppermute | solution.py:12
  56.5 3.5 %maximum_maximum_fusion = bf16[387,4096]{1,0:T(8,128)(2,1)S(1)} fusion(bf16[385,1024]{1,0:T(8,128)(2,1)} %copy-done.2, bf16[385,1024]{1,0:T(8,128)(2,1)} %copy-done.3, bf16[385,1024]{1,0:T(8,128)(2,1)} %copy-done.4, bf16[385,1024]{1,0:T(8,128)(2,1)} %copy-done.1, bf16[2,4096]{1,0:T(2,128)(2,1)S(1)} %collective-permute-done.2), kind=kLoop, calls=%fused_computation.16 | loop fusion | flops 15851520 | bytes 6340608 | tf_op jit(solution)/shard_map/concatenate | solution.py:100
  60.0 3.2 %fusion.7 = bf16[3,512,512]{2,1,0:T(8,128)(2,1)} fusion(s32[]{:T(128)S(6)} %select_n.106, bf16[4,512,512]{2,1,0:T(8,128)(2,1)} %bitcast.161), kind=kLoop, calls=%fused_computation.27 | loop fusion | flops 786432 | bytes 3670020 | tf_op jit(solution)/shard_map/concatenate | solution.py:104
  67.8 1.9 gather_fusion.2
  69.7 1.8 gather_fusion.3
  73.0 30.8 %all-gather.9.cloned.1.call-done = bf16[2048,1,512]{2,0,1:T(8,128)(2,1)} async-done(((bf16[512,1,512]{2,0,1:T(8,128)(2,1)}), bf16[2048,1,512]{2,0,1:T(8,128)(2,1)}) %all-gather.9.cloned.1.call-update) | async-done | bytes 2097168 | tf_op jit(solution)/shard_map/all_gather | solution.py:117
  103.8 2.1 fusion.6
  107.5 2.5 %convolution_bitcast_fusion.5 = f32[386,512]{1,0:T(8,128)S(1)} fusion(bf16[4,512,512]{2,1,0:T(8,128)(2,1)S(1)} %bitcast.162, bf16[4,386,512]{2,1,0:T(8,128)(2,1)} %gather_fusion.2, pred[4]{0:T(512)(128)(4,1)S(1)} %compare_and_fusion.1), kind=kOutput, calls=%fused_computation.34 | convolution fusion | flops 810291200 | bytes 4468740 | tf_op jit(solution)/shard_map/ktr,krc->tc/dot_general | solution.py:143
  114.3 2.2 fusion.15
  116.8 25.1 %collective-permute-done.4 = bf16[3,512,512]{2,1,0:T(8,128)(2,1)S(1)} collective-permute-done((bf16[3,512,512]{2,1,0:T(8,128)(2,1)S(1)}, bf16[3,512,512]{2,1,0:T(8,128)(2,1)S(1)}, u32[]{:S(2)}, u32[]{:S(2)}) %collective-permute-start.4) | collective-permute-done | bytes 1572896 | tf_op jit(solution)/shard_map/ppermute | solution.py:111
  143.9 6.0 %all-gather.11.cloned.1.call-done = bf16[2048,1,512]{2,0,1:T(8,128)(2,1)} async-done(((bf16[512,1,512]{2,0,1:T(8,128)(2,1)}), bf16[2048,1,512]{2,0,1:T(8,128)(2,1)}) %all-gather.11.cloned.1.call-update) | async-done | bytes 2097168 | tf_op jit(solution)/shard_map/all_gather | solution.py:117
  151.7 3.1 %convolution_bitcast_fusion.6 = f32[3,32,64,16]{2,3,0,1:T(8,128)S(1)} fusion(f32[32,64,128]{2,1,0:T(8,128)} %multiply_exponential_fusion, f32[3,128,32,16]{1,0,3,2:T(4,128)S(1)} %reshape.175), kind=kOutput, calls=%fused_computation.40 | convolution fusion | flops 150994944 | bytes 2228224 | tf_op jit(solution)/shard_map/gni,bigc->bgnc/dot_general | solution.py:166
  154.9 3.4 %collective-permute-start.8 = (f32[32,64,16]{1,2,0:T(8,128)S(1)}, f32[32,64,16]{1,2,0:T(8,128)S(1)}, u32[]{:S(2)}, u32[]{:S(2)}) collective-permute-start(f32[32,64,16]{1,2,0:T(8,128)S(1)} %fusion.60), channel_id=1, source_target_pairs={{0,12},{1,13},{2,14},{3,15},{16,28},{17,29},{18,30},{19,31}} | collective-permute-start | bytes 393224 | tf_op jit(solution)/shard_map/ppermute | solution.py:177
  159.7 2.7 %collective-permute-start.6 = (f32[32,64,16]{1,2,0:T(8,128)S(1)}, f32[32,64,16]{1,2,0:T(8,128)S(1)}, u32[]{:S(2)}, u32[]{:S(2)}) collective-permute-start(f32[32,64,16]{1,2,0:T(8,128)S(1)} %fusion.60), channel_id=1, source_target_pairs={{0,4},{4,8},{8,12},{1,5},{5,9},{9,13},{2,6},{6,10},{10,14},{3,7},{... | collective-permute-start | bytes 393224 | tf_op jit(solution)/shard_map/ppermute | solution.py:177
  166.7 4.0 %collective-permute-done.7 = f32[32,64,16]{1,2,0:T(8,128)S(1)} collective-permute-done((f32[32,64,16]{1,2,0:T(8,128)S(1)}, f32[32,64,16]{1,2,0:T(8,128)S(1)}, u32[]{:S(2)}, u32[]{:S(2)}) %collective-permute-start.7) | collective-permute-done | bytes 131104 | tf_op jit(solution)/shard_map/ppermute | solution.py:177
  170.8 4.7 %collective-permute-done.6 = f32[32,64,16]{1,2,0:T(8,128)S(1)} collective-permute-done((f32[32,64,16]{1,2,0:T(8,128)S(1)}, f32[32,64,16]{1,2,0:T(8,128)S(1)}, u32[]{:S(2)}, u32[]{:S(2)}) %collective-permute-start.6) | collective-permute-done | bytes 131104 | tf_op jit(solution)/shard_map/ppermute | solution.py:177
  177.1 3.4 %fusion.11 = f32[3,128,32,16]{1,3,0,2:T(8,128)S(1)} fusion(f32[32,3,16,128]{3,2,1,0:T(8,128)S(1)} %fusion.20, f32[32,128,128]{2,1,0:T(8,128)S(1)} %copy-done.17, f32[3,128,32,16]{1,0,3,2:T(4,128)S(1)} %reshape.175), kind=kOutput, calls=%fused_computation.39 | convolution fusion | flops 302186496 | bytes 4456448 | tf_op jit(solution)/shard_map/gij,bjgc->bigc/dot_general | solution.py:165
  181.0 17.8 %collective-permute-done.5 = bf16[3,512,512]{2,1,0:T(8,128)(2,1)S(1)} collective-permute-done((bf16[3,512,512]{2,1,0:T(8,128)(2,1)S(1)}, bf16[3,512,512]{2,1,0:T(8,128)(2,1)S(1)}, u32[]{:S(2)}, u32[]{:S(2)}) %collective-permute-start.5) | collective-permute-done | bytes 1572896 | tf_op jit(solution)/shard_map/ppermute | solution.py:111
  200.3 2.4 %fusion.19 = f32[386,512]{1,0:T(8,128)S(1)} fusion(f32[386,512]{1,0:T(8,128)} %convolution_add_fusion, bf16[4,386,512]{2,1,0:T(8,128)(2,1)S(1)} %broadcast_select_fusion.1, bf16[3,512,512]{2,1,0:T(8,128)(2,1)} %copy-done.35), kind=kOutput, calls=%fused_computation.46 | convolution fusion | flops 607520768 | bytes 4734976 | tf_op jit(solution)/shard_map/ktr,krc->tc/dot_general | solution.py:147
  204.3 8.4 %collective-permute-done.9 = bf16[1,384,512]{2,1,0:T(8,128)(2,1)S(1)} collective-permute-done((bf16[1,384,512]{2,1,0:T(8,128)(2,1)S(1)}, bf16[1,384,512]{2,1,0:T(8,128)(2,1)S(1)}, u32[]{:S(2)}, u32[]{:S(2)}) %collective-permute-start.9) | collective-permute-done | bytes 393248 | tf_op jit(solution)/shard_map/ppermute | solution.py:201
  212.9 1.9 fusion.31
  214.8 1.8 fusion.29
  217.8 1.6 add_convert_fusion
  (153 shorter events, 36.9 us)
Async XLA Ops:
  6.5 53.5 %all-gather.7.cloned.1.call-start = ((), (), s32[]{:S(2)}) async-start(), calls=%async_computation | async-start | bytes 2621440 | tf_op jit(solution)/shard_map/all_gather | solution.py:117
  6.5 3.4 %copy-start.33 = (bf16[1024]{0:T(1024)(128)(2,1)S(1)}, bf16[1024]{0:T(1024)(128)(2,1)}, u32[]{:S(2)}) copy-start(bf16[1024]{0:T(1024)(128)(2,1)} %param.11) | copy-start | bytes 6148
  6.5 3.5 %copy-start.9 = (bf16[384,1024]{1,0:T(8,128)(2,1)S(1)}, bf16[384,1024]{1,0:T(8,128)(2,1)}, u32[]{:S(2)}) copy-start(bf16[384,1024]{1,0:T(8,128)(2,1)} %param.10) | copy-start | bytes 2359300
  9.2 4.1 %copy-start = (s32[4]{0:T(128)S(1)}, s32[4]{0:T(128)}, u32[]{:S(2)}) copy-start(s32[4]{0:T(128)} %constant.121.clone) | copy-start | bytes 52
  9.2 94.6 %all-gather.9.cloned.1.call-start = ((), (), s32[]{:S(2)}) async-start(), calls=%async_computation.1 | async-start | bytes 2621440 | tf_op jit(solution)/shard_map/all_gather | solution.py:117
  9.2 4.8 %copy-start.23 = (f32[3,3,512]{2,1,0:T(4,128)S(1)}, f32[3,3,512]{2,1,0:T(4,128)}, u32[]{:S(2)}) copy-start(f32[3,3,512]{2,1,0:T(4,128)} %param.13) | copy-start | bytes 55300
  9.9 139.9 %all-gather.11.cloned.1.call-start = ((), (), s32[]{:S(2)}) async-start(), calls=%async_computation.2 | async-start | bytes 2621440 | tf_op jit(solution)/shard_map/all_gather | solution.py:117
  10.1 20.9 %collective-permute-start = (bf16[1,385,1024]{2,1,0:T(8,128)(2,1)S(1)}, bf16[1,385,1024]{2,1,0:T(8,128)(2,1)S(1)}, u32[]{:S(2)}, u32[]{:S(2)}) collective-permute-start(bf16[1,385,1024]{2,1,0:T(8,128)(2,1)S(1)} %maximum_bitcast_fusion), channel_id=1, source_target_pairs={{0,2},{1,3},{2,0},{3,1},{4,6},{5,7},{6,4},{7,5},{8,10},{9,11},{10,... | collective-permute-start | bytes 2365448 | tf_op jit(solution)/shard_map/ppermute | solution.py:57
  32.8 11.0 %collective-permute-start.1 = (bf16[2,385,1024]{2,0,1:T(2,128)(2,1)S(1)}, bf16[2,385,1024]{2,0,1:T(2,128)(2,1)S(1)}, u32[]{:S(2)}, u32[]{:S(2)}) collective-permute-start(bf16[2,385,1024]{2,0,1:T(2,128)(2,1)S(1)} %copy.44), channel_id=1, source_target_pairs={{0,1},{1,0},{2,3},{3,2},{4,5},{5,4},{6,7},{7,6},{8,9},{9,8},{10,11... | collective-permute-start | bytes 4730888 | tf_op jit(solution)/shard_map/ppermute | solution.py:57
  34.9 7.1 %copy-start.5 = (bf16[1024,3,512]{2,0,1:T(8,128)(2,1)S(1)}, bf16[1024,3,512]{2,0,1:T(8,128)(2,1)}, u32[]{:S(2)}) copy-start(bf16[1024,3,512]{2,0,1:T(8,128)(2,1)} %param.12) | copy-start | bytes 9437188
  51.3 5.2 %collective-permute-start.2 = (bf16[2,4096]{1,0:T(2,128)(2,1)S(1)}, bf16[2,4096]{1,0:T(2,128)(2,1)S(1)}, u32[]{:S(2)}, u32[]{:S(2)}) collective-permute-start(bf16[2,4096]{1,0:T(2,128)(2,1)S(1)} %pad_maximum_fusion.3), channel_id=1, source_target_pairs={{0,4},{4,8},{8,12},{1,5},{5,9},{9,13},{2,6},{6,10},{10,14},{3,7},{... | collective-permute-start | bytes 49160 | tf_op jit(solution)/shard_map/ppermute | solution.py:12
  55.1 56.5 %copy-start.36 = (pred[4]{0:T(512)(128)(4,1)}, pred[4]{0:T(512)(128)(4,1)S(1)}, u32[]{:S(2)}) copy-start(pred[4]{0:T(512)(128)(4,1)S(1)} %compare_and_fusion.1) | copy-start | bytes 16
  71.5 42.8 %collective-permute-start.3 = (bf16[3,512,512]{2,1,0:T(8,128)(2,1)}, bf16[3,512,512]{2,1,0:T(8,128)(2,1)}, u32[]{:S(2)}, u32[]{:S(2)}) collective-permute-start(bf16[3,512,512]{2,1,0:T(8,128)(2,1)} %fusion.7), channel_id=1, source_target_pairs={{0,16},{16,0},{1,17},{17,1},{2,18},{18,2},{3,19},{19,3},{4,20},{20... | collective-permute-start | bytes 4718600 | tf_op jit(solution)/shard_map/ppermute | solution.py:111
  103.8 3.7 %copy-start.15 = (bf16[2048,1,512]{2,0,1:T(8,128)(2,1)S(1)}, bf16[2048,1,512]{2,0,1:T(8,128)(2,1)}, u32[]{:S(2)}) copy-start(bf16[2048,1,512]{2,0,1:T(8,128)(2,1)} %all-gather.7.cloned.1.call-done) | copy-start | bytes 6291460
  105.9 4.0 %copy-start.6 = (bf16[4,386,512]{2,1,0:T(8,128)(2,1)S(1)}, bf16[4,386,512]{2,1,0:T(8,128)(2,1)}, u32[]{:S(2)}) copy-start(bf16[4,386,512]{2,1,0:T(8,128)(2,1)} %gather_fusion.3) | copy-start | bytes 4743172
  105.9 36.0 %collective-permute-start.4 = (bf16[3,512,512]{2,1,0:T(8,128)(2,1)S(1)}, bf16[3,512,512]{2,1,0:T(8,128)(2,1)S(1)}, u32[]{:S(2)}, u32[]{:S(2)}) collective-permute-start(bf16[3,512,512]{2,1,0:T(8,128)(2,1)S(1)} %fusion.6), channel_id=1, source_target_pairs={{0,16},{16,0},{1,17},{17,1},{2,18},{18,2},{3,19},{19,3},{4,20},{20... | collective-permute-start | bytes 4718600 | tf_op jit(solution)/shard_map/ppermute | solution.py:111
  116.8 25.9 %copy-start.27 = (f32[1,1,512]{2,1,0:T(1,128)S(1)}, f32[1,1,512]{2,1,0:T(1,128)}, u32[]{:S(2)}) copy-start(f32[1,1,512]{2,1,0:T(1,128)} %get-tuple-element.43) | copy-start | bytes 6148
  116.8 25.9 %copy-start.28 = (f32[1,1,512]{2,1,0:T(1,128)S(1)}, f32[1,1,512]{2,1,0:T(1,128)}, u32[]{:S(2)}) copy-start(f32[1,1,512]{2,1,0:T(1,128)} %get-tuple-element.44) | copy-start | bytes 6148
  116.8 25.9 %copy-start.29 = (f32[1,1,512]{2,1,0:T(1,128)S(1)}, f32[1,1,512]{2,1,0:T(1,128)}, u32[]{:S(2)}) copy-start(f32[1,1,512]{2,1,0:T(1,128)} %get-tuple-element.45) | copy-start | bytes 6148
  151.7 10.7 %copy-start.14 = (bf16[2048,1,512]{2,0,1:T(8,128)(2,1)S(1)}, bf16[2048,1,512]{2,0,1:T(8,128)(2,1)}, u32[]{:S(2)}) copy-start(bf16[2048,1,512]{2,0,1:T(8,128)(2,1)} %all-gather.11.cloned.1.call-done) | copy-start | bytes 6291460
  154.9 9.4 %copy-start.19 = (bf16[4,386,512]{2,1,0:T(8,128)(2,1)S(1)}, bf16[4,386,512]{2,1,0:T(8,128)(2,1)}, u32[]{:S(2)}) copy-start(bf16[4,386,512]{2,1,0:T(8,128)(2,1)} %gather_fusion.2) | copy-start | bytes 4743172
  154.9 9.4 %copy-start.37 = (pred[4]{0:T(512)(128)(4,1)S(1)}, pred[4]{0:T(512)(128)(4,1)}, u32[]{:S(2)}) copy-start(pred[4]{0:T(512)(128)(4,1)} %copy-done.36) | copy-start | bytes 16
  154.9 11.8 %collective-permute-start.8 = (f32[32,64,16]{1,2,0:T(8,128)S(1)}, f32[32,64,16]{1,2,0:T(8,128)S(1)}, u32[]{:S(2)}, u32[]{:S(2)}) collective-permute-start(f32[32,64,16]{1,2,0:T(8,128)S(1)} %fusion.60), channel_id=1, source_target_pairs={{0,12},{1,13},{2,14},{3,15},{16,28},{17,29},{18,30},{19,31}} | collective-permute-start | bytes 393224 | tf_op jit(solution)/shard_map/ppermute | solution.py:177
  158.4 12.4 %collective-permute-start.7 = (f32[32,64,16]{1,2,0:T(8,128)S(1)}, f32[32,64,16]{1,2,0:T(8,128)S(1)}, u32[]{:S(2)}, u32[]{:S(2)}) collective-permute-start(f32[32,64,16]{1,2,0:T(8,128)S(1)} %fusion.60), channel_id=1, source_target_pairs={{0,8},{4,12},{1,9},{5,13},{2,10},{6,14},{3,11},{7,15},{16,24},{20,... | collective-permute-start | bytes 393224 | tf_op jit(solution)/shard_map/ppermute | solution.py:177
  159.7 15.7 %collective-permute-start.6 = (f32[32,64,16]{1,2,0:T(8,128)S(1)}, f32[32,64,16]{1,2,0:T(8,128)S(1)}, u32[]{:S(2)}, u32[]{:S(2)}) collective-permute-start(f32[32,64,16]{1,2,0:T(8,128)S(1)} %fusion.60), channel_id=1, source_target_pairs={{0,4},{4,8},{8,12},{1,5},{5,9},{9,13},{2,6},{6,10},{10,14},{3,7},{... | collective-permute-start | bytes 393224 | tf_op jit(solution)/shard_map/ppermute | solution.py:177
  163.0 35.8 %collective-permute-start.5 = (bf16[3,512,512]{2,1,0:T(8,128)(2,1)S(1)}, bf16[3,512,512]{2,1,0:T(8,128)(2,1)S(1)}, u32[]{:S(2)}, u32[]{:S(2)}) collective-permute-start(bf16[3,512,512]{2,1,0:T(8,128)(2,1)S(1)} %fusion.5), channel_id=1, source_target_pairs={{0,16},{16,0},{1,17},{17,1},{2,18},{18,2},{3,19},{19,3},{4,20},{20... | collective-permute-start | bytes 4718600 | tf_op jit(solution)/shard_map/ppermute | solution.py:111
  165.4 10.0 %copy-start.20 = (f32[32,64]{1,0:T(8,128)S(1)}, f32[32,64]{1,0:T(8,128)}, u32[]{:S(2)}) copy-start(f32[32,64]{1,0:T(8,128)} %get-tuple-element.54) | copy-start | bytes 24580
  166.7 8.9 %copy-start.8 = (f32[32,128,64]{1,2,0:T(8,128)S(1)}, f32[32,128,64]{1,2,0:T(8,128)}, u32[]{:S(2)}) copy-start(f32[32,128,64]{1,2,0:T(8,128)} %exponential_multiply_fusion) | copy-start | bytes 3145732
  166.7 8.9 %copy-start.34 = (f32[3]{0:T(128)S(1)}, f32[3]{0:T(128)}, u32[]{:S(2)}) copy-start(f32[3]{0:T(128)} %pad.2.clone) | copy-start | bytes 40
  203.0 9.7 %collective-permute-start.9 = (bf16[1,384,512]{2,1,0:T(8,128)(2,1)S(1)}, bf16[1,384,512]{2,1,0:T(8,128)(2,1)S(1)}, u32[]{:S(2)}, u32[]{:S(2)}) collective-permute-start(bf16[1,384,512]{2,1,0:T(8,128)(2,1)S(1)} %bitcast.156), channel_id=1, source_target_pairs={{0,2},{1,3},{2,0},{3,1},{4,6},{5,7},{6,4},{7,5},{8,10},{9,11},{10,... | collective-permute-start | bytes 1179656 | tf_op jit(solution)/shard_map/ppermute | solution.py:201
  212.8 3.9 %collective-permute-start.10 = (bf16[2,384,512]{2,1,0:T(8,128)(2,1)S(1)}, bf16[2,384,512]{2,1,0:T(8,128)(2,1)S(1)}, u32[]{:S(2)}, u32[]{:S(2)}) collective-permute-start(bf16[2,384,512]{2,1,0:T(8,128)(2,1)S(1)} %pad_maximum_fusion.2), channel_id=1, source_target_pairs={{0,1},{1,0},{2,3},{3,2},{4,5},{5,4},{6,7},{7,6},{8,9},{9,8},{10,11... | collective-permute-start | bytes 2359304 | tf_op jit(solution)/shard_map/ppermute | solution.py:201
  212.9 3.8 %copy-start.7 = (bf16[2048,1024]{1,0:T(8,128)(2,1)S(1)}, bf16[2048,1024]{1,0:T(8,128)(2,1)}, u32[]{:S(2)}) copy-start(bf16[2048,1024]{1,0:T(8,128)(2,1)} %param.16) | copy-start | bytes 12582916
  (20 other events, 36.1 us)
Sparse Core Ops, SparseCore 0:
  9.3 48.3 all-gather.6
  59.3 44.4 all-gather.8
  105.4 44.4 all-gather.10

commit v10 on v6

--- a/solution.py
+++ b/solution.py
@@ -192,7 +192,7 @@
         return jnp.dot(block, rows, preferred_element_type=jnp.float32)
 
     if count & (count - 1) == 0:
-        mixed = contribution(gated, me_tp)
+        mixed = tokens.astype(jnp.float32) + contribution(gated, me_tp)
         held = gated[None]
         masks = [0]
         bit = count // 2
@@ -204,6 +204,7 @@
             held = jnp.concatenate([held, arrived], axis=0)
             masks = masks + [m ^ bit for m in masks]
             bit //= 2
+        return mixed.astype(jnp.bfloat16)
     else:
         pieces = gather_by_swaps(gated, "tp")
         mixed = jnp.einsum("qtc,qcf->tf", pieces, w_out.reshape(pieces.shape[0], local_width, -1),

time: 221 us -> 220 us (level)
  no operation moved by 1% of the time
where the time goes in v10:
time: 220 us; the launch traced here: 216 us
  waiting for transfers between devices  97.7 us (44%)
  matrix products  32.1 us (15%)
  other arithmetic  26.3 us (12%)
  local copies, waits for them, and re-layouts  25.6 us (12%)
  starting transfers between devices  20.7 us (9%)
  between operations  14 us (6%)
    all_gather x3, waiting for transfers between devices, body(): got = lax.all_gather(own[:, s, :], 'ctx', axis=0)  37.3 us
    ppermute x3, waiting for transfers between devices, relay(): received.append(lax.ppermute(send, 'grp', pairs))  27.9 us
    ppermute x2, waiting for transfers between devices, gather_by_swaps(): held = jnp.concatenate([held, lax.ppermute(held, axis, pairs)], axis=0)  14.6 us
    concatenate x3, other arithmetic, relay_send(): doubled = jnp.concatenate([got, got], axis=0)  8.49 us
    ppermute x3, waiting for transfers between devices, body(): arrived = lax.ppermute(own_state, 'ctx', pairs)  8.46 us
    ppermute x2, waiting for transfers between devices, body(): arrived = lax.ppermute(held, 'tp', pairs)  8.38 us
    unnamed x82, local copies, waits for them, and re-layouts  7.59 us
    ppermute x3, starting transfers between devices, body(): arrived = lax.ppermute(own_state, 'ctx', pairs)  7.11 us
  transfers between devices with their start and end apart: 14, of which 9 were waited for; matrix products, arithmetic and copies ran while one was open for 31% of the time, Pallas kernels for 0%

profile of v10, /device:TPU:0, one launch (start us, length us, event | category | flops | bytes accessed | tf_op | source)
XLA Modules:
  0.0 216.3 jit_solution(15533052229411053623)
XLA Ops:
  6.5 2.6 %constant_dynamic-slice_fusion.2 = (bf16[512,1,512]{2,0,1:T(8,128)(2,1)}, bf16[512,1,512]{2,0,1:T(8,128)(2,1)}, bf16[512,1,512]{2,0,1:T(8,128)(2,1)}) fusion(bf16[1024,3,512]{2,0,1:T(8,128)(2,1)} %param.14, s32[]{:T(128)S(6)} %select_n.104, s32[]{:T(128)S(6)} %add.242, s32[]{:T(128)S(6)} %add.241), kind=kLoop, calls=%fused_computation.135 | loop fusion | bytes 3145740 | tf_op jit(solution)/shard_map/slice | solution.py:117
  10.1 3.0 %collective-permute-start = (bf16[1,385,1024]{2,1,0:T(8,128)(2,1)S(1)}, bf16[1,385,1024]{2,1,0:T(8,128)(2,1)S(1)}, u32[]{:S(2)}, u32[]{:S(2)}) collective-permute-start(bf16[1,385,1024]{2,1,0:T(8,128)(2,1)S(1)} %maximum_bitcast_fusion), channel_id=1, source_target_pairs={{0,2},{1,3},{2,0},{3,1},{4,6},{5,7},{6,4},{7,5},{8,10},{9,11},{10,... | collective-permute-start | bytes 2365448 | tf_op jit(solution)/shard_map/ppermute | solution.py:57
  16.4 14.6 %collective-permute-done = bf16[1,385,1024]{2,1,0:T(8,128)(2,1)S(1)} collective-permute-done((bf16[1,385,1024]{2,1,0:T(8,128)(2,1)S(1)}, bf16[1,385,1024]{2,1,0:T(8,128)(2,1)S(1)}, u32[]{:S(2)}, u32[]{:S(2)}) %collective-permute-start) | collective-permute-done | bytes 788512 | tf_op jit(solution)/shard_map/ppermute | solution.py:57
  36.6 5.5 %convolution_select_fusion = f32[32,128,128]{2,1,0:T(8,128)} fusion(pred[128,128]{1,0:T(8,128)(4,1)S(1)} %broadcast_compare_fusion, f32[32,64]{1,0:T(8,128)S(1)} %copy-done.26, f32[128]{0:T(128)S(1)} %iota_convert_fusion.1, f32[32,64]{1,0:T(8,128)S(1)} %get-tuple-element.138, f32[32,64]{1,0:T(8,128)S(1)} %get-tuple-element.137), kind=kOutput, calls=%fused_computation.23 | convolution fusion | flops 403963904 | bytes 2138624 | tf_op jit(solution)/shard_map/gin,gjn->gij/dot_general | solution.py:91
  42.1 1.8 fusion.72
  44.3 2.0 pad_maximum_fusion
  46.3 2.7 %gather_fusion.1 = bf16[4,385,1024]{2,1,0:T(8,128)(2,1)S(1)} fusion(bf16[4,385,1024]{2,1,0:T(8,128)(2,1)} %pad_maximum_fusion, s32[1024]{0:T(1024)S(1)} %pad_clamp_fusion.2), kind=kCustom, calls=%fused_computation.3 | custom fusion | bytes 6307856 | tf_op jit(solution)/shard_map/jit(_take)/gather | solution.py:62
  51.4 4.3 %collective-permute-start.2 = (bf16[2,4096]{1,0:T(2,128)(2,1)S(1)}, bf16[2,4096]{1,0:T(2,128)(2,1)}, u32[]{:S(2)}, u32[]{:S(2)}) collective-permute-start(bf16[2,4096]{1,0:T(2,128)(2,1)S(1)} %pad_maximum_fusion.3), channel_id=1, source_target_pairs={{0,4},{4,8},{8,12},{1,5},{5,9},{9,13},{2,6},{6,10},{10,14},{3,7},{... | collective-permute-start | bytes 49160 | tf_op jit(solution)/shard_map/ppermute | solution.py:12
  56.5 3.5 %maximum_maximum_fusion = bf16[387,4096]{1,0:T(8,128)(2,1)S(1)} fusion(bf16[385,1024]{1,0:T(8,128)(2,1)} %copy-done.2, bf16[385,1024]{1,0:T(8,128)(2,1)} %copy-done.3, bf16[385,1024]{1,0:T(8,128)(2,1)} %copy-done.4, bf16[385,1024]{1,0:T(8,128)(2,1)} %copy-done.1, bf16[2,4096]{1,0:T(2,128)(2,1)} %collective-permute-done.2), kind=kLoop, calls=%fused_computation.18 | loop fusion | flops 15851520 | bytes 6340608 | tf_op jit(solution)/shard_map/concatenate | solution.py:100
  60.1 3.2 %fusion.7 = bf16[3,512,512]{2,1,0:T(8,128)(2,1)} fusion(s32[]{:T(128)S(6)} %select_n.106, bf16[4,512,512]{2,1,0:T(8,128)(2,1)} %bitcast.152), kind=kLoop, calls=%fused_computation.29 | loop fusion | flops 786432 | bytes 3670020 | tf_op jit(solution)/shard_map/concatenate | solution.py:104
  67.9 2.0 gather_fusion.2
  69.8 1.9 gather_fusion.3
  73.3 30.5 %all-gather.9.cloned.1.call-done = bf16[2048,1,512]{2,0,1:T(8,128)(2,1)} async-done(((bf16[512,1,512]{2,0,1:T(8,128)(2,1)}), bf16[2048,1,512]{2,0,1:T(8,128)(2,1)}) %all-gather.9.cloned.1.call-update) | async-done | bytes 2097168 | tf_op jit(solution)/shard_map/all_gather | solution.py:117
  103.8 2.1 fusion.6
  107.5 2.5 %convolution_bitcast_fusion.5 = f32[386,512]{1,0:T(8,128)S(1)} fusion(bf16[4,512,512]{2,1,0:T(8,128)(2,1)S(1)} %bitcast.153, bf16[4,386,512]{2,1,0:T(8,128)(2,1)} %gather_fusion.2, pred[4]{0:T(512)(128)(4,1)S(1)} %copy-done.39), kind=kOutput, calls=%fused_computation.36 | convolution fusion | flops 810291200 | bytes 4468740 | tf_op jit(solution)/shard_map/ktr,krc->tc/dot_general | solution.py:143
  114.8 2.2 %fusion.15 = f32[386,512]{1,0:T(8,128)S(1)} fusion(f32[386,512]{1,0:T(8,128)S(1)} %convolution_add_fusion.2, bf16[4,386,512]{2,1,0:T(8,128)(2,1)S(1)} %broadcast_select_fusion.1, bf16[3,512,512]{2,1,0:T(8,128)(2,1)} %collective-permute-done.3), kind=kOutput, calls=%fused_computation.44 | convolution fusion | flops 607520768 | bytes 4734976 | tf_op jit(solution)/shard_map/ktr,krc->tc/dot_general | solution.py:147
  117.3 24.7 %collective-permute-done.4 = bf16[3,512,512]{2,1,0:T(8,128)(2,1)S(1)} collective-permute-done((bf16[3,512,512]{2,1,0:T(8,128)(2,1)S(1)}, bf16[3,512,512]{2,1,0:T(8,128)(2,1)S(1)}, u32[]{:S(2)}, u32[]{:S(2)}) %collective-permute-start.4) | collective-permute-done | bytes 1572896 | tf_op jit(solution)/shard_map/ppermute | solution.py:111
  143.0 6.8 %all-gather.11.cloned.1.call-done = bf16[2048,1,512]{2,0,1:T(8,128)(2,1)} async-done(((bf16[512,1,512]{2,0,1:T(8,128)(2,1)}), bf16[2048,1,512]{2,0,1:T(8,128)(2,1)}) %all-gather.11.cloned.1.call-update) | async-done | bytes 2097168 | tf_op jit(solution)/shard_map/all_gather | solution.py:117
  149.8 3.2 %fusion.5 = bf16[3,512,512]{2,1,0:T(8,128)(2,1)} fusion(s32[]{:T(128)S(6)} %select_n.106, bf16[4,512,512]{2,1,0:T(8,128)(2,1)} %bitcast.150), kind=kLoop, calls=%fused_computation.27 | loop fusion | flops 786432 | bytes 3670020 | tf_op jit(solution)/shard_map/concatenate | solution.py:104
  155.9 2.0 convolution_bitcast_fusion.6
  157.8 2.6 %while.13 = (s32[]{:T(128)}, f32[32,64,16]{1,2,0:T(8,128)S(1)}, f32[3,32,64,16]{2,3,1,0:T(8,128)}, f32[32,64,1]{1,0,2:T(8,128)S(1)}, f32[3,32,64,16]{2,3,0,1:T(8,128)S(1)}, /*index=5*/s32[]{:T(128)}, s32[]{:T(128)}) while((s32[]{:T(128)}, f32[32,64,16]{1,2,0:T(8,128)S(1)}, f32[3,32,64,16]{2,3,1,0:T(8,128)}, ...), condition=%wide.region_2.4_spmd.clone, body=%wide.region_1.3_spmd.clone.sunk | while | flops 131075 | bytes 794728 | solution.py:173
  160.4 3.3 %collective-permute-start.8 = (f32[32,64,16]{1,2,0:T(8,128)S(1)}, f32[32,64,16]{1,2,0:T(8,128)S(1)}, u32[]{:S(2)}, u32[]{:S(2)}) collective-permute-start(f32[32,64,16]{1,2,0:T(8,128)S(1)} %get-tuple-element.53), channel_id=1, source_target_pairs={{0,12},{1,13},{2,14},{3,15},{16,28},{17,29},{18,30},{19,31}} | collective-permute-start | bytes 393224 | tf_op jit(solution)/shard_map/ppermute | solution.py:177
  165.1 2.5 %collective-permute-start.6 = (f32[32,64,16]{1,2,0:T(8,128)S(1)}, f32[32,64,16]{1,2,0:T(8,128)S(1)}, u32[]{:S(2)}, u32[]{:S(2)}) collective-permute-start(f32[32,64,16]{1,2,0:T(8,128)S(1)} %get-tuple-element.53), channel_id=1, source_target_pairs={{0,4},{4,8},{8,12},{1,5},{5,9},{9,13},{2,6},{6,10},{10,14},{3,7},{... | collective-permute-start | bytes 393224 | tf_op jit(solution)/shard_map/ppermute | solution.py:177
  167.6 3.1 %convolution_bitcast_fusion.3 = f32[386,512]{1,0:T(8,128)S(1)} fusion(bf16[4,512,512]{2,1,0:T(8,128)(2,1)} %bitcast.151, bf16[4,386,512]{2,1,0:T(8,128)(2,1)} %gather_fusion.2, pred[4]{0:T(512)(128)(4,1)S(1)} %copy-done.39), kind=kOutput, calls=%fused_computation.34 | convolution fusion | flops 810291200 | bytes 4468740 | tf_op jit(solution)/shard_map/ktr,krc->tc/dot_general | solution.py:143
  172.0 4.1 %collective-permute-done.7 = f32[32,64,16]{1,2,0:T(8,128)S(1)} collective-permute-done((f32[32,64,16]{1,2,0:T(8,128)S(1)}, f32[32,64,16]{1,2,0:T(8,128)S(1)}, u32[]{:S(2)}, u32[]{:S(2)}) %collective-permute-start.7) | collective-permute-done | bytes 131104 | tf_op jit(solution)/shard_map/ppermute | solution.py:177
  176.1 4.3 %collective-permute-done.6 = f32[32,64,16]{1,2,0:T(8,128)S(1)} collective-permute-done((f32[32,64,16]{1,2,0:T(8,128)S(1)}, f32[32,64,16]{1,2,0:T(8,128)S(1)}, u32[]{:S(2)}, u32[]{:S(2)}) %collective-permute-start.6) | collective-permute-done | bytes 131104 | tf_op jit(solution)/shard_map/ppermute | solution.py:177
  182.2 3.4 %fusion.11 = f32[3,128,32,16]{1,3,0,2:T(8,128)S(1)} fusion(f32[32,3,16,128]{3,2,1,0:T(8,128)S(1)} %fusion.20, f32[32,128,128]{2,1,0:T(8,128)S(1)} %copy-done.18, f32[3,128,32,16]{1,0,3,2:T(4,128)S(1)} %reshape.174), kind=kOutput, calls=%fused_computation.41 | convolution fusion | flops 302186496 | bytes 4456448 | tf_op jit(solution)/shard_map/gij,bjgc->bigc/dot_general | solution.py:165
  186.1 3.3 %collective-permute-done.5 = bf16[3,512,512]{2,1,0:T(8,128)(2,1)} collective-permute-done((bf16[3,512,512]{2,1,0:T(8,128)(2,1)}, bf16[3,512,512]{2,1,0:T(8,128)(2,1)}, u32[]{:S(2)}, u32[]{:S(2)}) %collective-permute-start.5) | collective-permute-done | bytes 1572896 | tf_op jit(solution)/shard_map/ppermute | solution.py:111
  190.5 2.5 %fusion.19 = f32[386,512]{1,0:T(8,128)S(1)} fusion(f32[386,512]{1,0:T(8,128)} %convolution_add_fusion, bf16[4,386,512]{2,1,0:T(8,128)(2,1)S(1)} %copy-done.8, bf16[3,512,512]{2,1,0:T(8,128)(2,1)} %collective-permute-done.5), kind=kOutput, calls=%fused_computation.48 | convolution fusion | flops 607520768 | bytes 4734976 | tf_op jit(solution)/shard_map/ktr,krc->tc/dot_general | solution.py:147
  194.8 8.4 %collective-permute-done.9 = bf16[1,384,512]{2,1,0:T(8,128)(2,1)S(1)} collective-permute-done((bf16[1,384,512]{2,1,0:T(8,128)(2,1)S(1)}, bf16[1,384,512]{2,1,0:T(8,128)(2,1)S(1)}, u32[]{:S(2)}, u32[]{:S(2)}) %collective-permute-start.9) | collective-permute-done | bytes 393248 | tf_op jit(solution)/shard_map/ppermute | solution.py:201
  203.4 1.9 fusion.31
  205.3 1.8 fusion.29
  (163 shorter events, 42.8 us)
Async XLA Ops:
  6.5 53.5 %all-gather.7.cloned.1.call-start = ((), (), s32[]{:S(2)}) async-start(), calls=%async_computation | async-start | bytes 2621440 | tf_op jit(solution)/shard_map/all_gather | solution.py:117
  9.1 4.1 %copy-start = (s32[4]{0:T(128)S(1)}, s32[4]{0:T(128)}, u32[]{:S(2)}) copy-start(s32[4]{0:T(128)} %constant.130.clone) | copy-start | bytes 52
  9.2 94.6 %all-gather.9.cloned.1.call-start = ((), (), s32[]{:S(2)}) async-start(), calls=%async_computation.1 | async-start | bytes 2621440 | tf_op jit(solution)/shard_map/all_gather | solution.py:117
  9.2 6.6 %copy-start.27 = (f32[3,3,512]{2,1,0:T(4,128)S(1)}, f32[3,3,512]{2,1,0:T(4,128)}, u32[]{:S(2)}) copy-start(f32[3,3,512]{2,1,0:T(4,128)} %param.15) | copy-start | bytes 55300
  9.9 139.9 %all-gather.11.cloned.1.call-start = ((), (), s32[]{:S(2)}) async-start(), calls=%async_computation.2 | async-start | bytes 2621440 | tf_op jit(solution)/shard_map/all_gather | solution.py:117
  10.1 20.9 %collective-permute-start = (bf16[1,385,1024]{2,1,0:T(8,128)(2,1)S(1)}, bf16[1,385,1024]{2,1,0:T(8,128)(2,1)S(1)}, u32[]{:S(2)}, u32[]{:S(2)}) collective-permute-start(bf16[1,385,1024]{2,1,0:T(8,128)(2,1)S(1)} %maximum_bitcast_fusion), channel_id=1, source_target_pairs={{0,2},{1,3},{2,0},{3,1},{4,6},{5,7},{6,4},{7,5},{8,10},{9,11},{10,... | collective-permute-start | bytes 2365448 | tf_op jit(solution)/shard_map/ppermute | solution.py:57
  32.8 11.1 %collective-permute-start.1 = (bf16[2,385,1024]{2,0,1:T(2,128)(2,1)S(1)}, bf16[2,385,1024]{2,0,1:T(2,128)(2,1)S(1)}, u32[]{:S(2)}, u32[]{:S(2)}) collective-permute-start(bf16[2,385,1024]{2,0,1:T(2,128)(2,1)S(1)} %copy.40), channel_id=1, source_target_pairs={{0,1},{1,0},{2,3},{3,2},{4,5},{5,4},{6,7},{7,6},{8,9},{9,8},{10,11... | collective-permute-start | bytes 4730888 | tf_op jit(solution)/shard_map/ppermute | solution.py:57
  35.0 7.1 %copy-start.5 = (bf16[1024,3,512]{2,0,1:T(8,128)(2,1)S(1)}, bf16[1024,3,512]{2,0,1:T(8,128)(2,1)}, u32[]{:S(2)}) copy-start(bf16[1024,3,512]{2,0,1:T(8,128)(2,1)} %param.14) | copy-start | bytes 9437188
  51.4 5.1 %collective-permute-start.2 = (bf16[2,4096]{1,0:T(2,128)(2,1)S(1)}, bf16[2,4096]{1,0:T(2,128)(2,1)}, u32[]{:S(2)}, u32[]{:S(2)}) collective-permute-start(bf16[2,4096]{1,0:T(2,128)(2,1)S(1)} %pad_maximum_fusion.3), channel_id=1, source_target_pairs={{0,4},{4,8},{8,12},{1,5},{5,9},{9,13},{2,6},{6,10},{10,14},{3,7},{... | collective-permute-start | bytes 49160 | tf_op jit(solution)/shard_map/ppermute | solution.py:12
  71.8 43.0 %collective-permute-start.3 = (bf16[3,512,512]{2,1,0:T(8,128)(2,1)}, bf16[3,512,512]{2,1,0:T(8,128)(2,1)}, u32[]{:S(2)}, u32[]{:S(2)}) collective-permute-start(bf16[3,512,512]{2,1,0:T(8,128)(2,1)} %fusion.7), channel_id=1, source_target_pairs={{0,16},{16,0},{1,17},{17,1},{2,18},{18,2},{3,19},{19,3},{4,20},{20... | collective-permute-start | bytes 4718600 | tf_op jit(solution)/shard_map/ppermute | solution.py:111
  103.8 3.7 %copy-start.19 = (bf16[2048,1,512]{2,0,1:T(8,128)(2,1)S(1)}, bf16[2048,1,512]{2,0,1:T(8,128)(2,1)}, u32[]{:S(2)}) copy-start(bf16[2048,1,512]{2,0,1:T(8,128)(2,1)} %all-gather.7.cloned.1.call-done) | copy-start | bytes 6291460
  103.8 3.7 %copy-start.39 = (pred[4]{0:T(512)(128)(4,1)S(1)}, pred[4]{0:T(512)(128)(4,1)}, u32[]{:S(2)}) copy-start(pred[4]{0:T(512)(128)(4,1)} %compare_and_fusion.1) | copy-start | bytes 16
  105.9 4.0 %copy-start.6 = (bf16[4,386,512]{2,1,0:T(8,128)(2,1)S(1)}, bf16[4,386,512]{2,1,0:T(8,128)(2,1)}, u32[]{:S(2)}) copy-start(bf16[4,386,512]{2,1,0:T(8,128)(2,1)} %gather_fusion.3) | copy-start | bytes 4743172
  105.9 4.0 %copy-start.38 = (pred[4]{0:T(512)(128)(4,1)S(1)}, pred[4]{0:T(512)(128)(4,1)}, u32[]{:S(2)}) copy-start(pred[4]{0:T(512)(128)(4,1)} %get-tuple-element.111) | copy-start | bytes 16
  105.9 36.0 %collective-permute-start.4 = (bf16[3,512,512]{2,1,0:T(8,128)(2,1)S(1)}, bf16[3,512,512]{2,1,0:T(8,128)(2,1)S(1)}, u32[]{:S(2)}, u32[]{:S(2)}) collective-permute-start(bf16[3,512,512]{2,1,0:T(8,128)(2,1)S(1)} %fusion.6), channel_id=1, source_target_pairs={{0,16},{16,0},{1,17},{17,1},{2,18},{18,2},{3,19},{19,3},{4,20},{20... | collective-permute-start | bytes 4718600 | tf_op jit(solution)/shard_map/ppermute | solution.py:111
  110.2 31.8 %copy-start.7 = (bf16[4,386,512]{2,1,0:T(8,128)(2,1)}, bf16[4,386,512]{2,1,0:T(8,128)(2,1)S(1)}, u32[]{:S(2)}) copy-start(bf16[4,386,512]{2,1,0:T(8,128)(2,1)S(1)} %broadcast_select_fusion.1) | copy-start | bytes 4743172
  117.3 25.5 %copy-start.31 = (f32[1,1,512]{2,1,0:T(1,128)S(1)}, f32[1,1,512]{2,1,0:T(1,128)}, u32[]{:S(2)}) copy-start(f32[1,1,512]{2,1,0:T(1,128)} %get-tuple-element.124) | copy-start | bytes 6148
  117.3 25.5 %copy-start.32 = (f32[1,1,512]{2,1,0:T(1,128)S(1)}, f32[1,1,512]{2,1,0:T(1,128)}, u32[]{:S(2)}) copy-start(f32[1,1,512]{2,1,0:T(1,128)} %get-tuple-element.125) | copy-start | bytes 6148
  117.3 25.5 %copy-start.33 = (f32[1,1,512]{2,1,0:T(1,128)S(1)}, f32[1,1,512]{2,1,0:T(1,128)}, u32[]{:S(2)}) copy-start(f32[1,1,512]{2,1,0:T(1,128)} %get-tuple-element.126) | copy-start | bytes 6148
  153.0 36.3 %collective-permute-start.5 = (bf16[3,512,512]{2,1,0:T(8,128)(2,1)}, bf16[3,512,512]{2,1,0:T(8,128)(2,1)}, u32[]{:S(2)}, u32[]{:S(2)}) collective-permute-start(bf16[3,512,512]{2,1,0:T(8,128)(2,1)} %fusion.5), channel_id=1, source_target_pairs={{0,16},{16,0},{1,17},{17,1},{2,18},{18,2},{3,19},{19,3},{4,20},{20... | collective-permute-start | bytes 4718600 | tf_op jit(solution)/shard_map/ppermute | solution.py:111
  160.4 10.3 %copy-start.8 = (bf16[4,386,512]{2,1,0:T(8,128)(2,1)S(1)}, bf16[4,386,512]{2,1,0:T(8,128)(2,1)}, u32[]{:S(2)}) copy-start(bf16[4,386,512]{2,1,0:T(8,128)(2,1)} %copy-done.7) | copy-start | bytes 4743172
  160.4 10.3 %copy-start.15 = (bf16[1024,1,512]{2,0,1:T(8,128)(2,1)S(1)}, bf16[1024,1,512]{2,0,1:T(8,128)(2,1)}, u32[]{:S(2)}) copy-start(bf16[1024,1,512]{2,0,1:T(8,128)(2,1)} %get-tuple-element.117) | copy-start | bytes 3145732
  160.4 11.6 %collective-permute-start.8 = (f32[32,64,16]{1,2,0:T(8,128)S(1)}, f32[32,64,16]{1,2,0:T(8,128)S(1)}, u32[]{:S(2)}, u32[]{:S(2)}) collective-permute-start(f32[32,64,16]{1,2,0:T(8,128)S(1)} %get-tuple-element.53), channel_id=1, source_target_pairs={{0,12},{1,13},{2,14},{3,15},{16,28},{17,29},{18,30},{19,31}} | collective-permute-start | bytes 393224 | tf_op jit(solution)/shard_map/ppermute | solution.py:177
  163.8 12.4 %collective-permute-start.7 = (f32[32,64,16]{1,2,0:T(8,128)S(1)}, f32[32,64,16]{1,2,0:T(8,128)S(1)}, u32[]{:S(2)}, u32[]{:S(2)}) collective-permute-start(f32[32,64,16]{1,2,0:T(8,128)S(1)} %get-tuple-element.53), channel_id=1, source_target_pairs={{0,8},{4,12},{1,9},{5,13},{2,10},{6,14},{3,11},{7,15},{16,24},{20,... | collective-permute-start | bytes 393224 | tf_op jit(solution)/shard_map/ppermute | solution.py:177
  165.1 15.4 %collective-permute-start.6 = (f32[32,64,16]{1,2,0:T(8,128)S(1)}, f32[32,64,16]{1,2,0:T(8,128)S(1)}, u32[]{:S(2)}, u32[]{:S(2)}) collective-permute-start(f32[32,64,16]{1,2,0:T(8,128)S(1)} %get-tuple-element.53), channel_id=1, source_target_pairs={{0,4},{4,8},{8,12},{1,5},{5,9},{9,13},{2,6},{6,10},{10,14},{3,7},{... | collective-permute-start | bytes 393224 | tf_op jit(solution)/shard_map/ppermute | solution.py:177
  170.7 9.8 %copy-start.23 = (f32[32,64]{1,0:T(8,128)S(1)}, f32[32,64]{1,0:T(8,128)}, u32[]{:S(2)}) copy-start(f32[32,64]{1,0:T(8,128)} %get-tuple-element.134) | copy-start | bytes 24580
  170.7 9.8 %copy-start.24 = (f32[32,64]{1,0:T(8,128)S(1)}, f32[32,64]{1,0:T(8,128)}, u32[]{:S(2)}) copy-start(f32[32,64]{1,0:T(8,128)} %get-tuple-element.135) | copy-start | bytes 24580
  170.7 9.9 %copy-start.11 = (f32[32,128,64]{1,2,0:T(8,128)S(1)}, f32[32,128,64]{1,2,0:T(8,128)}, u32[]{:S(2)}) copy-start(f32[32,128,64]{1,2,0:T(8,128)} %exponential_multiply_fusion) | copy-start | bytes 3145732
  170.7 9.9 %copy-start.22 = (f32[3,32,64,16]{2,3,1,0:T(8,128)S(1)}, f32[3,32,64,16]{2,3,1,0:T(8,128)}, u32[]{:S(2)}) copy-start(f32[3,32,64,16]{2,3,1,0:T(8,128)} %get-tuple-element.54) | copy-start | bytes 1179652
  193.3 9.9 %collective-permute-start.9 = (bf16[1,384,512]{2,1,0:T(8,128)(2,1)S(1)}, bf16[1,384,512]{2,1,0:T(8,128)(2,1)S(1)}, u32[]{:S(2)}, u32[]{:S(2)}) collective-permute-start(bf16[1,384,512]{2,1,0:T(8,128)(2,1)S(1)} %bitcast.147), channel_id=1, source_target_pairs={{0,2},{1,3},{2,0},{3,1},{4,6},{5,7},{6,4},{7,5},{8,10},{9,11},{10,... | collective-permute-start | bytes 1179656 | tf_op jit(solution)/shard_map/ppermute | solution.py:201
  203.3 3.9 %collective-permute-start.10 = (bf16[2,384,512]{2,1,0:T(8,128)(2,1)S(1)}, bf16[2,384,512]{2,1,0:T(8,128)(2,1)S(1)}, u32[]{:S(2)}, u32[]{:S(2)}) collective-permute-start(bf16[2,384,512]{2,1,0:T(8,128)(2,1)S(1)} %pad_maximum_fusion.2), channel_id=1, source_target_pairs={{0,1},{1,0},{2,3},{3,2},{4,5},{5,4},{6,7},{7,6},{8,9},{9,8},{10,11... | collective-permute-start | bytes 2359304 | tf_op jit(solution)/shard_map/ppermute | solution.py:201
  203.4 3.8 %copy-start.9 = (bf16[2048,1024]{1,0:T(8,128)(2,1)S(1)}, bf16[2048,1024]{1,0:T(8,128)(2,1)}, u32[]{:S(2)}) copy-start(bf16[2048,1024]{1,0:T(8,128)(2,1)} %param.18) | copy-start | bytes 12582916
  (22 other events, 44.6 us)
Sparse Core Ops, SparseCore 0:
  9.3 48.3 all-gather.6
  59.3 44.4 all-gather.8
  105.3 44.4 all-gather.10
